TPU v7x, 256 devices: a whole 4x4x8 slice. The times are simulated.
256 devices in a mesh: blk: 16 (over x_lo, y, core), exp: 16 (over z, x_hi).
Axes of the slice: x: 4 (x_hi: 2, x_lo: 2; x = x_hi * 2 + x_lo), y: 4, z: 8, core: 2. Of those that a mesh axis runs over, the one named last changes fastest.
Arguments:
- hidden: bfloat16 [4096, 2560], P('exp', 'blk'), may hold values from -6 to 6
- attn_gain: float32 [2560], replicated, may hold values from 0.25 to 1.75
- qkv_weight: bfloat16 [2560, 3584], P(None, 'blk'), may hold values from -0.125 to 0.125
- out_weight: bfloat16 [2560, 2560], P(None, 'blk'), may hold values from -0.125 to 0.125
- kv_pool: bfloat16 [16, 64, 128, 1024], P('exp', 'blk'), may hold values from -64 to 64
- page_table: int32 [16, 64], P('exp'), may hold values from 0 to 63, each once within a row
- cache_lens: int32 [16], P('exp'), may hold values from 1 to 7936, as said below
- ffn_gain: float32 [2560], replicated, may hold values from 0.25 to 1.75
- route_ids: int32 [4096, 6], P('exp'), may hold values from 0 to 63, all different within a row; in each aligned block of 256 rows (0 to 255, 256 to 511, ...) at most 32 rows name the same one
- route_weights: float32 [4096, 6], P('exp'), may hold values from 0.05 to 2
- shared_gate_up: bfloat16 [2560, 2, 3072], P(None, None, 'blk'), may hold values from -0.125 to 0.125
- shared_down: bfloat16 [3072, 2560], P('blk'), may hold values from -0.109375 to 0.109375
- expert_gate_up: bfloat16 [256, 2560, 768], P(('blk', 'exp')), may hold values from -0.125 to 0.125
- expert_down: bfloat16 [256, 384, 2560], P(('blk', 'exp')), may hold values from -0.3125 to 0.3125
Outputs:
- hidden_out: bfloat16 [4096, 2560], P('exp', 'blk')
- kv_pool_out: bfloat16 [16, 64, 128, 1024], P('exp', 'blk')
Inputs may be any that keep to these rules, and one draw needn't show every extreme that they name: `route_ids`: among the 256 tokens of one request at most 32 choose any one expert, and some expert is chosen by exactly 32 of them; a token's 6 experts differ. `page_table`: each row names every page of the request's pool once. `cache_lens`: some request has exactly 7936 cached tokens.
All inputs are finite; a program needn't handle non-finite values.
Results may differ from a plain program's by a relative error of at most 0.02.
The roundings to bfloat16 on the way count: a program that leaves them out, or rounds other values in their place, can miss the bound.
Values may be sent and summed in bfloat16 or wider, within the bound.
No kernel may reach another device: no remote copies, remote signals or barrier semaphores. Data moves between devices by JAX's collectives and lax.ppermute only.
A program may use at most 256 MiB of HBM per device.

v0:
```python
import math

import jax
import jax.numpy as jnp
from jax import lax
from jax.sharding import PartitionSpec as P

HEADS = 20
KV_HEADS = 4
HEAD_DIM = 128
TOPK = 6
SPLIT = 4
PAGE = 128
NEW = 256
FF_PART = 384


rope_base = 500000.0
norm_eps = 1e-05


def normalize(inputs, gain_vec):
    values = inputs.astype(jnp.float32)
    inv_rms = lax.rsqrt(jnp.mean(values * values, axis=-1, keepdims=True) + norm_eps)
    return (values * inv_rms * gain_vec).astype(jnp.bfloat16)


def rotate(inputs, positions):
    half_dim = HEAD_DIM // 2
    frequency = rope_base ** (-(jnp.arange(half_dim).astype(jnp.float32) * 2.0 / HEAD_DIM))
    angles = positions.astype(jnp.float32)[:, None] * frequency[None, :]
    cosine = jnp.cos(angles)[:, None, :]
    sine_vals = jnp.sin(angles)[:, None, :]
    lower_half = inputs[..., :half_dim]
    upper_half = inputs[..., half_dim:]
    return jnp.concatenate(
        [
            lower_half * cosine - upper_half * sine_vals,
            upper_half * cosine + lower_half * sine_vals,
        ],
        axis=-1,
    )


def partial_softmax(queries, query_pos, block_rows, key_pos):
    key_width = KV_HEADS * HEAD_DIM
    key_rows = block_rows[:, :key_width].reshape(-1, KV_HEADS, HEAD_DIM)
    value_rows = block_rows[:, key_width:].reshape(-1, KV_HEADS, HEAD_DIM)
    scores = jnp.einsum("tkgd,skd->tkgs", queries, key_rows, preferred_element_type=jnp.float32) * (
        1.0 / math.sqrt(HEAD_DIM)
    )
    allowed = (key_pos[None, :] <= query_pos[:, None])[:, None, None, :]
    maxima = jnp.max(jnp.where(allowed, scores, -1e30), axis=-1)
    weights = jnp.where(allowed, jnp.exp(scores - maxima[..., None]), 0.0)
    totals = jnp.sum(weights, axis=-1)
    weighted = jnp.einsum(
        "tkgs,skd->tkgd",
        weights.astype(jnp.bfloat16),
        value_rows,
        preferred_element_type=jnp.float32,
    )
    return (maxima, totals, weighted)


def combine_parts(earlier, later):
    peak_early, sum_early, acc_early = earlier
    peak_late, sum_late, acc_late = later
    peak_both = jnp.maximum(peak_early, peak_late)
    factor_late = jnp.exp(peak_late - peak_both)
    return (peak_both, sum_late * factor_late, acc_late * factor_late[..., None])


def per_device(
    hidden,
    attn_gain,
    qkv_weight,
    out_weight,
    kv_pool,
    page_table,
    cache_lens,
    ffn_gain,
    route_ids,
    route_weights,
    shared_gate_up,
    shared_down,
    expert_gate_up,
    expert_down,
):
    blocks = lax.axis_size("blk")
    groups = lax.axis_size("exp")
    block_index = lax.axis_index("blk")
    model_width = hidden.shape[1] * blocks
    query_width = HEADS * HEAD_DIM
    key_width = KV_HEADS * HEAD_DIM
    group_size = HEADS // KV_HEADS
    own_rows = NEW // blocks
    full_rows = lax.all_gather(hidden, "blk", axis=1, tiled=True)
    attn_in = normalize(full_rows, attn_gain)
    projected = jnp.dot(attn_in, qkv_weight, preferred_element_type=jnp.float32).astype(
        jnp.bfloat16
    )
    projected_all = lax.all_gather(projected, "blk", axis=1, tiled=True)
    length = cache_lens[0]
    positions = length + jnp.arange(NEW, dtype=jnp.int32)
    queries = rotate(
        projected_all[:, :query_width].astype(jnp.float32).reshape(NEW, HEADS, HEAD_DIM), positions
    ).astype(jnp.bfloat16)
    fresh_keys = rotate(
        projected_all[:, query_width : query_width + key_width]
        .astype(jnp.float32)
        .reshape(NEW, KV_HEADS, HEAD_DIM),
        positions,
    ).astype(jnp.bfloat16)
    appended = jnp.concatenate(
        [fresh_keys.reshape(NEW, key_width), projected_all[:, query_width + key_width :]], axis=1
    )
    page_map = page_table[0]
    pool_pages = page_map.shape[0]
    page_index = jnp.arange(pool_pages, dtype=jnp.int32)
    logical = jnp.sum(
        jnp.where(page_map[None, :] == page_index[:, None], page_index[None, :], 0), axis=1
    )
    local_pages = kv_pool.shape[1]
    local_logical = lax.dynamic_slice_in_dim(logical, block_index * local_pages, local_pages)
    slot_offsets = jnp.arange(PAGE, dtype=jnp.int32)
    local_pos = local_logical[:, None] * PAGE + slot_offsets[None, :]
    offset = local_pos - length
    written = (offset >= 0) & (offset < NEW)
    picked = appended[jnp.clip(offset, 0, NEW - 1)]
    pool_out = jnp.where(written[:, :, None], picked, kv_pool[0])
    grouped = queries.reshape(NEW, KV_HEADS, group_size, HEAD_DIM)
    own_queries = lax.dynamic_slice_in_dim(grouped, block_index * own_rows, own_rows, 0)
    own_pos = lax.dynamic_slice_in_dim(positions, block_index * own_rows, own_rows, 0)
    initial = (
        jnp.full((own_rows, KV_HEADS, group_size), -1e30, jnp.float32),
        jnp.zeros((own_rows, KV_HEADS, group_size), jnp.float32),
        jnp.zeros((own_rows, KV_HEADS, group_size, HEAD_DIM), jnp.float32),
    )
    shard_pages = lax.all_gather(pool_out, "blk", axis=0, tiled=True)
    page_count = shard_pages.shape[0]
    key_pos = (logical[:, None] * PAGE + slot_offsets[None, :]).reshape(-1)
    block_rows = shard_pages.reshape(page_count * PAGE, 2 * key_width)
    maxima, totals, weighted = combine_parts(
        initial, partial_softmax(own_queries, own_pos, block_rows, key_pos)
    )
    own_attention = (
        (weighted / totals[..., None]).reshape(own_rows, query_width).astype(jnp.bfloat16)
    )
    attended = jnp.dot(
        lax.all_gather(own_attention, "blk", axis=0, tiled=True),
        out_weight,
        preferred_element_type=jnp.float32,
    )
    mixed_cols = (hidden.astype(jnp.float32) + attended).astype(jnp.bfloat16)
    mixed_rows = lax.all_gather(mixed_cols, "blk", axis=1, tiled=True)
    ffn_in = normalize(mixed_rows, ffn_gain)
    shared_cols = shared_gate_up.shape[2]
    gate_up = jnp.dot(
        ffn_in,
        shared_gate_up.reshape(model_width, 2 * shared_cols),
        preferred_element_type=jnp.float32,
    )
    shared_act = (jax.nn.silu(gate_up[:, :shared_cols]) * gate_up[:, shared_cols:]).astype(
        jnp.bfloat16
    )
    shared_term = jnp.dot(shared_act, shared_down, preferred_element_type=jnp.float32)
    row_experts = groups // SPLIT
    expert_count = row_experts * blocks
    capacity = NEW * TOPK * 4 // (expert_count * 3)
    row_expert_ids = block_index * row_experts + jnp.arange(row_experts, dtype=jnp.int32)
    route_hits = route_ids[:, :, None] == row_expert_ids[None, None, :]
    chosen = jnp.any(route_hits, axis=1)
    route_share = jnp.sum(jnp.where(route_hits, route_weights[:, :, None], 0.0), axis=1)
    slot_rank = jnp.cumsum(chosen.astype(jnp.int32), axis=0) - 1
    slot_ids = jnp.arange(capacity, dtype=jnp.int32)
    placed = chosen.T[:, None, :] & (slot_rank.T[:, None, :] == slot_ids[None, :, None])
    selector = placed.astype(jnp.bfloat16)
    outgoing = jnp.einsum(
        "ect,td->ecd", selector, ffn_in, preferred_element_type=jnp.float32
    ).astype(jnp.bfloat16)
    outgoing = jnp.repeat(outgoing, SPLIT, axis=0)
    received = lax.all_to_all(outgoing, "exp", split_axis=0, concat_axis=0, tiled=True)
    flat_rows = received.reshape(-1, model_width)
    expert_gu = jnp.dot(flat_rows, expert_gate_up[0], preferred_element_type=jnp.float32)
    activated = (jax.nn.silu(expert_gu[:, :FF_PART]) * expert_gu[:, FF_PART:]).astype(jnp.bfloat16)
    result = jnp.dot(activated, expert_down[0], preferred_element_type=jnp.float32).astype(
        jnp.bfloat16
    )
    returned = lax.all_to_all(
        result.reshape(received.shape), "exp", split_axis=0, concat_axis=0, tiled=True
    )
    summed = jnp.sum(
        returned.reshape(row_experts, SPLIT, capacity, model_width).astype(jnp.float32), axis=1
    )
    slot_weight = jnp.sum(placed.astype(jnp.float32) * route_share.T[:, None, :], axis=2)
    slot_values = summed * slot_weight[:, :, None]
    upper_part = slot_values.astype(jnp.bfloat16)
    lower_part = (slot_values - upper_part.astype(jnp.float32)).astype(jnp.bfloat16)
    routed = jnp.einsum(
        "ect,ecd->td", selector, upper_part, preferred_element_type=jnp.float32
    ) + jnp.einsum("ect,ecd->td", selector, lower_part, preferred_element_type=jnp.float32)
    layer_term = shared_term + routed
    summed_cols = lax.psum_scatter(layer_term, "blk", scatter_dimension=1, tiled=True)
    hidden_out = (mixed_cols.astype(jnp.float32) + summed_cols).astype(jnp.bfloat16)
    return (hidden_out, pool_out[None])


def solution(mesh):
    placed = (
        P("exp", "blk"),
        P(),
        P(None, "blk"),
        P(None, "blk"),
        P("exp", "blk", None, None),
        P("exp", None),
        P("exp"),
        P(),
        P("exp", None),
        P("exp", None),
        P(None, None, "blk"),
        P("blk", None),
        P(("blk", "exp"), None, None),
        P(("blk", "exp"), None, None),
    )
    return jax.shard_map(
        per_device,
        mesh=mesh,
        in_specs=placed,
        out_specs=(P("exp", "blk"), P("exp", "blk", None, None)),
        check_vma=False,
    )
```

profile of v0, /device:TPU:1, one launch (start us, length us, event | category | flops | bytes accessed | tf_op | source)
XLA Modules:
  0.0 549.8 jit_solution(16799546149269719078)
XLA Ops:
  8.0 41.6 %all-gather.6.cloned.1.call-done = bf16[256,2560]{0,1:T(8,128)(2,1)} async-done(((bf16[256,160]{0,1:T(8,128)(2,1)}), bf16[256,2560]{0,1:T(8,128)(2,1)}) %all-gather.6.cloned.1.call-update) | async-done | bytes 1310736 | tf_op jit(solution)/shard_map/all_gather | solution.py:97
  49.6 1.7 fusion.11
  51.3 3.0 fusion.23
  55.7 35.0 %all-gather.8.cloned.1.call-done = bf16[256,3584]{0,1:T(8,128)(2,1)} async-done(((bf16[256,224]{0,1:T(8,128)(2,1)}), bf16[256,3584]{0,1:T(8,128)(2,1)}) %all-gather.8.cloned.1.call-update) | async-done | bytes 1835024 | tf_op jit(solution)/shard_map/all_gather | solution.py:102
  92.2 2.1 gather_fusion
  94.2 2.4 bitcast_select_fusion
  98.5 1.5 add_convert_fusion
  100.0 2.3 copy.51
  102.4 2.3 copy.50
  104.7 86.3 %all-gather.10.cloned.1.call-done = bf16[64,128,1024]{2,1,0:T(8,128)(2,1)} async-done(((bf16[4,128,1024]{2,1,0:T(8,128)(2,1)}), bf16[64,128,1024]{2,1,0:T(8,128)(2,1)}) %all-gather.10.cloned.1.call-update) | async-done | bytes 16777232 | tf_op jit(solution)/shard_map/all_gather | solution.py:139
  191.0 11.3 %fusion.75 = (bf16[8192,512]{1,0:T(8,128)(2,1)}, bf16[8192,512]{1,0:T(8,128)(2,1)}) fusion(bf16[8192,1024]{1,0:T(8,128)(2,1)} %bitcast.81), kind=kLoop, calls=%fused_computation.109 | loop fusion | bytes 33554432 | tf_op jit(solution)/shard_map/slice | solution.py:47
  202.4 12.0 %copy.68 = bf16[8192,512]{0,1:T(8,128)(2,1)} copy(bf16[8192,512]{1,0:T(8,128)(2,1)} %get-tuple-element.2) | data formatting | bytes 16777216
  214.3 10.1 %select_reduce_fusion = (f32[16,4,5]{0,2,1:T(8,128)S(1)}, f32[16,4,5,8192]{3,0,2,1:T(8,128)}) fusion(pred[16,8192]{1,0:T(8,128)(4,1)S(1)} %broadcast_compare_fusion, bf16[8192,4,128,1]{0,2,3,1:T(8,128)(2,1)} %bitcast.86, s32[]{:T(128)S(6)} %select_n.43, bf16[256,4,5,64]{3,0,2,1:T(8,128)(2,1)} %bitcast.91, bf16[256,4,5,64]{3,0,2,1:T(8,128)(2,1)} %bitcast.90), kind=kOutput, calls=%fused_computation.4 | convolution fusion | flops 679116480 | bytes 20317444 | tf_op jit(solution)/shard_map/tkgd,skd->tkgs/dot_general | solution.py:49
  224.4 6.2 %fusion.1 = f32[16,4,5]{0,2,1:T(8,128)S(1)} fusion(f32[16,4,5,8192]{3,0,2,1:T(8,128)} %get-tuple-element.15, f32[16,4,5]{0,2,1:T(8,128)S(1)} %get-tuple-element.14, pred[16,8192]{1,0:T(8,128)(4,1)S(1)} %broadcast_compare_fusion), kind=kLoop, calls=%fused_computation.5 | loop fusion | flops 7864000 | bytes 10619392 | tf_op jit(solution)/shard_map/reduce_sum | solution.py:55
  230.6 12.0 %copy.67 = bf16[8192,512]{0,1:T(8,128)(2,1)} copy(bf16[8192,512]{1,0:T(8,128)(2,1)} %get-tuple-element.3) | data formatting | bytes 16777216
  242.6 9.5 %fusion.36 = bf16[16,4,5,128]{3,0,2,1:T(8,128)(2,1)S(1)} fusion(bf16[8192,4,128,1]{0,2,3,1:T(8,128)(2,1)} %bitcast.85, f32[16,4,5,8192]{3,0,2,1:T(8,128)} %get-tuple-element.15, f32[16,4,5]{0,2,1:T(8,128)S(1)} %get-tuple-element.14, pred[16,8192]{1,0:T(8,128)(4,1)S(1)} %broadcast_compare_fusion, f32[16,4,5]{0,2,1:T(8,128)S(1)} %get-tuple-element.11, ...), kind=kOutput, calls=%fused_computation.47 | convolution fusion | flops 679075840 | bytes 19091200 | tf_op jit(solution)/shard_map/tkgs,skd->tkgd/dot_general | solution.py:56
  252.9 36.6 %all-gather.12.cloned.1.call-done = bf16[256,2560]{1,0:T(8,128)(2,1)} async-done(((bf16[16,2560]{1,0:T(8,128)(2,1)}), bf16[256,2560]{1,0:T(8,128)(2,1)}) %all-gather.12.cloned.1.call-update) | async-done | bytes 1310736 | tf_op jit(solution)/shard_map/all_gather | solution.py:150
  289.5 2.7 fusion.32
  294.0 34.0 %all-gather.14.cloned.1.call-done = bf16[256,2560]{0,1:T(8,128)(2,1)} async-done(((bf16[256,160]{0,1:T(8,128)(2,1)}), bf16[256,2560]{0,1:T(8,128)(2,1)}) %all-gather.14.cloned.1.call-update) | async-done | bytes 1310736 | tf_op jit(solution)/shard_map/all_gather | solution.py:155
  328.0 1.7 fusion.14
  329.7 2.0 convolution_convert_fusion.1
  332.0 71.6 %all_to_all.10 = bf16[16,32,2560]{2,1,0:T(8,128)(2,1)S(1)} all-to-all(bf16[16,32,2560]{2,1,0:T(8,128)(2,1)S(1)} %bitcast.82), channel_id=1, replica_groups=mesh['blk'=16,'exp'=16] {'exp'}, dimensions={0} | all-to-all | bytes 5242880 | tf_op jit(solution)/shard_map/all_to_all | solution.py:182
  403.6 2.2 fusion.9
  405.8 3.1 convolution_convert_fusion
  408.8 4.6 all-to-all-start.1
  413.7 3.3 fusion.45
  417.0 57.9 %all-to-all-done.1 = bf16[16,32,2560]{2,1,0:T(8,128)(2,1)} async-done(((bf16[16,32,2560]{2,1,0:T(8,128)(2,1)}), bf16[16,32,2560]{2,1,0:T(8,128)(2,1)}, u32[]{:S(2)}, u32[]{:S(2)}) %all-to-all-start.1) | async-done | bytes 2621472 | tf_op jit(solution)/shard_map/all_to_all | solution.py:189
  474.8 2.3 convert_reduce_fusion
  479.0 2.3 convolution_add_fusion
  481.3 2.4 broadcast_select_fusion
  483.7 57.7 %reduce-scatter.2.cloned.1.call-done = f32[256,160]{0,1:T(8,128)} async-done(((f32[256,2560]{0,1:T(8,128)}), f32[256,160]{0,1:T(8,128)}) %reduce-scatter.2.cloned.1.call-update) | async-done | bytes 163856 | tf_op jit(solution)/shard_map/reduce_scatter | solution.py:203
  541.4 1.6 add_convert_fusion.2
  (82 shorter events, 9.7 us)
Async XLA Ops:
  7.2 398.6 %copy-start = (bf16[1,384,2560]{2,1,0:T(8,128)(2,1)S(1)}, bf16[1,384,2560]{2,1,0:T(8,128)(2,1)}, u32[]{:S(2)}) copy-start(bf16[1,384,2560]{2,1,0:T(8,128)(2,1)} %param.27) | copy-start | bytes 5898244
  7.2 42.4 %all-gather.6.cloned.1.call-start = ((), (), s32[]{:S(2)}) async-start(), calls=%async_computation.3 | async-start | bytes 1392640 | tf_op jit(solution)/shard_map/all_gather | solution.py:97
  7.9 47.1 %copy-start.12 = (s32[1,64]{1,0:T(1,128)S(1)}, s32[1,64]{1,0:T(1,128)}, u32[]{:S(2)}) copy-start(s32[1,64]{1,0:T(1,128)} %param.19) | copy-start | bytes 772
  7.9 82.7 %all-gather.8.cloned.1.call-start = ((), (), s32[]{:S(2)}) async-start(), calls=%async_computation.4 | async-start | bytes 1949696 | tf_op jit(solution)/shard_map/all_gather | solution.py:102
  54.2 136.8 %all-gather.10.cloned.1.call-start = ((), (), s32[]{:S(2)}) async-start(), calls=%async_computation.5 | async-start | bytes 17825792 | tf_op jit(solution)/shard_map/all_gather | solution.py:139
  55.6 36.2 %copy-start.3 = (f32[256,64]{0,1:T(8,128)}, f32[256,64]{0,1:T(8,128)S(1)}, u32[]{:S(2)}) copy-start(f32[256,64]{0,1:T(8,128)S(1)} %get-tuple-element.12) | copy-start | bytes 196612
  55.7 36.2 %copy-start.5 = (f32[256,64]{0,1:T(8,128)}, f32[256,64]{0,1:T(8,128)S(1)}, u32[]{:S(2)}) copy-start(f32[256,64]{0,1:T(8,128)S(1)} %get-tuple-element.13) | copy-start | bytes 196612
  96.6 192.9 %all-gather.12.cloned.1.call-start = ((), (), s32[]{:S(2)}) async-start(), calls=%async_computation.6 | async-start | bytes 1392640 | tf_op jit(solution)/shard_map/all_gather | solution.py:150
  96.9 1.3 slice-start
  97.2 1.3 copy-start.4
  97.2 1.3 copy-start.6
  242.6 46.9 %copy-start.7 = (bf16[256,160]{0,1:T(8,128)(2,1)S(1)}, bf16[256,160]{0,1:T(8,128)(2,1)}, u32[]{:S(2)}) copy-start(bf16[256,160]{0,1:T(8,128)(2,1)} %param.14) | copy-start | bytes 245764
  252.0 40.2 %copy-start.8 = (s32[256,6]{0,1:T(8,128)S(1)}, s32[256,6]{0,1:T(8,128)}, u32[]{:S(2)}) copy-start(s32[256,6]{0,1:T(8,128)} %param.22) | copy-start | bytes 18436
  252.0 77.7 %copy-start.11 = (f32[2560]{0:T(1024)S(1)}, f32[2560]{0:T(1024)}, u32[]{:S(2)}) copy-start(f32[2560]{0:T(1024)} %param.21) | copy-start | bytes 30724
  252.9 75.2 %all-gather.14.cloned.1.call-start = ((), (), s32[]{:S(2)}) async-start(), calls=%async_computation.7 | async-start | bytes 1392640 | tf_op jit(solution)/shard_map/all_gather | solution.py:155
  331.9 71.6 %copy-start.10 = (bf16[1,2560,768]{2,1,0:T(8,128)(2,1)S(1)}, bf16[1,2560,768]{2,1,0:T(8,128)(2,1)}, u32[]{:S(2)}) copy-start(bf16[1,2560,768]{2,1,0:T(8,128)(2,1)} %param.26) | copy-start | bytes 11796484
  408.8 4.7 copy-start.9
  408.8 66.0 %all-to-all-start.1 = ((bf16[16,32,2560]{2,1,0:T(8,128)(2,1)}), bf16[16,32,2560]{2,1,0:T(8,128)(2,1)}, u32[]{:S(2)}, u32[]{:S(2)}) async-start(bf16[16,32,2560]{2,1,0:T(8,128)(2,1)} %bitcast.88), calls=%async_computation.1 | async-start | bytes 5242880 | tf_op jit(solution)/shard_map/all_to_all | solution.py:189
  413.4 127.9 %reduce-scatter.2.cloned.1.call-start = ((), (), s32[]{:S(2)}) async-start(), calls=%async_computation.8 | async-start | bytes 2785280 | tf_op jit(solution)/shard_map/reduce_scatter | solution.py:203
  477.8 1.2 copy-start.1
  481.3 60.1 %copy-start.2 = (bf16[256,160]{0,1:T(8,128)(2,1)S(1)}, bf16[256,160]{0,1:T(8,128)(2,1)}, u32[]{:S(2)}) copy-start(bf16[256,160]{0,1:T(8,128)(2,1)} %fusion.32) | copy-start | bytes 245764
Sparse Core Ops, SparseCore 0:
  9.9 39.6 all-gather.5
  54.4 36.2 all-gather.7
  96.7 94.2 all-gather.9
  253.0 36.4 all-gather.11
  292.4 35.5 all-gather.13
  481.5 59.8 reduce-scatter.1
where the time goes:
time: 553 us; the launch traced here: 550 us
  waiting for transfers between devices  350 us (63%)
  blocking collectives  71.6 us (13%)
  local copies, waits for them, and re-layouts  46.3 us (8%)
  matrix products  39.2 us (7%)
  other arithmetic  22.7 us (4%)
  between operations  15.1 us (3%)
    all_gather x1, waiting for transfers between devices, per_device(): shard_pages = lax.all_gather(pool_out, 'blk', axis=0, tiled=True)  86.3 us
    all_to_all x1, blocking collectives, per_device(): lax.all_to_all(outgoing, 'exp', split_axis=0, concat_axis=0, tiled=True)  71.6 us
    all_to_all x1, waiting for transfers between devices, per_device(): lax.all_to_all(result.reshape(received.shape), 'exp', split_axis=0, conca...  57.9 us
    reduce_scatter x1, waiting for transfers between devices, per_device(): lax.psum_scatter(layer_term, 'blk', scatter_dimension=1, tiled=True)  57.7 us
    all_gather x1, waiting for transfers between devices, per_device(): full_rows = lax.all_gather(hidden, 'blk', axis=1, tiled=True)  41.6 us
    all_gather x1, waiting for transfers between devices, per_device(): lax.all_gather(own_attention, 'blk', axis=0, tiled=True)  36.6 us
    all_gather x1, waiting for transfers between devices, per_device(): projected_all = lax.all_gather(projected, 'blk', axis=1, tiled=True)  35 us
    all_gather x1, waiting for transfers between devices, per_device(): mixed_rows = lax.all_gather(mixed_cols, 'blk', axis=1, tiled=True)  34 us
  transfers between devices with their start and end apart: 7, of which 7 were waited for; matrix products, arithmetic and copies ran while one was open for 3% of the time, Pallas kernels for 0%

commit v1 on v0

--- a/solution.py
+++ b/solution.py
@@ -60,14 +60,6 @@
         preferred_element_type=jnp.float32,
     )
     return (maxima, totals, weighted)
-
-
-def combine_parts(earlier, later):
-    peak_early, sum_early, acc_early = earlier
-    peak_late, sum_late, acc_late = later
-    peak_both = jnp.maximum(peak_early, peak_late)
-    factor_late = jnp.exp(peak_late - peak_both)
-    return (peak_both, sum_late * factor_late, acc_late * factor_late[..., None])
 
 
 def per_device(
@@ -129,22 +121,26 @@
     picked = appended[jnp.clip(offset, 0, NEW - 1)]
     pool_out = jnp.where(written[:, :, None], picked, kv_pool[0])
     grouped = queries.reshape(NEW, KV_HEADS, group_size, HEAD_DIM)
-    own_queries = lax.dynamic_slice_in_dim(grouped, block_index * own_rows, own_rows, 0)
-    own_pos = lax.dynamic_slice_in_dim(positions, block_index * own_rows, own_rows, 0)
-    initial = (
-        jnp.full((own_rows, KV_HEADS, group_size), -1e30, jnp.float32),
-        jnp.zeros((own_rows, KV_HEADS, group_size), jnp.float32),
-        jnp.zeros((own_rows, KV_HEADS, group_size, HEAD_DIM), jnp.float32),
-    )
-    shard_pages = lax.all_gather(pool_out, "blk", axis=0, tiled=True)
-    page_count = shard_pages.shape[0]
-    key_pos = (logical[:, None] * PAGE + slot_offsets[None, :]).reshape(-1)
-    block_rows = shard_pages.reshape(page_count * PAGE, 2 * key_width)
-    maxima, totals, weighted = combine_parts(
-        initial, partial_softmax(own_queries, own_pos, block_rows, key_pos)
-    )
+    slot_rows = pool_out.reshape(local_pages * PAGE, 2 * key_width)
+    maxima, totals, weighted = partial_softmax(grouped, positions, slot_rows, local_pos.reshape(-1))
+    payload = jnp.concatenate(
+        [
+            weighted.reshape(NEW, query_width),
+            maxima.reshape(NEW, HEADS),
+            totals.reshape(NEW, HEADS),
+        ],
+        axis=1,
+    ).reshape(blocks, own_rows, query_width + 2 * HEADS)
+    gathered = lax.all_to_all(payload, "blk", split_axis=0, concat_axis=0, tiled=True)
+    part_acc = gathered[:, :, :query_width].reshape(blocks, own_rows, HEADS, HEAD_DIM)
+    part_max = gathered[:, :, query_width : query_width + HEADS]
+    part_sum = gathered[:, :, query_width + HEADS :]
+    overall = jnp.max(part_max, axis=0)
+    factors = jnp.exp(part_max - overall[None])
+    total_sum = jnp.sum(part_sum * factors, axis=0)
+    total_acc = jnp.sum(part_acc * factors[..., None], axis=0)
     own_attention = (
-        (weighted / totals[..., None]).reshape(own_rows, query_width).astype(jnp.bfloat16)
+        (total_acc / total_sum[..., None]).reshape(own_rows, query_width).astype(jnp.bfloat16)
     )
     attended = jnp.dot(
         lax.all_gather(own_attention, "blk", axis=0, tiled=True),

time: 553 us -> 495 us (0.90)
  waiting for transfers between devices: 350 us -> 261 us
  blocking collectives: 71.6 us -> 110 us
  local copies, waits for them, and re-layouts: 46.3 us -> 38.8 us
    all_gather x1 -> x0, waiting for transfers between devices: 86.3 us -> none  [per_device(): shard_pages = lax.all_gather(pool_out, 'blk', axis=0, tiled=True)]
    all_to_all x0 -> x1, blocking collectives: none -> 38.4 us  [per_device(): lax.all_to_all(payload, 'blk', split_axis=0, concat_axis=0, tiled=True)]
    unnamed x29 -> x35, local copies, waits for them, and re-layouts: 24.6 us -> 2.2 us
    concatenate x0 -> x6, local copies, waits for them, and re-layouts: none -> 10.8 us  [per_device(): jnp.concatenate([weighted.reshape(NEW, query_width), maxima.reshape(NEW,...]
    slice x1 -> x2, local copies, waits for them, and re-layouts: 11.3 us -> 2.34 us  [partial_softmax(): key_rows = block_rows[:, :key_width].reshape(-1, KV_HEADS, HEAD_DIM)]
    mul x0 -> x2, local copies, waits for them, and re-layouts: none -> 6.35 us  [per_device(): total_acc = jnp.sum(part_acc * factors[..., None], axis=0)]
  transfers between devices with their start and end apart: 7 -> 6, of which waited for: 7 -> 6; matrix products, arithmetic and copies ran while one was open for 3% -> 2% of each run, Pallas kernels for 0% -> 0%
where the time goes in v1:
time: 495 us; the launch traced here: 492 us
  waiting for transfers between devices  261 us (53%)
  blocking collectives  110 us (22%)
  local copies, waits for them, and re-layouts  38.8 us (8%)
  matrix products  36.3 us (7%)
  other arithmetic  26 us (5%)
  between operations  14.8 us (3%)
    all_to_all x1, blocking collectives, per_device(): lax.all_to_all(outgoing, 'exp', split_axis=0, concat_axis=0, tiled=True)  71.6 us
    all_to_all x1, waiting for transfers between devices, per_device(): lax.all_to_all(result.reshape(received.shape), 'exp', split_axis=0, conca...  57.9 us
    reduce_scatter x1, waiting for transfers between devices, per_device(): lax.psum_scatter(layer_term, 'blk', scatter_dimension=1, tiled=True)  57.6 us
    all_gather x1, waiting for transfers between devices, per_device(): full_rows = lax.all_gather(hidden, 'blk', axis=1, tiled=True)  41.6 us
    all_to_all x1, blocking collectives, per_device(): lax.all_to_all(payload, 'blk', split_axis=0, concat_axis=0, tiled=True)  38.4 us
    all_gather x1, waiting for transfers between devices, per_device(): lax.all_gather(own_attention, 'blk', axis=0, tiled=True)  35 us
    all_gather x1, waiting for transfers between devices, per_device(): projected_all = lax.all_gather(projected, 'blk', axis=1, tiled=True)  34.1 us
    all_gather x1, waiting for transfers between devices, per_device(): mixed_rows = lax.all_gather(mixed_cols, 'blk', axis=1, tiled=True)  34 us
  transfers between devices with their start and end apart: 6, of which 6 were waited for; matrix products, arithmetic and copies ran while one was open for 2% of the time, Pallas kernels for 0%

profile of v1, /device:TPU:1, one launch (start us, length us, event | category | flops | bytes accessed | tf_op | source)
XLA Modules:
  0.0 491.7 jit_solution(17672671257017205096)
XLA Ops:
  8.0 41.6 %all-gather.5.cloned.1.call-done = bf16[256,2560]{0,1:T(8,128)(2,1)} async-done(((bf16[256,160]{0,1:T(8,128)(2,1)}), bf16[256,2560]{0,1:T(8,128)(2,1)}) %all-gather.5.cloned.1.call-update) | async-done | bytes 1310736 | tf_op jit(solution)/shard_map/all_gather | solution.py:89
  51.3 3.0 fusion.34
  56.6 34.1 %all-gather.7.cloned.1.call-done = bf16[256,3584]{0,1:T(8,128)(2,1)} async-done(((bf16[256,224]{0,1:T(8,128)(2,1)}), bf16[256,3584]{0,1:T(8,128)(2,1)}) %all-gather.7.cloned.1.call-update) | async-done | bytes 1835024 | tf_op jit(solution)/shard_map/all_gather | solution.py:94
  92.2 2.1 gather_fusion
  101.1 2.3 copy.59
  103.5 2.3 copy.60
  105.8 8.8 %fusion = (f32[256,4,5]{0,2,1:T(8,128)}, f32[4,512,256,5]{2,1,3,0:T(8,128)}) fusion(pred[256,512]{0,1:T(8,128)(4,1)} %broadcast_compare_fusion, bf16[512,4,128,1]{0,2,3,1:T(8,128)(2,1)S(1)} %bitcast.103, bf16[256,4,5,64]{3,0,2,1:T(8,128)(2,1)} %bitcast.101, bf16[256,4,5,64]{3,0,2,1:T(8,128)(2,1)} %bitcast.100), kind=kOutput, calls=%fused_computation.3 | convolution fusion | flops 681569280 | bytes 12472320 | tf_op jit(solution)/shard_map/tkgd,skd->tkgs/dot_general | solution.py:49
  115.5 6.1 %fusion.3 = f32[256,4,5]{0,2,1:T(8,128)S(1)} fusion(f32[4,512,256,5]{2,1,3,0:T(8,128)} %get-tuple-element.15, f32[256,4,5]{0,2,1:T(8,128)} %get-tuple-element.14, pred[256,512]{0,1:T(8,128)(4,1)} %broadcast_compare_fusion), kind=kLoop, calls=%fused_computation.6 | loop fusion | flops 10480640 | bytes 10657792 | tf_op jit(solution)/shard_map/reduce_sum | solution.py:55
  122.5 2.0 copy.57
  124.6 7.8 %fusion.22 = f32[256,4,5,128]{0,3,2,1:T(8,128)} fusion(bf16[512,4,128,1]{0,2,3,1:T(8,128)(2,1)} %bitcast.109, f32[4,512,256,5]{2,1,3,0:T(8,128)} %get-tuple-element.15, f32[256,4,5]{0,2,1:T(8,128)S(1)} %copy-done.11, pred[256,512]{0,1:T(8,128)(4,1)S(1)} %copy-done.2), kind=kOutput, calls=%fused_computation.35 | convolution fusion | flops 681574400 | bytes 13783040 | tf_op jit(solution)/shard_map/tkgs,skd->tkgd/dot_general | solution.py:56
  132.4 5.1 %copy.63 = f32[256,4,5,128]{3,2,1,0:T(8,128)} copy(f32[256,4,5,128]{0,3,2,1:T(8,128)} %fusion.22) | data formatting | bytes 5242880 | tf_op jit(solution)/shard_map/tkgs,skd->tkgd/transpose | solution.py:56
  137.6 4.7 concatenate.31
  142.5 4.0 concatenate.34
  146.6 38.4 %all_to_all.15 = f32[16,16,2600]{2,1,0:T(8,128)S(1)} all-to-all(f32[16,16,2600]{2,1,0:T(8,128)} %concatenate.34), channel_id=1, replica_groups=mesh['blk'=16,'exp'=16] {'blk'}, dimensions={0} | all-to-all | bytes 5324800 | tf_op jit(solution)/shard_map/all_to_all | solution.py:134
  186.6 2.2 mul.210
  188.8 4.2 mul.211
  193.0 2.8 fusion.20
  196.7 35.0 %all-gather.9.cloned.1.call-done = bf16[256,2560]{1,0:T(8,128)(2,1)} async-done(((bf16[16,2560]{1,0:T(8,128)(2,1)}), bf16[256,2560]{1,0:T(8,128)(2,1)}) %all-gather.9.cloned.1.call-update) | async-done | bytes 1310736 | tf_op jit(solution)/shard_map/all_gather | solution.py:146
  231.7 2.8 fusion.37
  236.3 34.0 %all-gather.11.cloned.1.call-done = bf16[256,2560]{0,1:T(8,128)(2,1)} async-done(((bf16[256,160]{0,1:T(8,128)(2,1)}), bf16[256,2560]{0,1:T(8,128)(2,1)}) %all-gather.11.cloned.1.call-update) | async-done | bytes 1310736 | tf_op jit(solution)/shard_map/all_gather | solution.py:151
  270.3 1.7 fusion.17
  272.0 2.0 convolution_convert_fusion.1
  274.2 71.6 %all_to_all.16 = bf16[16,32,2560]{2,1,0:T(8,128)(2,1)S(1)} all-to-all(bf16[16,32,2560]{2,1,0:T(8,128)(2,1)S(1)} %bitcast.98), channel_id=1, replica_groups=mesh['blk'=16,'exp'=16] {'exp'}, dimensions={0} | all-to-all | bytes 5242880 | tf_op jit(solution)/shard_map/all_to_all | solution.py:178
  345.8 2.2 fusion.12
  348.0 3.1 convolution_convert_fusion
  351.1 4.6 all-to-all-start.2
  356.0 3.3 fusion.44
  359.2 57.9 %all-to-all-done.2 = bf16[16,32,2560]{2,1,0:T(8,128)(2,1)} async-done(((bf16[16,32,2560]{2,1,0:T(8,128)(2,1)}), bf16[16,32,2560]{2,1,0:T(8,128)(2,1)}, u32[]{:S(2)}, u32[]{:S(2)}) %all-to-all-start.2) | async-done | bytes 2621472 | tf_op jit(solution)/shard_map/all_to_all | solution.py:185
  417.1 2.3 convert_reduce_fusion
  421.3 2.3 convolution_add_fusion
  423.7 2.4 broadcast_select_fusion
  426.0 57.6 %reduce-scatter.2.cloned.1.call-done = f32[256,160]{0,1:T(8,128)} async-done(((f32[256,2560]{0,1:T(8,128)}), f32[256,160]{0,1:T(8,128)}) %reduce-scatter.2.cloned.1.call-update) | async-done | bytes 163856 | tf_op jit(solution)/shard_map/reduce_scatter | solution.py:199
  (97 shorter events, 22.6 us)
Async XLA Ops:
  7.2 340.9 %copy-start = (bf16[1,384,2560]{2,1,0:T(8,128)(2,1)S(1)}, bf16[1,384,2560]{2,1,0:T(8,128)(2,1)}, u32[]{:S(2)}) copy-start(bf16[1,384,2560]{2,1,0:T(8,128)(2,1)} %param.27) | copy-start | bytes 5898244
  7.2 42.4 %all-gather.5.cloned.1.call-start = ((), (), s32[]{:S(2)}) async-start(), calls=%async_computation.4 | async-start | bytes 1392640 | tf_op jit(solution)/shard_map/all_gather | solution.py:89
  7.9 47.1 %copy-start.16 = (s32[1,64]{1,0:T(1,128)S(1)}, s32[1,64]{1,0:T(1,128)}, u32[]{:S(2)}) copy-start(s32[1,64]{1,0:T(1,128)} %param.19) | copy-start | bytes 772
  7.9 82.7 %all-gather.7.cloned.1.call-start = ((), (), s32[]{:S(2)}) async-start(), calls=%async_computation.5 | async-start | bytes 1949696 | tf_op jit(solution)/shard_map/all_gather | solution.py:94
  54.3 177.5 %all-gather.9.cloned.1.call-start = ((), (), s32[]{:S(2)}) async-start(), calls=%async_computation.6 | async-start | bytes 1392640 | tf_op jit(solution)/shard_map/all_gather | solution.py:146
  55.7 36.1 %copy-start.5 = (f32[256,64]{0,1:T(8,128)}, f32[256,64]{0,1:T(8,128)S(1)}, u32[]{:S(2)}) copy-start(f32[256,64]{0,1:T(8,128)S(1)} %get-tuple-element.12) | copy-start | bytes 196612
  55.8 36.1 %copy-start.7 = (f32[256,64]{0,1:T(8,128)}, f32[256,64]{0,1:T(8,128)S(1)}, u32[]{:S(2)}) copy-start(f32[256,64]{0,1:T(8,128)S(1)} %get-tuple-element.13) | copy-start | bytes 196612
  98.0 1.4 slice-start
  98.0 1.7 copy-start.6
  98.0 1.7 copy-start.8
  115.4 9.2 %copy-start.2 = (pred[256,512]{0,1:T(8,128)(4,1)S(1)}, pred[256,512]{0,1:T(8,128)(4,1)}, u32[]{:S(2)}) copy-start(pred[256,512]{0,1:T(8,128)(4,1)} %broadcast_compare_fusion) | copy-start | bytes 393220
  115.4 9.1 %copy-start.11 = (f32[256,4,5]{0,2,1:T(8,128)S(1)}, f32[256,4,5]{0,2,1:T(8,128)}, u32[]{:S(2)}) copy-start(f32[256,4,5]{0,2,1:T(8,128)} %get-tuple-element.14) | copy-start | bytes 61444
  137.6 4.9 %copy-start.9 = (f32[16,16,20]{2,1,0:T(8,128)S(1)}, f32[16,16,20]{2,1,0:T(8,128)}, u32[]{:S(2)}) copy-start(f32[16,16,20]{2,1,0:T(8,128)} %copy.65) | copy-start | bytes 61444
  184.9 1.6 copy-start.1
  193.0 38.8 %copy-start.10 = (bf16[256,160]{0,1:T(8,128)(2,1)S(1)}, bf16[256,160]{0,1:T(8,128)(2,1)}, u32[]{:S(2)}) copy-start(bf16[256,160]{0,1:T(8,128)(2,1)} %param.14) | copy-start | bytes 245764
  195.8 38.7 %copy-start.12 = (s32[256,6]{0,1:T(8,128)S(1)}, s32[256,6]{0,1:T(8,128)}, u32[]{:S(2)}) copy-start(s32[256,6]{0,1:T(8,128)} %param.22) | copy-start | bytes 18436
  195.8 76.2 %copy-start.15 = (f32[2560]{0:T(1024)S(1)}, f32[2560]{0:T(1024)}, u32[]{:S(2)}) copy-start(f32[2560]{0:T(1024)} %param.21) | copy-start | bytes 30724
  196.7 73.6 %all-gather.11.cloned.1.call-start = ((), (), s32[]{:S(2)}) async-start(), calls=%async_computation.7 | async-start | bytes 1392640 | tf_op jit(solution)/shard_map/all_gather | solution.py:151
  274.2 71.6 %copy-start.14 = (bf16[1,2560,768]{2,1,0:T(8,128)(2,1)S(1)}, bf16[1,2560,768]{2,1,0:T(8,128)(2,1)}, u32[]{:S(2)}) copy-start(bf16[1,2560,768]{2,1,0:T(8,128)(2,1)} %param.26) | copy-start | bytes 11796484
  351.1 4.6 copy-start.13
  351.1 66.0 %all-to-all-start.2 = ((bf16[16,32,2560]{2,1,0:T(8,128)(2,1)}), bf16[16,32,2560]{2,1,0:T(8,128)(2,1)}, u32[]{:S(2)}, u32[]{:S(2)}) async-start(bf16[16,32,2560]{2,1,0:T(8,128)(2,1)} %bitcast.104), calls=%async_computation.2 | async-start | bytes 5242880 | tf_op jit(solution)/shard_map/all_to_all | solution.py:185
  355.7 127.9 %reduce-scatter.2.cloned.1.call-start = ((), (), s32[]{:S(2)}) async-start(), calls=%async_computation.8 | async-start | bytes 2785280 | tf_op jit(solution)/shard_map/reduce_scatter | solution.py:199
  420.1 1.2 copy-start.3
  423.6 60.1 %copy-start.4 = (bf16[256,160]{0,1:T(8,128)(2,1)S(1)}, bf16[256,160]{0,1:T(8,128)(2,1)}, u32[]{:S(2)}) copy-start(bf16[256,160]{0,1:T(8,128)(2,1)} %fusion.37) | copy-start | bytes 245764
Sparse Core Ops, SparseCore 0:
  9.9 39.6 all-gather.4
  54.4 36.2 all-gather.6
  196.8 34.9 all-gather.8
  234.6 35.5 all-gather.10
  423.7 59.8 reduce-scatter.1

commit v2 on v1

--- a/solution.py
+++ b/solution.py
@@ -3,6 +3,8 @@
 import jax
 import jax.numpy as jnp
 from jax import lax
+from jax.experimental import pallas as pl
+from jax.experimental.pallas import tpu as pltpu
 from jax.sharding import PartitionSpec as P
 
 HEADS = 20
@@ -42,24 +44,80 @@
     )
 
 
-def partial_softmax(queries, query_pos, block_rows, key_pos):
+def attention_kernel(proj_ref, cos_ref, sin_ref, slot_ref, qpos_ref, kpos_ref, out_ref):
     key_width = KV_HEADS * HEAD_DIM
-    key_rows = block_rows[:, :key_width].reshape(-1, KV_HEADS, HEAD_DIM)
-    value_rows = block_rows[:, key_width:].reshape(-1, KV_HEADS, HEAD_DIM)
-    scores = jnp.einsum("tkgd,skd->tkgs", queries, key_rows, preferred_element_type=jnp.float32) * (
-        1.0 / math.sqrt(HEAD_DIM)
-    )
-    allowed = (key_pos[None, :] <= query_pos[:, None])[:, None, None, :]
-    maxima = jnp.max(jnp.where(allowed, scores, -1e30), axis=-1)
-    weights = jnp.where(allowed, jnp.exp(scores - maxima[..., None]), 0.0)
-    totals = jnp.sum(weights, axis=-1)
-    weighted = jnp.einsum(
-        "tkgs,skd->tkgd",
-        weights.astype(jnp.bfloat16),
-        value_rows,
-        preferred_element_type=jnp.float32,
-    )
-    return (maxima, totals, weighted)
+    group_size = HEADS // KV_HEADS
+    allowed = kpos_ref[...] <= qpos_ref[...]
+    cosine = cos_ref[...]
+    sine_signed = sin_ref[...]
+    lane = lax.broadcasted_iota(jnp.int32, (NEW, 128), 1)
+    stats = jnp.zeros((NEW, 128), jnp.float32)
+    for head in range(HEADS):
+        kv = head // group_size
+        raw = proj_ref[:, head * HEAD_DIM : (head + 1) * HEAD_DIM].astype(jnp.float32)
+        swapped = pltpu.roll(raw, HEAD_DIM // 2, 1)
+        query = (raw * cosine + swapped * sine_signed).astype(jnp.bfloat16)
+        keys = slot_ref[:, kv * HEAD_DIM : (kv + 1) * HEAD_DIM]
+        values = slot_ref[:, key_width + kv * HEAD_DIM : key_width + (kv + 1) * HEAD_DIM]
+        scores = lax.dot_general(
+            query, keys, (((1,), (1,)), ((), ())), preferred_element_type=jnp.float32
+        ) * (1.0 / math.sqrt(HEAD_DIM))
+        scores = jnp.where(allowed, scores, -1e30)
+        peak = jnp.max(scores, axis=1, keepdims=True)
+        probs = jnp.where(allowed, jnp.exp(scores - peak), 0.0)
+        total = jnp.sum(probs, axis=1, keepdims=True)
+        out_ref[:, head * HEAD_DIM : (head + 1) * HEAD_DIM] = jnp.dot(
+            probs.astype(jnp.bfloat16), values, preferred_element_type=jnp.float32
+        )
+        stats = jnp.where(lane == head, peak, stats)
+        stats = jnp.where(lane == HEADS + head, total, stats)
+    out_ref[:, HEADS * HEAD_DIM :] = stats
+
+
+def local_attention(projected_all, cosine, sine_signed, slot_rows, positions, key_pos):
+    width = HEADS * HEAD_DIM + 128
+    return pl.pallas_call(
+        attention_kernel,
+        out_shape=jax.ShapeDtypeStruct((NEW, width), jnp.float32),
+        in_specs=[pl.BlockSpec(memory_space=pltpu.VMEM)] * 6,
+        out_specs=pl.BlockSpec(memory_space=pltpu.VMEM),
+        cost_estimate=pl.CostEstimate(
+            flops=4 * NEW * slot_rows.shape[0] * HEAD_DIM * HEADS,
+            transcendentals=NEW * slot_rows.shape[0] * HEADS,
+            bytes_accessed=NEW * width * 4 + slot_rows.size * 2 + projected_all.size * 2,
+        ),
+    )(projected_all, cosine, sine_signed, slot_rows, positions[:, None], key_pos[None, :])
+
+
+def combine_kernel(part_ref, out_ref):
+    stats = part_ref[:, :, HEADS * HEAD_DIM :]
+    overall = jnp.max(stats, axis=0, keepdims=True)
+    factors = jnp.exp(stats - overall)
+    lane = lax.broadcasted_iota(jnp.int32, stats.shape, 2)
+    for head in range(HEADS):
+        factor = jnp.sum(jnp.where(lane == head, factors, 0.0), axis=2, keepdims=True)
+        total = jnp.sum(jnp.where(lane == HEADS + head, stats, 0.0), axis=2, keepdims=True)
+        denominator = jnp.sum(factor * total, axis=0)
+        numerator = jnp.sum(
+            part_ref[:, :, head * HEAD_DIM : (head + 1) * HEAD_DIM] * factor, axis=0
+        )
+        out_ref[:, head * HEAD_DIM : (head + 1) * HEAD_DIM] = (
+            numerator / denominator
+        ).astype(out_ref.dtype)
+
+
+def combine_attention(parts):
+    sources, rows, width = parts.shape
+    return pl.pallas_call(
+        combine_kernel,
+        out_shape=jax.ShapeDtypeStruct((rows, HEADS * HEAD_DIM), jnp.bfloat16),
+        in_specs=[pl.BlockSpec(memory_space=pltpu.VMEM)],
+        out_specs=pl.BlockSpec(memory_space=pltpu.VMEM),
+        cost_estimate=pl.CostEstimate(
+            flops=3 * parts.size, transcendentals=sources * rows * 128,
+            bytes_accessed=parts.size * 4 + rows * HEADS * HEAD_DIM * 2,
+        ),
+    )(parts)
 
 
 def per_device(
@@ -94,9 +152,6 @@
     projected_all = lax.all_gather(projected, "blk", axis=1, tiled=True)
     length = cache_lens[0]
     positions = length + jnp.arange(NEW, dtype=jnp.int32)
-    queries = rotate(
-        projected_all[:, :query_width].astype(jnp.float32).reshape(NEW, HEADS, HEAD_DIM), positions
-    ).astype(jnp.bfloat16)
     fresh_keys = rotate(
         projected_all[:, query_width : query_width + key_width]
         .astype(jnp.float32)
@@ -120,28 +175,19 @@
     written = (offset >= 0) & (offset < NEW)
     picked = appended[jnp.clip(offset, 0, NEW - 1)]
     pool_out = jnp.where(written[:, :, None], picked, kv_pool[0])
-    grouped = queries.reshape(NEW, KV_HEADS, group_size, HEAD_DIM)
+    half_dim = HEAD_DIM // 2
+    frequency = rope_base ** (-(jnp.arange(half_dim).astype(jnp.float32) * 2.0 / HEAD_DIM))
+    angles = positions.astype(jnp.float32)[:, None] * frequency[None, :]
+    cosine = jnp.cos(angles)
+    sine_vals = jnp.sin(angles)
+    cosine_full = jnp.concatenate([cosine, cosine], axis=1)
+    sine_signed = jnp.concatenate([-sine_vals, sine_vals], axis=1)
     slot_rows = pool_out.reshape(local_pages * PAGE, 2 * key_width)
-    maxima, totals, weighted = partial_softmax(grouped, positions, slot_rows, local_pos.reshape(-1))
-    payload = jnp.concatenate(
-        [
-            weighted.reshape(NEW, query_width),
-            maxima.reshape(NEW, HEADS),
-            totals.reshape(NEW, HEADS),
-        ],
-        axis=1,
-    ).reshape(blocks, own_rows, query_width + 2 * HEADS)
+    payload = local_attention(
+        projected_all, cosine_full, sine_signed, slot_rows, positions, local_pos.reshape(-1)
+    ).reshape(blocks, own_rows, query_width + 128)
     gathered = lax.all_to_all(payload, "blk", split_axis=0, concat_axis=0, tiled=True)
-    part_acc = gathered[:, :, :query_width].reshape(blocks, own_rows, HEADS, HEAD_DIM)
-    part_max = gathered[:, :, query_width : query_width + HEADS]
-    part_sum = gathered[:, :, query_width + HEADS :]
-    overall = jnp.max(part_max, axis=0)
-    factors = jnp.exp(part_max - overall[None])
-    total_sum = jnp.sum(part_sum * factors, axis=0)
-    total_acc = jnp.sum(part_acc * factors[..., None], axis=0)
-    own_attention = (
-        (total_acc / total_sum[..., None]).reshape(own_rows, query_width).astype(jnp.bfloat16)
-    )
+    own_attention = combine_attention(gathered)
     attended = jnp.dot(
         lax.all_gather(own_attention, "blk", axis=0, tiled=True),
         out_weight,

time: 495 us -> 453 us (0.915)
  local copies, waits for them, and re-layouts: 38.8 us -> 9.36 us
  matrix products: 36.3 us -> 19.7 us
  Pallas kernels: 0 us -> 14.4 us
  other arithmetic: 26 us -> 17.5 us
    dot_general x2 -> x0, matrix products: 16.6 us -> none  [the longest x1 8.78 us: partial_softmax(): jnp.einsum('tkgd,skd->tkgs', queries, key_rows, preferred_element_type=jn...]
    pallas_call x0 -> x2, Pallas kernels: none -> 14.4 us  [the longest x1 10.5 us: local_attention(): pl.pallas_call(attention_kernel, out_shape=jax.ShapeDtypeStruct((NEW, wid...]
    concatenate x7 -> x0, local copies, waits for them, and re-layouts: 11 us -> none  [the longest x6 10.8 us: per_device(): jnp.concatenate([weighted.reshape(NEW, query_width), maxima.reshape(NEW,...]
    reduce_sum x3 -> x0, other arithmetic: 9.08 us -> none  [the longest x1 6.14 us: partial_softmax(): totals = jnp.sum(weights, axis=-1)]
    mul x2 -> x0, local copies, waits for them, and re-layouts: 6.35 us -> none  [per_device(): total_acc = jnp.sum(part_acc * factors[..., None], axis=0)]
    transpose x1 -> x0, local copies, waits for them, and re-layouts: 5.14 us -> none  [partial_softmax(): jnp.einsum('tkgs,skd->tkgd', weights.astype(jnp.bfloat16), value_rows, pr...]
    slice x7 -> x5, local copies, waits for them, and re-layouts: 5.91 us -> 0.93 us  [the longest x1 0.74 us: rotate(): upper_half = inputs[..., half_dim:]]
where the time goes in v2:
time: 453 us; the launch traced here: 450 us
  waiting for transfers between devices  259 us (57%)
  blocking collectives  110 us (24%)
  matrix products  19.7 us (4%)
  other arithmetic  17.5 us (4%)
  between operations  14.7 us (3%)
  Pallas kernels  14.4 us (3%)
  local copies, waits for them, and re-layouts  9.36 us (2%)
  starting transfers between devices  4.78 us (1%)
    all_to_all x1, blocking collectives, per_device(): lax.all_to_all(outgoing, 'exp', split_axis=0, concat_axis=0, tiled=True)  71.6 us
    all_to_all x1, waiting for transfers between devices, per_device(): lax.all_to_all(result.reshape(received.shape), 'exp', split_axis=0, conca...  57.9 us
    reduce_scatter x1, waiting for transfers between devices, per_device(): lax.psum_scatter(layer_term, 'blk', scatter_dimension=1, tiled=True)  57.6 us
    all_gather x1, waiting for transfers between devices, per_device(): full_rows = lax.all_gather(hidden, 'blk', axis=1, tiled=True)  41.6 us
    all_to_all x1, blocking collectives, per_device(): lax.all_to_all(payload, 'blk', split_axis=0, concat_axis=0, tiled=True)  38.9 us
    all_gather x1, waiting for transfers between devices, per_device(): lax.all_gather(own_attention, 'blk', axis=0, tiled=True)  35 us
    all_gather x1, waiting for transfers between devices, per_device(): mixed_rows = lax.all_gather(mixed_cols, 'blk', axis=1, tiled=True)  34 us
    all_gather x1, waiting for transfers between devices, per_device(): projected_all = lax.all_gather(projected, 'blk', axis=1, tiled=True)  32.6 us
  transfers between devices with their start and end apart: 6, of which 6 were waited for; matrix products, arithmetic and copies ran while one was open for 2% of the time, Pallas kernels for 0%

profile of v2, /device:TPU:1, one launch (start us, length us, event | category | flops | bytes accessed | tf_op | source)
XLA Modules:
  0.0 450.3 jit_solution(2943285629791819566)
XLA Ops:
  7.2 0.7 all-gather.5.cloned.1.call-update
  8.0 41.6 %all-gather.5.cloned.1.call-done = bf16[256,2560]{0,1:T(8,128)(2,1)} async-done(((bf16[256,160]{0,1:T(8,128)(2,1)}), bf16[256,2560]{0,1:T(8,128)(2,1)}) %all-gather.5.cloned.1.call-update) | async-done | bytes 1310736 | tf_op jit(solution)/shard_map/all_gather | solution.py:147
  49.6 1.7 fusion.3
  51.3 3.0 fusion.15
  55.3 0.7 iota_add_fusion.qpos_ref
  56.5 0.8 pad_maximum_fusion.2
  58.1 32.6 %all-gather.7.cloned.1.call-done = bf16[256,3584]{0,1:T(8,128)(2,1)} async-done(((bf16[256,224]{0,1:T(8,128)(2,1)}), bf16[256,3584]{0,1:T(8,128)(2,1)}) %all-gather.7.cloned.1.call-update) | async-done | bytes 1835024 | tf_op jit(solution)/shard_map/all_gather | solution.py:152
  90.7 3.9 copy.40.proj_ref
  94.6 0.7 fusion.45
  95.6 1.2 copy.46
  97.6 2.1 gather_fusion
  99.6 2.4 bitcast_select_fusion.slot_ref
  102.0 10.5 %shard_map.149 = f32[256,2688]{1,0:T(8,128)} custom-call(bf16[256,3584]{1,0:T(8,128)(2,1)} %copy.40.proj_ref, f32[256,128]{1,0:T(8,128)} %get-tuple-element.9.cos_ref, f32[256,128]{1,0:T(8,128)} %get-tuple-element.10.sin_ref, bf16[512,1024]{1,0:T(8,128)(2,1)} %bitcast_select_fusion.slot_ref, s32[256,1]{1,0:T(8,128)} %iota_add_fusion.qpos_ref, s32[1,512]{1,0:T(1,128)} %bitcast.76), custom_call_target="tpu_custom_call" | custom-call | flops 1342177280 | bytes 5636096 | tf_op jit(solution)/shard_map/pallas_call | solution.py:79
  112.5 38.9 %all_to_all.15.part_ref = f32[16,16,2688]{2,1,0:T(8,128)} all-to-all(f32[16,16,2688]{2,1,0:T(8,128)} %bitcast.59), channel_id=1, replica_groups=mesh['blk'=16,'exp'=16] {'blk'}, dimensions={0} | all-to-all | bytes 5505024 | tf_op jit(solution)/shard_map/all_to_all | solution.py:189
  151.4 3.9 shard_map.150
  155.4 35.0 %all-gather.9.cloned.1.call-done = bf16[256,2560]{1,0:T(8,128)(2,1)} async-done(((bf16[16,2560]{1,0:T(8,128)(2,1)}), bf16[256,2560]{1,0:T(8,128)(2,1)}) %all-gather.9.cloned.1.call-update) | async-done | bytes 1310736 | tf_op jit(solution)/shard_map/all_gather | solution.py:192
  190.4 2.7 fusion.18
  193.3 1.2 reduce-window.6
  194.9 34.0 %all-gather.11.cloned.1.call-done = bf16[256,2560]{0,1:T(8,128)(2,1)} async-done(((bf16[256,160]{0,1:T(8,128)(2,1)}), bf16[256,2560]{0,1:T(8,128)(2,1)}) %all-gather.11.cloned.1.call-update) | async-done | bytes 1310736 | tf_op jit(solution)/shard_map/all_gather | solution.py:197
  228.9 1.7 fusion.6
  230.6 2.0 convolution_convert_fusion.1
  232.8 71.6 %all_to_all.16 = bf16[16,32,2560]{2,1,0:T(8,128)(2,1)S(1)} all-to-all(bf16[16,32,2560]{2,1,0:T(8,128)(2,1)S(1)} %bitcast.60), channel_id=1, replica_groups=mesh['blk'=16,'exp'=16] {'exp'}, dimensions={0} | all-to-all | bytes 5242880 | tf_op jit(solution)/shard_map/all_to_all | solution.py:224
  304.5 2.2 fusion.1
  306.7 3.1 convolution_convert_fusion
  309.7 4.6 %all-to-all-start.2 = ((bf16[16,32,2560]{2,1,0:T(8,128)(2,1)}), bf16[16,32,2560]{2,1,0:T(8,128)(2,1)}, u32[]{:S(2)}, u32[]{:S(2)}) async-start(bf16[16,32,2560]{2,1,0:T(8,128)(2,1)} %bitcast.62), calls=%async_computation.2 | async-start | bytes 5242880 | tf_op jit(solution)/shard_map/all_to_all | solution.py:231
  314.6 3.3 fusion.25
  317.8 57.9 %all-to-all-done.2 = bf16[16,32,2560]{2,1,0:T(8,128)(2,1)} async-done(((bf16[16,32,2560]{2,1,0:T(8,128)(2,1)}), bf16[16,32,2560]{2,1,0:T(8,128)(2,1)}, u32[]{:S(2)}, u32[]{:S(2)}) %all-to-all-start.2) | async-done | bytes 2621472 | tf_op jit(solution)/shard_map/all_to_all | solution.py:231
  375.7 2.3 convert_reduce_fusion
  379.9 2.3 convolution_add_fusion
  382.3 2.4 broadcast_select_fusion
  384.6 57.6 %reduce-scatter.2.cloned.1.call-done = f32[256,160]{0,1:T(8,128)} async-done(((f32[256,2560]{0,1:T(8,128)}), f32[256,160]{0,1:T(8,128)}) %reduce-scatter.2.cloned.1.call-update) | async-done | bytes 163856 | tf_op jit(solution)/shard_map/reduce_scatter | solution.py:245
  442.2 1.6 add_convert_fusion.1
  (64 shorter events, 5.7 us)
Async XLA Ops:
  7.2 299.5 %copy-start = (bf16[1,384,2560]{2,1,0:T(8,128)(2,1)S(1)}, bf16[1,384,2560]{2,1,0:T(8,128)(2,1)}, u32[]{:S(2)}) copy-start(bf16[1,384,2560]{2,1,0:T(8,128)(2,1)} %param.27) | copy-start | bytes 5898244
  7.2 42.4 %all-gather.5.cloned.1.call-start = ((), (), s32[]{:S(2)}) async-start(), calls=%async_computation.4 | async-start | bytes 1392640 | tf_op jit(solution)/shard_map/all_gather | solution.py:147
  7.9 82.7 %all-gather.7.cloned.1.call-start = ((), (), s32[]{:S(2)}) async-start(), calls=%async_computation.5 | async-start | bytes 1949696 | tf_op jit(solution)/shard_map/all_gather | solution.py:152
  51.3 3.7 copy-start.8
  54.3 136.1 %all-gather.9.cloned.1.call-start = ((), (), s32[]{:S(2)}) async-start(), calls=%async_computation.6 | async-start | bytes 1392640 | tf_op jit(solution)/shard_map/all_gather | solution.py:192
  90.7 3.9 slice-start.1
  95.5 1.9 slice-start
  151.4 39.0 %copy-start.3 = (bf16[256,160]{0,1:T(8,128)(2,1)S(1)}, bf16[256,160]{0,1:T(8,128)(2,1)}, u32[]{:S(2)}) copy-start(bf16[256,160]{0,1:T(8,128)(2,1)} %param.14) | copy-start | bytes 245764
  151.4 41.7 %copy-start.4 = (s32[256,6]{0,1:T(8,128)S(1)}, s32[256,6]{0,1:T(8,128)}, u32[]{:S(2)}) copy-start(s32[256,6]{0,1:T(8,128)} %param.22) | copy-start | bytes 18436
  155.3 75.3 %copy-start.7 = (f32[2560]{0:T(1024)S(1)}, f32[2560]{0:T(1024)}, u32[]{:S(2)}) copy-start(f32[2560]{0:T(1024)} %param.21) | copy-start | bytes 30724
  155.3 73.6 %all-gather.11.cloned.1.call-start = ((), (), s32[]{:S(2)}) async-start(), calls=%async_computation.7 | async-start | bytes 1392640 | tf_op jit(solution)/shard_map/all_gather | solution.py:197
  232.8 71.6 %copy-start.6 = (bf16[1,2560,768]{2,1,0:T(8,128)(2,1)S(1)}, bf16[1,2560,768]{2,1,0:T(8,128)(2,1)}, u32[]{:S(2)}) copy-start(bf16[1,2560,768]{2,1,0:T(8,128)(2,1)} %param.26) | copy-start | bytes 11796484
  309.7 4.6 %copy-start.5 = (f32[256,6]{0,1:T(8,128)S(1)}, f32[256,6]{0,1:T(8,128)}, u32[]{:S(2)}) copy-start(f32[256,6]{0,1:T(8,128)} %param.23) | copy-start | bytes 18436
  309.7 66.0 %all-to-all-start.2 = ((bf16[16,32,2560]{2,1,0:T(8,128)(2,1)}), bf16[16,32,2560]{2,1,0:T(8,128)(2,1)}, u32[]{:S(2)}, u32[]{:S(2)}) async-start(bf16[16,32,2560]{2,1,0:T(8,128)(2,1)} %bitcast.62), calls=%async_computation.2 | async-start | bytes 5242880 | tf_op jit(solution)/shard_map/all_to_all | solution.py:231
  314.3 127.9 %reduce-scatter.2.cloned.1.call-start = ((), (), s32[]{:S(2)}) async-start(), calls=%async_computation.8 | async-start | bytes 2785280 | tf_op jit(solution)/shard_map/reduce_scatter | solution.py:245
  378.7 1.2 copy-start.1
  382.2 60.1 %copy-start.2 = (bf16[256,160]{0,1:T(8,128)(2,1)S(1)}, bf16[256,160]{0,1:T(8,128)(2,1)}, u32[]{:S(2)}) copy-start(bf16[256,160]{0,1:T(8,128)(2,1)} %fusion.18) | copy-start | bytes 245764
Sparse Core Ops, SparseCore 0:
  9.9 39.6 all-gather.4
  54.4 36.2 all-gather.6
  155.5 34.8 all-gather.8
  193.3 35.5 all-gather.10
  382.3 59.8 reduce-scatter.1

commit v3 on v2

--- a/solution.py
+++ b/solution.py
@@ -120,6 +120,21 @@
     )(parts)
 
 
+def gather_blocks(values, axis):
+    count = lax.axis_size("blk")
+    stacked = jnp.broadcast_to(values[None], (count,) + values.shape)
+    received = lax.all_to_all(stacked, "blk", split_axis=0, concat_axis=0, tiled=True)
+    return jnp.concatenate([received[i] for i in range(count)], axis=axis)
+
+
+def scatter_sum_blocks(values):
+    count = lax.axis_size("blk")
+    rows, width = values.shape
+    pieces = values.reshape(rows, count, width // count).transpose(1, 0, 2)
+    received = lax.all_to_all(pieces, "blk", split_axis=0, concat_axis=0, tiled=True)
+    return jnp.sum(received, axis=0)
+
+
 def per_device(
     hidden,
     attn_gain,
@@ -144,12 +159,12 @@
     key_width = KV_HEADS * HEAD_DIM
     group_size = HEADS // KV_HEADS
     own_rows = NEW // blocks
-    full_rows = lax.all_gather(hidden, "blk", axis=1, tiled=True)
+    full_rows = gather_blocks(hidden, 1)
     attn_in = normalize(full_rows, attn_gain)
     projected = jnp.dot(attn_in, qkv_weight, preferred_element_type=jnp.float32).astype(
         jnp.bfloat16
     )
-    projected_all = lax.all_gather(projected, "blk", axis=1, tiled=True)
+    projected_all = gather_blocks(projected, 1)
     length = cache_lens[0]
     positions = length + jnp.arange(NEW, dtype=jnp.int32)
     fresh_keys = rotate(
@@ -189,12 +204,12 @@
     gathered = lax.all_to_all(payload, "blk", split_axis=0, concat_axis=0, tiled=True)
     own_attention = combine_attention(gathered)
     attended = jnp.dot(
-        lax.all_gather(own_attention, "blk", axis=0, tiled=True),
+        gather_blocks(own_attention, 0),
         out_weight,
         preferred_element_type=jnp.float32,
     )
     mixed_cols = (hidden.astype(jnp.float32) + attended).astype(jnp.bfloat16)
-    mixed_rows = lax.all_gather(mixed_cols, "blk", axis=1, tiled=True)
+    mixed_rows = gather_blocks(mixed_cols, 1)
     ffn_in = normalize(mixed_rows, ffn_gain)
     shared_cols = shared_gate_up.shape[2]
     gate_up = jnp.dot(
@@ -242,7 +257,7 @@
         "ect,ecd->td", selector, upper_part, preferred_element_type=jnp.float32
     ) + jnp.einsum("ect,ecd->td", selector, lower_part, preferred_element_type=jnp.float32)
     layer_term = shared_term + routed
-    summed_cols = lax.psum_scatter(layer_term, "blk", scatter_dimension=1, tiled=True)
+    summed_cols = scatter_sum_blocks(layer_term)
     hidden_out = (mixed_cols.astype(jnp.float32) + summed_cols).astype(jnp.bfloat16)
     return (hidden_out, pool_out[None])
 

time: 453 us -> 410 us (0.905)
  waiting for transfers between devices: 259 us -> 128 us
  blocking collectives: 110 us -> 159 us
  local copies, waits for them, and re-layouts: 9.36 us -> 49.9 us
  starting transfers between devices: 4.78 us -> 22.2 us
  between operations: 14.7 us -> 1.97 us
  matrix products: 19.7 us -> 13.6 us
    all_gather x4 -> x0, waiting for transfers between devices: 143 us -> none  [the longest x1 41.6 us: per_device(): full_rows = lax.all_gather(hidden, 'blk', axis=1, tiled=True)]
    all_to_all x0 -> x3, waiting for transfers between devices: none -> 69.9 us  [the longest x2 38.5 us: gather_blocks(): lax.all_to_all(stacked, 'blk', split_axis=0, concat_axis=0, tiled=True)]
    reduce_scatter x1 -> x0, waiting for transfers between devices: 57.6 us -> none  [per_device(): lax.psum_scatter(layer_term, 'blk', scatter_dimension=1, tiled=True)]
    all_to_all x0 -> x2, blocking collectives: none -> 46.7 us  [gather_blocks(): lax.all_to_all(stacked, 'blk', split_axis=0, concat_axis=0, tiled=True)]
    unnamed x22 -> x117, local copies, waits for them, and re-layouts: 2.1 us -> 31.6 us
    all_to_all x0 -> x3, starting transfers between devices: none -> 17.3 us  [the longest x2 10.5 us: gather_blocks(): lax.all_to_all(stacked, 'blk', split_axis=0, concat_axis=0, tiled=True)]
    concatenate x0 -> x4, local copies, waits for them, and re-layouts: none -> 4.91 us  [gather_blocks(): return jnp.concatenate([received[i] for i in range(count)], axis=axis)]
    broadcast_in_dim x0 -> x4, local copies, waits for them, and re-layouts: none -> 4.75 us  [gather_blocks(): stacked = jnp.broadcast_to(values[None], (count,) + values.shape)]
  transfers between devices with their start and end apart: 6 -> 4, of which waited for: 6 -> 4; matrix products, arithmetic and copies ran while one was open for 2% -> 3% of each run, Pallas kernels for 0% -> 0%
where the time goes in v3:
time: 410 us; the launch traced here: 405 us
  blocking collectives  159 us (39%)
  waiting for transfers between devices  128 us (31%)
  local copies, waits for them, and re-layouts  49.9 us (12%)
  starting transfers between devices  22.2 us (5%)
  other arithmetic  16.3 us (4%)
  Pallas kernels  14.4 us (4%)
  matrix products  13.6 us (3%)
    all_to_all x1, blocking collectives, per_device(): lax.all_to_all(outgoing, 'exp', split_axis=0, concat_axis=0, tiled=True)  72.6 us
    all_to_all x1, waiting for transfers between devices, per_device(): lax.all_to_all(result.reshape(received.shape), 'exp', split_axis=0, conca...  57.8 us
    all_to_all x2, blocking collectives, gather_blocks(): lax.all_to_all(stacked, 'blk', split_axis=0, concat_axis=0, tiled=True)  46.7 us
    all_to_all x1, blocking collectives, per_device(): lax.all_to_all(payload, 'blk', split_axis=0, concat_axis=0, tiled=True)  39.6 us
    all_to_all x2, waiting for transfers between devices, gather_blocks(): lax.all_to_all(stacked, 'blk', split_axis=0, concat_axis=0, tiled=True)  38.5 us
    unnamed x117, local copies, waits for them, and re-layouts  31.6 us
    all_to_all x1, waiting for transfers between devices, scatter_sum_blocks(): lax.all_to_all(pieces, 'blk', split_axis=0, concat_axis=0, tiled=True)  31.4 us
    pallas_call x1, Pallas kernels, local_attention(): pl.pallas_call(attention_kernel, out_shape=jax.ShapeDtypeStruct((NEW, wid...  10.5 us
  transfers between devices with their start and end apart: 4, of which 4 were waited for; matrix products, arithmetic and copies ran while one was open for 3% of the time, Pallas kernels for 0%

profile of v3, /device:TPU:1, one launch (start us, length us, event | category | flops | bytes accessed | tf_op | source)
XLA Modules:
  0.0 405.0 jit_solution(12523958300856993343)
XLA Ops:
  1.8 25.1 %all_to_all.40 = bf16[16,256,160]{1,2,0:T(8,128)(2,1)S(1)} all-to-all(bf16[16,256,160]{1,2,0:T(8,128)(2,1)S(1)} %broadcast_in_dim.40), channel_id=1, replica_groups=mesh['blk'=16,'exp'=16] {'blk'}, dimensions={0} | all-to-all | bytes 2621440 | tf_op jit(solution)/shard_map/all_to_all | solution.py:126
  29.0 1.4 broadcast_in_dim.41
  30.4 5.3 %all-to-all-start.1 = ((bf16[16,256,224]{1,2,0:T(8,128)(2,1)}), bf16[16,256,224]{1,2,0:T(8,128)(2,1)}, u32[]{:S(2)}, u32[]{:S(2)}) async-start(bf16[16,256,224]{1,2,0:T(8,128)(2,1)} %broadcast_in_dim.41), calls=%async_computation.1 | async-start | bytes 3670016 | tf_op jit(solution)/shard_map/all_to_all | solution.py:126
  39.4 21.3 %all-to-all-done.1 = bf16[16,256,224]{1,2,0:T(8,128)(2,1)} async-done(((bf16[16,256,224]{1,2,0:T(8,128)(2,1)}), bf16[16,256,224]{1,2,0:T(8,128)(2,1)}, u32[]{:S(2)}, u32[]{:S(2)}) %all-to-all-start.1) | async-done | bytes 1835040 | tf_op jit(solution)/shard_map/all_to_all | solution.py:126
  60.7 2.6 fusion.50
  67.7 1.7 copy.75
  69.4 1.6 copy.76
  71.0 1.7 copy.77
  72.7 1.7 copy.78
  79.8 2.1 gather_fusion
  81.9 2.4 bitcast_select_fusion.slot_ref
  84.4 4.0 concatenate.32.proj_ref
  88.4 10.5 %shard_map.149 = f32[256,2688]{1,0:T(8,128)} custom-call(bf16[256,3584]{1,0:T(8,128)(2,1)} %concatenate.32.proj_ref, f32[256,128]{1,0:T(8,128)} %get-tuple-element.23.cos_ref, f32[256,128]{1,0:T(8,128)} %get-tuple-element.24.sin_ref, bf16[512,1024]{1,0:T(8,128)(2,1)} %bitcast_select_fusion.slot_ref, s32[256,1]{1,0:T(8,128)} %iota_add_fusion.qpos_ref, ...), custom_call_target="tpu_custom_call" | custom-call | flops 1342177280 | bytes 5636096 | tf_op jit(solution)/shard_map/pallas_call | solution.py:79
  98.9 39.6 %all_to_all.41.part_ref = f32[16,16,2688]{2,1,0:T(8,128)} all-to-all(f32[16,16,2688]{2,1,0:T(8,128)} %bitcast.268), channel_id=1, replica_groups=mesh['blk'=16,'exp'=16] {'blk'}, dimensions={0} | all-to-all | bytes 5505024 | tf_op jit(solution)/shard_map/all_to_all | solution.py:204
  138.5 3.9 shard_map.150
  143.4 21.6 %all_to_all.42 = bf16[16,16,2560]{2,1,0:T(8,128)(2,1)S(1)} all-to-all(bf16[16,16,2560]{2,1,0:T(8,128)(2,1)S(1)} %broadcast_in_dim.45), channel_id=1, replica_groups=mesh['blk'=16,'exp'=16] {'blk'}, dimensions={0} | all-to-all | bytes 2621440 | tf_op jit(solution)/shard_map/all_to_all | solution.py:126
  167.9 5.3 %all-to-all-start.4 = ((bf16[16,256,160]{1,2,0:T(8,128)(2,1)}), bf16[16,256,160]{1,2,0:T(8,128)(2,1)}, u32[]{:S(2)}, u32[]{:S(2)}) async-start(bf16[16,256,160]{1,2,0:T(8,128)(2,1)} %broadcast_in_dim.46), calls=%async_computation.4 | async-start | bytes 2621440 | tf_op jit(solution)/shard_map/all_to_all | solution.py:126
  173.3 1.2 reduce-window.6
  174.9 17.1 %all-to-all-done.4 = bf16[16,256,160]{1,2,0:T(8,128)(2,1)} async-done(((bf16[16,256,160]{1,2,0:T(8,128)(2,1)}), bf16[16,256,160]{1,2,0:T(8,128)(2,1)}, u32[]{:S(2)}, u32[]{:S(2)}) %all-to-all-start.4) | async-done | bytes 1310752 | tf_op jit(solution)/shard_map/all_to_all | solution.py:126
  208.3 72.6 %all_to_all.43 = bf16[16,32,2560]{2,1,0:T(8,128)(2,1)S(1)} all-to-all(bf16[16,32,2560]{2,1,0:T(8,128)(2,1)S(1)} %bitcast.270), channel_id=1, replica_groups=mesh['blk'=16,'exp'=16] {'exp'}, dimensions={0} | all-to-all | bytes 5242880 | tf_op jit(solution)/shard_map/all_to_all | solution.py:239
  281.0 2.2 fusion.1
  283.2 3.0 convolution_convert_fusion
  286.2 4.9 %all-to-all-start.6 = ((bf16[16,32,2560]{2,1,0:T(8,128)(2,1)}), bf16[16,32,2560]{2,1,0:T(8,128)(2,1)}, u32[]{:S(2)}, u32[]{:S(2)}) async-start(bf16[16,32,2560]{2,1,0:T(8,128)(2,1)} %bitcast.272), calls=%async_computation.6 | async-start | bytes 5242880 | tf_op jit(solution)/shard_map/all_to_all | solution.py:246
  291.3 3.3 fusion.29
  294.6 57.8 %all-to-all-done.6 = bf16[16,32,2560]{2,1,0:T(8,128)(2,1)} async-done(((bf16[16,32,2560]{2,1,0:T(8,128)(2,1)}), bf16[16,32,2560]{2,1,0:T(8,128)(2,1)}, u32[]{:S(2)}, u32[]{:S(2)}) %all-to-all-start.6) | async-done | bytes 2621472 | tf_op jit(solution)/shard_map/all_to_all | solution.py:246
  352.3 2.3 convert_reduce_fusion
  356.5 2.1 convolution_add_fusion
  358.5 3.2 copy.72
  361.8 6.8 %all-to-all-start.7 = ((f32[16,256,160]{1,2,0:T(8,128)}), f32[16,256,160]{1,2,0:T(8,128)}, u32[]{:S(2)}, u32[]{:S(2)}) async-start(f32[16,256,160]{1,2,0:T(8,128)} %bitcast.269), calls=%async_computation.7 | async-start | bytes 5242880 | tf_op jit(solution)/shard_map/all_to_all | solution.py:134
  368.7 2.4 broadcast_select_fusion
  371.0 31.4 %all-to-all-done.7 = f32[16,256,160]{1,2,0:T(8,128)} async-done(((f32[16,256,160]{1,2,0:T(8,128)}), f32[16,256,160]{1,2,0:T(8,128)}, u32[]{:S(2)}, u32[]{:S(2)}) %all-to-all-start.7) | async-done | bytes 2621472 | tf_op jit(solution)/shard_map/all_to_all | solution.py:134
  402.4 1.9 reduce_sum.69
  (159 shorter events, 39.1 us)
Async XLA Ops:
  0.6 282.5 %copy-start = (bf16[1,384,2560]{2,1,0:T(8,128)(2,1)S(1)}, bf16[1,384,2560]{2,1,0:T(8,128)(2,1)}, u32[]{:S(2)}) copy-start(bf16[1,384,2560]{2,1,0:T(8,128)(2,1)} %param.27) | copy-start | bytes 5898244
  27.0 1.3 copy-start.23
  27.0 1.3 copy-start.24
  30.4 5.9 %copy-start.26 = (s32[1,64]{1,0:T(1,128)S(1)}, s32[1,64]{1,0:T(1,128)}, u32[]{:S(2)}) copy-start(s32[1,64]{1,0:T(1,128)} %param.19) | copy-start | bytes 772
  30.4 30.3 %all-to-all-start.1 = ((bf16[16,256,224]{1,2,0:T(8,128)(2,1)}), bf16[16,256,224]{1,2,0:T(8,128)(2,1)}, u32[]{:S(2)}, u32[]{:S(2)}) async-start(bf16[16,256,224]{1,2,0:T(8,128)(2,1)} %broadcast_in_dim.41), calls=%async_computation.1 | async-start | bytes 3670016 | tf_op jit(solution)/shard_map/all_to_all | solution.py:126
  63.4 0.6 copy-start.4
  63.5 0.7 copy-start.6
  63.7 16.0 %copy-start.1 = (bf16[1,256,224]{2,1,0:T(8,128)(2,1)}, bf16[1,256,224]{2,1,0:T(8,128)(2,1)S(1)}, u32[]{:S(2)}) copy-start(bf16[1,256,224]{2,1,0:T(8,128)(2,1)S(1)} %copy.88) | copy-start | bytes 344068
  65.0 9.3 %copy-start.18 = (bf16[1,256,224]{1,2,0:T(8,128)(2,1)S(1)}, bf16[1,256,224]{1,2,0:T(8,128)(2,1)}, u32[]{:S(2)}) copy-start(bf16[1,256,224]{1,2,0:T(8,128)(2,1)} %get-tuple-element.13) | copy-start | bytes 344068
  65.4 9.7 %copy-start.17 = (bf16[1,256,224]{1,2,0:T(8,128)(2,1)S(1)}, bf16[1,256,224]{1,2,0:T(8,128)(2,1)}, u32[]{:S(2)}) copy-start(bf16[1,256,224]{1,2,0:T(8,128)(2,1)} %get-tuple-element.12) | copy-start | bytes 344068
  65.4 10.4 %copy-start.16 = (bf16[1,256,224]{1,2,0:T(8,128)(2,1)S(1)}, bf16[1,256,224]{1,2,0:T(8,128)(2,1)}, u32[]{:S(2)}) copy-start(bf16[1,256,224]{1,2,0:T(8,128)(2,1)} %get-tuple-element.11) | copy-start | bytes 344068
  65.4 11.2 %copy-start.15 = (bf16[1,256,224]{1,2,0:T(8,128)(2,1)S(1)}, bf16[1,256,224]{1,2,0:T(8,128)(2,1)}, u32[]{:S(2)}) copy-start(bf16[1,256,224]{1,2,0:T(8,128)(2,1)} %get-tuple-element.10) | copy-start | bytes 344068
  65.5 11.9 %copy-start.14 = (bf16[1,256,224]{1,2,0:T(8,128)(2,1)S(1)}, bf16[1,256,224]{1,2,0:T(8,128)(2,1)}, u32[]{:S(2)}) copy-start(bf16[1,256,224]{1,2,0:T(8,128)(2,1)} %get-tuple-element.9) | copy-start | bytes 344068
  65.5 12.6 %copy-start.13 = (bf16[1,256,224]{1,2,0:T(8,128)(2,1)S(1)}, bf16[1,256,224]{1,2,0:T(8,128)(2,1)}, u32[]{:S(2)}) copy-start(bf16[1,256,224]{1,2,0:T(8,128)(2,1)} %get-tuple-element.8) | copy-start | bytes 344068
  66.6 13.0 %copy-start.8 = (bf16[1,256,224]{2,1,0:T(8,128)(2,1)}, bf16[1,256,224]{2,1,0:T(8,128)(2,1)S(1)}, u32[]{:S(2)}) copy-start(bf16[1,256,224]{2,1,0:T(8,128)(2,1)S(1)} %copy.89) | copy-start | bytes 344068
  67.7 12.0 %copy-start.10 = (bf16[1,256,224]{2,1,0:T(8,128)(2,1)}, bf16[1,256,224]{2,1,0:T(8,128)(2,1)S(1)}, u32[]{:S(2)}) copy-start(bf16[1,256,224]{2,1,0:T(8,128)(2,1)S(1)} %copy.90) | copy-start | bytes 344068
  81.9 2.5 copy-start.2
  81.9 2.5 copy-start.5
  81.9 2.5 copy-start.7
  81.9 2.5 copy-start.9
  165.0 1.1 copy-start.12
  165.0 1.1 copy-start.19
  167.9 5.3 %copy-start.20 = (s32[256,6]{0,1:T(8,128)S(1)}, s32[256,6]{0,1:T(8,128)}, u32[]{:S(2)}) copy-start(s32[256,6]{0,1:T(8,128)} %param.22) | copy-start | bytes 18436
  167.9 24.1 %all-to-all-start.4 = ((bf16[16,256,160]{1,2,0:T(8,128)(2,1)}), bf16[16,256,160]{1,2,0:T(8,128)(2,1)}, u32[]{:S(2)}, u32[]{:S(2)}) async-start(bf16[16,256,160]{1,2,0:T(8,128)(2,1)} %broadcast_in_dim.46), calls=%async_computation.4 | async-start | bytes 2621440 | tf_op jit(solution)/shard_map/all_to_all | solution.py:126
  199.1 8.3 %copy-start.25 = (f32[2560]{0:T(1024)S(1)}, f32[2560]{0:T(1024)}, u32[]{:S(2)}) copy-start(f32[2560]{0:T(1024)} %param.21) | copy-start | bytes 30724
  206.3 1.1 copy-start.3
  208.3 72.7 %copy-start.22 = (bf16[1,2560,768]{2,1,0:T(8,128)(2,1)S(1)}, bf16[1,2560,768]{2,1,0:T(8,128)(2,1)}, u32[]{:S(2)}) copy-start(bf16[1,2560,768]{2,1,0:T(8,128)(2,1)} %param.26) | copy-start | bytes 11796484
  286.2 4.9 %copy-start.21 = (f32[256,6]{0,1:T(8,128)S(1)}, f32[256,6]{0,1:T(8,128)}, u32[]{:S(2)}) copy-start(f32[256,6]{0,1:T(8,128)} %param.23) | copy-start | bytes 18436
  286.2 66.1 %all-to-all-start.6 = ((bf16[16,32,2560]{2,1,0:T(8,128)(2,1)}), bf16[16,32,2560]{2,1,0:T(8,128)(2,1)}, u32[]{:S(2)}, u32[]{:S(2)}) async-start(bf16[16,32,2560]{2,1,0:T(8,128)(2,1)} %bitcast.272), calls=%async_computation.6 | async-start | bytes 5242880 | tf_op jit(solution)/shard_map/all_to_all | solution.py:246
  355.3 1.2 copy-start.11
  361.8 40.7 %all-to-all-start.7 = ((f32[16,256,160]{1,2,0:T(8,128)}), f32[16,256,160]{1,2,0:T(8,128)}, u32[]{:S(2)}, u32[]{:S(2)}) async-start(f32[16,256,160]{1,2,0:T(8,128)} %bitcast.269), calls=%async_computation.7 | async-start | bytes 5242880 | tf_op jit(solution)/shard_map/all_to_all | solution.py:134

commit v4 on v3

--- a/solution.py
+++ b/solution.py
@@ -124,7 +124,9 @@
     count = lax.axis_size("blk")
     stacked = jnp.broadcast_to(values[None], (count,) + values.shape)
     received = lax.all_to_all(stacked, "blk", split_axis=0, concat_axis=0, tiled=True)
-    return jnp.concatenate([received[i] for i in range(count)], axis=axis)
+    if axis == 0:
+        return received.reshape((count * values.shape[0],) + values.shape[1:])
+    return received.transpose(1, 0, 2).reshape(values.shape[0], count * values.shape[1])
 
 
 def scatter_sum_blocks(values):

time: 410 us -> 376 us (0.917)
  local copies, waits for them, and re-layouts: 49.9 us -> 18.4 us
    unnamed x117 -> x32, local copies, waits for them, and re-layouts: 31.6 us -> 2.54 us
    concatenate x4 -> x0, local copies, waits for them, and re-layouts: 4.91 us -> none  [gather_blocks(): return jnp.concatenate([received[i] for i in range(count)], axis=axis)]
  transfers between devices with their start and end apart: 4 -> 4, of which waited for: 4 -> 4; matrix products, arithmetic and copies ran while one was open for 3% -> 2% of each run, Pallas kernels for 0% -> 0%
where the time goes in v4:
time: 376 us; the launch traced here: 372 us
  blocking collectives  159 us (42%)
  waiting for transfers between devices  128 us (34%)
  starting transfers between devices  21.7 us (6%)
  local copies, waits for them, and re-layouts  18.4 us (5%)
  other arithmetic  17.4 us (5%)
  Pallas kernels  14.4 us (4%)
  matrix products  11 us (3%)
    all_to_all x1, blocking collectives, per_device(): lax.all_to_all(outgoing, 'exp', split_axis=0, concat_axis=0, tiled=True)  72.6 us
    all_to_all x1, waiting for transfers between devices, per_device(): lax.all_to_all(result.reshape(received.shape), 'exp', split_axis=0, conca...  58.7 us
    all_to_all x2, blocking collectives, gather_blocks(): lax.all_to_all(stacked, 'blk', split_axis=0, concat_axis=0, tiled=True)  46.7 us
    all_to_all x1, blocking collectives, per_device(): lax.all_to_all(payload, 'blk', split_axis=0, concat_axis=0, tiled=True)  39.7 us
    all_to_all x2, waiting for transfers between devices, gather_blocks(): lax.all_to_all(stacked, 'blk', split_axis=0, concat_axis=0, tiled=True)  38.3 us
    all_to_all x1, waiting for transfers between devices, scatter_sum_blocks(): lax.all_to_all(pieces, 'blk', split_axis=0, concat_axis=0, tiled=True)  31.4 us
    pallas_call x1, Pallas kernels, local_attention(): pl.pallas_call(attention_kernel, out_shape=jax.ShapeDtypeStruct((NEW, wid...  10.5 us
    all_to_all x2, starting transfers between devices, gather_blocks(): lax.all_to_all(stacked, 'blk', split_axis=0, concat_axis=0, tiled=True)  9.88 us
  transfers between devices with their start and end apart: 4, of which 4 were waited for; matrix products, arithmetic and copies ran while one was open for 2% of the time, Pallas kernels for 0%

profile of v4, /device:TPU:1, one launch (start us, length us, event | category | flops | bytes accessed | tf_op | source)
XLA Modules:
  0.0 372.1 jit_solution(11832051633144030336)
XLA Ops:
  0.6 1.1 broadcast_in_dim.40
  1.8 25.1 %all_to_all.40 = bf16[16,256,160]{1,2,0:T(8,128)(2,1)S(1)} all-to-all(bf16[16,256,160]{1,2,0:T(8,128)(2,1)S(1)} %broadcast_in_dim.40), channel_id=1, replica_groups=mesh['blk'=16,'exp'=16] {'blk'}, dimensions={0} | all-to-all | bytes 2621440 | tf_op jit(solution)/shard_map/all_to_all | solution.py:126
  28.7 1.4 broadcast_in_dim.41
  30.1 5.3 %all-to-all-start.1 = ((bf16[16,256,224]{1,2,0:T(8,128)(2,1)}), bf16[16,256,224]{1,2,0:T(8,128)(2,1)}, u32[]{:S(2)}, u32[]{:S(2)}) async-start(bf16[16,256,224]{1,2,0:T(8,128)(2,1)} %broadcast_in_dim.41), calls=%async_computation.1 | async-start | bytes 3670016 | tf_op jit(solution)/shard_map/all_to_all | solution.py:126
  39.1 21.3 %all-to-all-done.1 = bf16[16,256,224]{1,2,0:T(8,128)(2,1)} async-done(((bf16[16,256,224]{1,2,0:T(8,128)(2,1)}), bf16[16,256,224]{1,2,0:T(8,128)(2,1)}, u32[]{:S(2)}, u32[]{:S(2)}) %all-to-all-start.1) | async-done | bytes 1835040 | tf_op jit(solution)/shard_map/all_to_all | solution.py:126
  60.4 1.0 slice.42
  61.4 3.9 %copy.36.proj_ref = bf16[256,3584]{1,0:T(8,128)(2,1)} copy(bf16[256,3584]{0,1:T(8,128)(2,1)} %bitcast.3) | data formatting | bytes 3670016 | tf_op jit(solution)/shard_map/reshape | solution.py:129
  66.8 2.1 gather_fusion
  68.9 2.7 bitcast_select_fusion.slot_ref
  71.6 10.5 %shard_map.149 = f32[256,2688]{1,0:T(8,128)} custom-call(bf16[256,3584]{1,0:T(8,128)(2,1)} %copy.36.proj_ref, f32[256,128]{1,0:T(8,128)} %get-tuple-element.9.cos_ref, f32[256,128]{1,0:T(8,128)} %get-tuple-element.10.sin_ref, bf16[512,1024]{1,0:T(8,128)(2,1)} %bitcast_select_fusion.slot_ref, s32[256,1]{1,0:T(8,128)} %iota_add_fusion.qpos_ref, s32[1,512]{1,0:T(1,128)} %bitcast.108), custom_call_target="tpu_custom_call" | custom-call | flops 1342177280 | bytes 5636096 | tf_op jit(solution)/shard_map/pallas_call | solution.py:79
  82.2 39.7 %all_to_all.41.part_ref = f32[16,16,2688]{2,1,0:T(8,128)} all-to-all(f32[16,16,2688]{2,1,0:T(8,128)} %bitcast.87), channel_id=1, replica_groups=mesh['blk'=16,'exp'=16] {'blk'}, dimensions={0} | all-to-all | bytes 5505024 | tf_op jit(solution)/shard_map/all_to_all | solution.py:206
  121.8 3.9 %shard_map.150 = bf16[16,2560]{1,0:T(8,128)(2,1)} custom-call(f32[16,16,2688]{2,1,0:T(8,128)} %all_to_all.41.part_ref), custom_call_target="tpu_custom_call" | custom-call | flops 2064384 | bytes 2834432 | tf_op jit(solution)/shard_map/pallas_call | solution.py:111
  125.7 1.1 broadcast_in_dim.45
  126.8 21.6 %all_to_all.42 = bf16[16,16,2560]{2,1,0:T(8,128)(2,1)S(1)} all-to-all(bf16[16,16,2560]{2,1,0:T(8,128)(2,1)S(1)} %broadcast_in_dim.45), channel_id=1, replica_groups=mesh['blk'=16,'exp'=16] {'blk'}, dimensions={0} | all-to-all | bytes 2621440 | tf_op jit(solution)/shard_map/all_to_all | solution.py:126
  149.0 1.2 broadcast_in_dim.46
  150.2 4.6 %all-to-all-start.4 = ((bf16[16,256,160]{1,2,0:T(8,128)(2,1)}), bf16[16,256,160]{1,2,0:T(8,128)(2,1)S(1)}, u32[]{:S(2)}, u32[]{:S(2)}) async-start(bf16[16,256,160]{1,2,0:T(8,128)(2,1)} %broadcast_in_dim.46), calls=%async_computation.4 | async-start | bytes 2621440 | tf_op jit(solution)/shard_map/all_to_all | solution.py:126
  154.9 1.2 reduce-window.6
  156.5 17.0 %all-to-all-done.4 = bf16[16,256,160]{1,2,0:T(8,128)(2,1)S(1)} async-done(((bf16[16,256,160]{1,2,0:T(8,128)(2,1)}), bf16[16,256,160]{1,2,0:T(8,128)(2,1)S(1)}, u32[]{:S(2)}, u32[]{:S(2)}) %all-to-all-start.4) | async-done | bytes 1310752 | tf_op jit(solution)/shard_map/all_to_all | solution.py:126
  175.2 72.6 %all_to_all.43 = bf16[16,32,2560]{2,1,0:T(8,128)(2,1)S(1)} all-to-all(bf16[16,32,2560]{2,1,0:T(8,128)(2,1)S(1)} %bitcast.89), channel_id=1, replica_groups=mesh['blk'=16,'exp'=16] {'exp'}, dimensions={0} | all-to-all | bytes 5242880 | tf_op jit(solution)/shard_map/all_to_all | solution.py:241
  247.8 2.2 fusion.1
  250.0 3.1 convolution_convert_fusion
  253.1 4.9 %all-to-all-start.6 = ((bf16[16,32,2560]{2,1,0:T(8,128)(2,1)}), bf16[16,32,2560]{2,1,0:T(8,128)(2,1)}, u32[]{:S(2)}, u32[]{:S(2)}) async-start(bf16[16,32,2560]{2,1,0:T(8,128)(2,1)} %bitcast.93), calls=%async_computation.6 | async-start | bytes 5242880 | tf_op jit(solution)/shard_map/all_to_all | solution.py:248
  258.7 0.9 copy-done.3
  259.6 0.9 fusion.34
  260.5 58.7 %all-to-all-done.6 = bf16[16,32,2560]{2,1,0:T(8,128)(2,1)} async-done(((bf16[16,32,2560]{2,1,0:T(8,128)(2,1)}), bf16[16,32,2560]{2,1,0:T(8,128)(2,1)}, u32[]{:S(2)}, u32[]{:S(2)}) %all-to-all-start.6) | async-done | bytes 2621472 | tf_op jit(solution)/shard_map/all_to_all | solution.py:248
  319.2 2.3 convert_reduce_fusion
  323.4 2.1 convolution_add_fusion
  325.5 3.2 copy.40
  328.7 6.9 %all-to-all-start.7 = ((f32[16,256,160]{1,2,0:T(8,128)}), f32[16,256,160]{1,2,0:T(8,128)}, u32[]{:S(2)}, u32[]{:S(2)}) async-start(f32[16,256,160]{1,2,0:T(8,128)} %bitcast.88), calls=%async_computation.7 | async-start | bytes 5242880 | tf_op jit(solution)/shard_map/all_to_all | solution.py:136
  335.7 2.4 broadcast_select_fusion
  338.1 31.4 %all-to-all-done.7 = f32[16,256,160]{1,2,0:T(8,128)} async-done(((f32[16,256,160]{1,2,0:T(8,128)}), f32[16,256,160]{1,2,0:T(8,128)}, u32[]{:S(2)}, u32[]{:S(2)}) %all-to-all-start.7) | async-done | bytes 2621472 | tf_op jit(solution)/shard_map/all_to_all | solution.py:136
  369.5 1.9 reduce_sum.69
  (76 shorter events, 12.1 us)
Async XLA Ops:
  0.6 249.4 %copy-start = (bf16[1,384,2560]{2,1,0:T(8,128)(2,1)S(1)}, bf16[1,384,2560]{2,1,0:T(8,128)(2,1)}, u32[]{:S(2)}) copy-start(bf16[1,384,2560]{2,1,0:T(8,128)(2,1)} %param.27) | copy-start | bytes 5898244
  1.8 25.5 %copy-start.10 = (f32[2560]{0:T(1024)S(1)}, f32[2560]{0:T(1024)}, u32[]{:S(2)}) copy-start(f32[2560]{0:T(1024)} %param.15) | copy-start | bytes 30724
  26.9 1.3 copy-start.4
  30.1 5.9 %copy-start.13 = (s32[1,64]{1,0:T(1,128)S(1)}, s32[1,64]{1,0:T(1,128)}, u32[]{:S(2)}) copy-start(s32[1,64]{1,0:T(1,128)} %param.19) | copy-start | bytes 772
  30.1 30.3 %all-to-all-start.1 = ((bf16[16,256,224]{1,2,0:T(8,128)(2,1)}), bf16[16,256,224]{1,2,0:T(8,128)(2,1)}, u32[]{:S(2)}, u32[]{:S(2)}) async-start(bf16[16,256,224]{1,2,0:T(8,128)(2,1)} %broadcast_in_dim.41), calls=%async_computation.1 | async-start | bytes 3670016 | tf_op jit(solution)/shard_map/all_to_all | solution.py:126
  65.8 1.0 slice-start
  68.9 13.3 %copy-start.1 = (bf16[512,1024]{1,0:T(8,128)(2,1)}, bf16[512,1024]{1,0:T(8,128)(2,1)S(1)}, u32[]{:S(2)}) copy-start(bf16[512,1024]{1,0:T(8,128)(2,1)S(1)} %gather_fusion) | copy-start | bytes 3145732
  125.7 22.7 %copy-start.6 = (bf16[2560,160]{0,1:T(8,128)(2,1)S(1)}, bf16[2560,160]{0,1:T(8,128)(2,1)}, u32[]{:S(2)}) copy-start(bf16[2560,160]{0,1:T(8,128)(2,1)} %param.17) | copy-start | bytes 2457604
  125.7 22.7 %copy-start.7 = (bf16[256,160]{0,1:T(8,128)(2,1)S(1)}, bf16[256,160]{0,1:T(8,128)(2,1)}, u32[]{:S(2)}) copy-start(bf16[256,160]{0,1:T(8,128)(2,1)} %param.14) | copy-start | bytes 245764
  149.0 5.8 %copy-start.9 = (s32[256,6]{0,1:T(8,128)S(1)}, s32[256,6]{0,1:T(8,128)}, u32[]{:S(2)}) copy-start(s32[256,6]{0,1:T(8,128)} %param.22) | copy-start | bytes 18436
  150.2 23.8 %copy-start.8 = (f32[2560]{0:T(1024)S(1)}, f32[2560]{0:T(1024)}, u32[]{:S(2)}) copy-start(f32[2560]{0:T(1024)} %param.21) | copy-start | bytes 30724
  150.2 23.4 %all-to-all-start.4 = ((bf16[16,256,160]{1,2,0:T(8,128)(2,1)}), bf16[16,256,160]{1,2,0:T(8,128)(2,1)S(1)}, u32[]{:S(2)}, u32[]{:S(2)}) async-start(bf16[16,256,160]{1,2,0:T(8,128)(2,1)} %broadcast_in_dim.46), calls=%async_computation.4 | async-start | bytes 2621440 | tf_op jit(solution)/shard_map/all_to_all | solution.py:126
  175.2 72.7 %copy-start.12 = (bf16[1,2560,768]{2,1,0:T(8,128)(2,1)S(1)}, bf16[1,2560,768]{2,1,0:T(8,128)(2,1)}, u32[]{:S(2)}) copy-start(bf16[1,2560,768]{2,1,0:T(8,128)(2,1)} %param.26) | copy-start | bytes 11796484
  253.1 4.9 %copy-start.11 = (f32[256,6]{0,1:T(8,128)S(1)}, f32[256,6]{0,1:T(8,128)}, u32[]{:S(2)}) copy-start(f32[256,6]{0,1:T(8,128)} %param.23) | copy-start | bytes 18436
  253.1 66.1 %all-to-all-start.6 = ((bf16[16,32,2560]{2,1,0:T(8,128)(2,1)}), bf16[16,32,2560]{2,1,0:T(8,128)(2,1)}, u32[]{:S(2)}, u32[]{:S(2)}) async-start(bf16[16,32,2560]{2,1,0:T(8,128)(2,1)} %bitcast.93), calls=%async_computation.6 | async-start | bytes 5242880 | tf_op jit(solution)/shard_map/all_to_all | solution.py:248
  258.0 1.5 copy-start.3
  322.1 1.2 copy-start.5
  328.7 7.0 %copy-start.2 = (bf16[512,1024]{1,0:T(8,128)(2,1)S(1)}, bf16[512,1024]{1,0:T(8,128)(2,1)}, u32[]{:S(2)}) copy-start(bf16[512,1024]{1,0:T(8,128)(2,1)} %copy-done.1) | copy-start | bytes 3145732
  328.7 40.8 %all-to-all-start.7 = ((f32[16,256,160]{1,2,0:T(8,128)}), f32[16,256,160]{1,2,0:T(8,128)}, u32[]{:S(2)}, u32[]{:S(2)}) async-start(f32[16,256,160]{1,2,0:T(8,128)} %bitcast.88), calls=%async_computation.7 | async-start | bytes 5242880 | tf_op jit(solution)/shard_map/all_to_all | solution.py:136

commit v5 on v4

--- a/solution.py
+++ b/solution.py
@@ -42,6 +42,14 @@
         ],
         axis=-1,
     )
+
+
+def split_three(value):
+    high = value.astype(jnp.bfloat16).astype(jnp.float32)
+    rest = value - high
+    middle = rest.astype(jnp.bfloat16).astype(jnp.float32)
+    low = (rest - middle).astype(jnp.bfloat16).astype(jnp.float32)
+    return [high, middle, low]
 
 
 def attention_kernel(proj_ref, cos_ref, sin_ref, slot_ref, qpos_ref, kpos_ref, out_ref):
@@ -68,38 +76,42 @@
         total = jnp.sum(probs, axis=1, keepdims=True)
         out_ref[:, head * HEAD_DIM : (head + 1) * HEAD_DIM] = jnp.dot(
             probs.astype(jnp.bfloat16), values, preferred_element_type=jnp.float32
-        )
-        stats = jnp.where(lane == head, peak, stats)
-        stats = jnp.where(lane == HEADS + head, total, stats)
-    out_ref[:, HEADS * HEAD_DIM :] = stats
+        ).astype(out_ref.dtype)
+        for slot, value in enumerate(split_three(peak) + split_three(total)):
+            stats = jnp.where(lane == slot * HEADS + head, value, stats)
+    out_ref[:, HEADS * HEAD_DIM :] = stats.astype(out_ref.dtype)
 
 
 def local_attention(projected_all, cosine, sine_signed, slot_rows, positions, key_pos):
     width = HEADS * HEAD_DIM + 128
     return pl.pallas_call(
         attention_kernel,
-        out_shape=jax.ShapeDtypeStruct((NEW, width), jnp.float32),
+        out_shape=jax.ShapeDtypeStruct((NEW, width), jnp.bfloat16),
         in_specs=[pl.BlockSpec(memory_space=pltpu.VMEM)] * 6,
         out_specs=pl.BlockSpec(memory_space=pltpu.VMEM),
         cost_estimate=pl.CostEstimate(
             flops=4 * NEW * slot_rows.shape[0] * HEAD_DIM * HEADS,
             transcendentals=NEW * slot_rows.shape[0] * HEADS,
-            bytes_accessed=NEW * width * 4 + slot_rows.size * 2 + projected_all.size * 2,
+            bytes_accessed=NEW * width * 2 + slot_rows.size * 2 + projected_all.size * 2,
         ),
     )(projected_all, cosine, sine_signed, slot_rows, positions[:, None], key_pos[None, :])
 
 
 def combine_kernel(part_ref, out_ref):
-    stats = part_ref[:, :, HEADS * HEAD_DIM :]
-    overall = jnp.max(stats, axis=0, keepdims=True)
-    factors = jnp.exp(stats - overall)
-    lane = lax.broadcasted_iota(jnp.int32, stats.shape, 2)
+    coded = part_ref[:, :, HEADS * HEAD_DIM :].astype(jnp.float32)
+    lane = lax.broadcasted_iota(jnp.int32, coded.shape, 2)
+
+    def pick(slot):
+        return jnp.sum(jnp.where(lane == slot, coded, 0.0), axis=2, keepdims=True)
+
     for head in range(HEADS):
-        factor = jnp.sum(jnp.where(lane == head, factors, 0.0), axis=2, keepdims=True)
-        total = jnp.sum(jnp.where(lane == HEADS + head, stats, 0.0), axis=2, keepdims=True)
+        peak = (pick(head) + pick(HEADS + head)) + pick(2 * HEADS + head)
+        total = (pick(3 * HEADS + head) + pick(4 * HEADS + head)) + pick(5 * HEADS + head)
+        factor = jnp.exp(peak - jnp.max(peak, axis=0, keepdims=True))
         denominator = jnp.sum(factor * total, axis=0)
         numerator = jnp.sum(
-            part_ref[:, :, head * HEAD_DIM : (head + 1) * HEAD_DIM] * factor, axis=0
+            part_ref[:, :, head * HEAD_DIM : (head + 1) * HEAD_DIM].astype(jnp.float32) * factor,
+            axis=0,
         )
         out_ref[:, head * HEAD_DIM : (head + 1) * HEAD_DIM] = (
             numerator / denominator
@@ -115,7 +127,7 @@
         out_specs=pl.BlockSpec(memory_space=pltpu.VMEM),
         cost_estimate=pl.CostEstimate(
             flops=3 * parts.size, transcendentals=sources * rows * 128,
-            bytes_accessed=parts.size * 4 + rows * HEADS * HEAD_DIM * 2,
+            bytes_accessed=parts.size * 2 + rows * HEADS * HEAD_DIM * 2,
         ),
     )(parts)
 

time: 376 us -> 365 us (0.971)
  blocking collectives: 159 us -> 144 us
    all_to_all x1, blocking collectives: 39.7 us -> 24.3 us  [per_device(): lax.all_to_all(payload, 'blk', split_axis=0, concat_axis=0, tiled=True)]
where the time goes in v5:
time: 365 us; the launch traced here: 360 us
  blocking collectives  144 us (39%)
  waiting for transfers between devices  128 us (35%)
  starting transfers between devices  21.7 us (6%)
  local copies, waits for them, and re-layouts  18.4 us (5%)
  Pallas kernels  17.6 us (5%)
  other arithmetic  17.4 us (5%)
  matrix products  11 us (3%)
    all_to_all x1, blocking collectives, per_device(): lax.all_to_all(outgoing, 'exp', split_axis=0, concat_axis=0, tiled=True)  72.6 us
    all_to_all x1, waiting for transfers between devices, per_device(): lax.all_to_all(result.reshape(received.shape), 'exp', split_axis=0, conca...  58.7 us
    all_to_all x2, blocking collectives, gather_blocks(): lax.all_to_all(stacked, 'blk', split_axis=0, concat_axis=0, tiled=True)  47.2 us
    all_to_all x2, waiting for transfers between devices, gather_blocks(): lax.all_to_all(stacked, 'blk', split_axis=0, concat_axis=0, tiled=True)  38.4 us
    all_to_all x1, waiting for transfers between devices, scatter_sum_blocks(): lax.all_to_all(pieces, 'blk', split_axis=0, concat_axis=0, tiled=True)  31.4 us
    all_to_all x1, blocking collectives, per_device(): lax.all_to_all(payload, 'blk', split_axis=0, concat_axis=0, tiled=True)  24.3 us
    pallas_call x1, Pallas kernels, local_attention(): pl.pallas_call(attention_kernel, out_shape=jax.ShapeDtypeStruct((NEW, wid...  11.5 us
    all_to_all x2, starting transfers between devices, gather_blocks(): lax.all_to_all(stacked, 'blk', split_axis=0, concat_axis=0, tiled=True)  9.89 us
  transfers between devices with their start and end apart: 4, of which 4 were waited for; matrix products, arithmetic and copies ran while one was open for 2% of the time, Pallas kernels for 0%

profile of v5, /device:TPU:1, one launch (start us, length us, event | category | flops | bytes accessed | tf_op | source)
XLA Modules:
  0.0 360.4 jit_solution(4250187751300240307)
XLA Ops:
  0.6 1.1 broadcast_in_dim.40
  1.8 25.1 %all_to_all.40 = bf16[16,256,160]{1,2,0:T(8,128)(2,1)S(1)} all-to-all(bf16[16,256,160]{1,2,0:T(8,128)(2,1)S(1)} %broadcast_in_dim.40), channel_id=1, replica_groups=mesh['blk'=16,'exp'=16] {'blk'}, dimensions={0} | all-to-all | bytes 2621440 | tf_op jit(solution)/shard_map/all_to_all | solution.py:138
  28.7 1.4 broadcast_in_dim.41
  30.1 5.3 %all-to-all-start.1 = ((bf16[16,256,224]{1,2,0:T(8,128)(2,1)}), bf16[16,256,224]{1,2,0:T(8,128)(2,1)}, u32[]{:S(2)}, u32[]{:S(2)}) async-start(bf16[16,256,224]{1,2,0:T(8,128)(2,1)} %broadcast_in_dim.41), calls=%async_computation.1 | async-start | bytes 3670016 | tf_op jit(solution)/shard_map/all_to_all | solution.py:138
  39.0 21.4 %all-to-all-done.1 = bf16[16,256,224]{1,2,0:T(8,128)(2,1)} async-done(((bf16[16,256,224]{1,2,0:T(8,128)(2,1)}), bf16[16,256,224]{1,2,0:T(8,128)(2,1)}, u32[]{:S(2)}, u32[]{:S(2)}) %all-to-all-start.1) | async-done | bytes 1835040 | tf_op jit(solution)/shard_map/all_to_all | solution.py:138
  60.4 1.0 slice.42
  61.4 3.9 %copy.36.proj_ref = bf16[256,3584]{1,0:T(8,128)(2,1)} copy(bf16[256,3584]{0,1:T(8,128)(2,1)} %bitcast.3) | data formatting | bytes 3670016 | tf_op jit(solution)/shard_map/reshape | solution.py:141
  66.8 2.1 gather_fusion
  68.9 2.7 bitcast_select_fusion.slot_ref
  71.6 11.5 %shard_map.149 = bf16[256,2688]{1,0:T(8,128)(2,1)} custom-call(bf16[256,3584]{1,0:T(8,128)(2,1)} %copy.36.proj_ref, f32[256,128]{1,0:T(8,128)} %get-tuple-element.9.cos_ref, f32[256,128]{1,0:T(8,128)} %get-tuple-element.10.sin_ref, bf16[512,1024]{1,0:T(8,128)(2,1)} %bitcast_select_fusion.slot_ref, s32[256,1]{1,0:T(8,128)} %iota_add_fusion.qpos_ref, ...), custom_call_target="tpu_custom_call" | custom-call | flops 1342177280 | bytes 4259840 | tf_op jit(solution)/shard_map/pallas_call | solution.py:87
  83.1 24.3 %all_to_all.41.part_ref = bf16[16,16,2688]{2,1,0:T(8,128)(2,1)} all-to-all(bf16[16,16,2688]{2,1,0:T(8,128)(2,1)} %bitcast.96), channel_id=1, replica_groups=mesh['blk'=16,'exp'=16] {'blk'}, dimensions={0} | all-to-all | bytes 2752512 | tf_op jit(solution)/shard_map/all_to_all | solution.py:218
  107.4 6.1 %shard_map.150 = bf16[16,2560]{1,0:T(8,128)(2,1)} custom-call(bf16[16,16,2688]{2,1,0:T(8,128)(2,1)} %all_to_all.41.part_ref), custom_call_target="tpu_custom_call" | custom-call | flops 2064384 | bytes 1458176 | tf_op jit(solution)/shard_map/pallas_call | solution.py:123
  113.5 1.1 broadcast_in_dim.45
  114.6 22.1 %all_to_all.42 = bf16[16,16,2560]{2,1,0:T(8,128)(2,1)S(1)} all-to-all(bf16[16,16,2560]{2,1,0:T(8,128)(2,1)S(1)} %broadcast_in_dim.45), channel_id=1, replica_groups=mesh['blk'=16,'exp'=16] {'blk'}, dimensions={0} | all-to-all | bytes 2621440 | tf_op jit(solution)/shard_map/all_to_all | solution.py:138
  137.3 1.2 broadcast_in_dim.46
  138.5 4.6 %all-to-all-start.4 = ((bf16[16,256,160]{1,2,0:T(8,128)(2,1)}), bf16[16,256,160]{1,2,0:T(8,128)(2,1)S(1)}, u32[]{:S(2)}, u32[]{:S(2)}) async-start(bf16[16,256,160]{1,2,0:T(8,128)(2,1)} %broadcast_in_dim.46), calls=%async_computation.4 | async-start | bytes 2621440 | tf_op jit(solution)/shard_map/all_to_all | solution.py:138
  143.2 1.2 reduce-window.6
  144.9 17.0 %all-to-all-done.4 = bf16[16,256,160]{1,2,0:T(8,128)(2,1)S(1)} async-done(((bf16[16,256,160]{1,2,0:T(8,128)(2,1)}), bf16[16,256,160]{1,2,0:T(8,128)(2,1)S(1)}, u32[]{:S(2)}, u32[]{:S(2)}) %all-to-all-start.4) | async-done | bytes 1310752 | tf_op jit(solution)/shard_map/all_to_all | solution.py:138
  163.5 72.6 %all_to_all.43 = bf16[16,32,2560]{2,1,0:T(8,128)(2,1)S(1)} all-to-all(bf16[16,32,2560]{2,1,0:T(8,128)(2,1)S(1)} %bitcast.88), channel_id=1, replica_groups=mesh['blk'=16,'exp'=16] {'exp'}, dimensions={0} | all-to-all | bytes 5242880 | tf_op jit(solution)/shard_map/all_to_all | solution.py:253
  236.1 2.2 fusion.1
  238.3 3.1 convolution_convert_fusion
  241.4 4.9 %all-to-all-start.6 = ((bf16[16,32,2560]{2,1,0:T(8,128)(2,1)}), bf16[16,32,2560]{2,1,0:T(8,128)(2,1)}, u32[]{:S(2)}, u32[]{:S(2)}) async-start(bf16[16,32,2560]{2,1,0:T(8,128)(2,1)} %bitcast.92), calls=%async_computation.6 | async-start | bytes 5242880 | tf_op jit(solution)/shard_map/all_to_all | solution.py:260
  247.0 0.9 copy-done.3
  247.9 0.9 fusion.34
  248.8 58.7 %all-to-all-done.6 = bf16[16,32,2560]{2,1,0:T(8,128)(2,1)} async-done(((bf16[16,32,2560]{2,1,0:T(8,128)(2,1)}), bf16[16,32,2560]{2,1,0:T(8,128)(2,1)}, u32[]{:S(2)}, u32[]{:S(2)}) %all-to-all-start.6) | async-done | bytes 2621472 | tf_op jit(solution)/shard_map/all_to_all | solution.py:260
  307.6 2.3 convert_reduce_fusion
  311.7 2.1 convolution_add_fusion
  313.8 3.2 copy.40
  317.0 6.9 %all-to-all-start.7 = ((f32[16,256,160]{1,2,0:T(8,128)}), f32[16,256,160]{1,2,0:T(8,128)}, u32[]{:S(2)}, u32[]{:S(2)}) async-start(f32[16,256,160]{1,2,0:T(8,128)} %bitcast.87), calls=%async_computation.7 | async-start | bytes 5242880 | tf_op jit(solution)/shard_map/all_to_all | solution.py:148
  324.0 2.4 broadcast_select_fusion
  326.4 31.4 %all-to-all-done.7 = f32[16,256,160]{1,2,0:T(8,128)} async-done(((f32[16,256,160]{1,2,0:T(8,128)}), f32[16,256,160]{1,2,0:T(8,128)}, u32[]{:S(2)}, u32[]{:S(2)}) %all-to-all-start.7) | async-done | bytes 2621472 | tf_op jit(solution)/shard_map/all_to_all | solution.py:148
  357.8 1.9 reduce_sum.69
  (76 shorter events, 12.1 us)
Async XLA Ops:
  0.6 237.7 %copy-start = (bf16[1,384,2560]{2,1,0:T(8,128)(2,1)S(1)}, bf16[1,384,2560]{2,1,0:T(8,128)(2,1)}, u32[]{:S(2)}) copy-start(bf16[1,384,2560]{2,1,0:T(8,128)(2,1)} %param.27) | copy-start | bytes 5898244
  1.8 25.5 %copy-start.10 = (f32[2560]{0:T(1024)S(1)}, f32[2560]{0:T(1024)}, u32[]{:S(2)}) copy-start(f32[2560]{0:T(1024)} %param.15) | copy-start | bytes 30724
  26.9 1.3 copy-start.4
  30.1 5.9 %copy-start.13 = (s32[1,64]{1,0:T(1,128)S(1)}, s32[1,64]{1,0:T(1,128)}, u32[]{:S(2)}) copy-start(s32[1,64]{1,0:T(1,128)} %param.19) | copy-start | bytes 772
  30.1 30.3 %all-to-all-start.1 = ((bf16[16,256,224]{1,2,0:T(8,128)(2,1)}), bf16[16,256,224]{1,2,0:T(8,128)(2,1)}, u32[]{:S(2)}, u32[]{:S(2)}) async-start(bf16[16,256,224]{1,2,0:T(8,128)(2,1)} %broadcast_in_dim.41), calls=%async_computation.1 | async-start | bytes 3670016 | tf_op jit(solution)/shard_map/all_to_all | solution.py:138
  65.8 1.0 slice-start
  68.9 14.2 %copy-start.1 = (bf16[512,1024]{1,0:T(8,128)(2,1)}, bf16[512,1024]{1,0:T(8,128)(2,1)S(1)}, u32[]{:S(2)}) copy-start(bf16[512,1024]{1,0:T(8,128)(2,1)S(1)} %gather_fusion) | copy-start | bytes 3145732
  113.5 23.2 %copy-start.6 = (bf16[2560,160]{0,1:T(8,128)(2,1)S(1)}, bf16[2560,160]{0,1:T(8,128)(2,1)}, u32[]{:S(2)}) copy-start(bf16[2560,160]{0,1:T(8,128)(2,1)} %param.17) | copy-start | bytes 2457604
  113.5 23.2 %copy-start.7 = (bf16[256,160]{0,1:T(8,128)(2,1)S(1)}, bf16[256,160]{0,1:T(8,128)(2,1)}, u32[]{:S(2)}) copy-start(bf16[256,160]{0,1:T(8,128)(2,1)} %param.14) | copy-start | bytes 245764
  137.3 5.8 %copy-start.9 = (s32[256,6]{0,1:T(8,128)S(1)}, s32[256,6]{0,1:T(8,128)}, u32[]{:S(2)}) copy-start(s32[256,6]{0,1:T(8,128)} %param.22) | copy-start | bytes 18436
  138.5 23.8 %copy-start.8 = (f32[2560]{0:T(1024)S(1)}, f32[2560]{0:T(1024)}, u32[]{:S(2)}) copy-start(f32[2560]{0:T(1024)} %param.21) | copy-start | bytes 30724
  138.5 23.4 %all-to-all-start.4 = ((bf16[16,256,160]{1,2,0:T(8,128)(2,1)}), bf16[16,256,160]{1,2,0:T(8,128)(2,1)S(1)}, u32[]{:S(2)}, u32[]{:S(2)}) async-start(bf16[16,256,160]{1,2,0:T(8,128)(2,1)} %broadcast_in_dim.46), calls=%async_computation.4 | async-start | bytes 2621440 | tf_op jit(solution)/shard_map/all_to_all | solution.py:138
  163.5 72.7 %copy-start.12 = (bf16[1,2560,768]{2,1,0:T(8,128)(2,1)S(1)}, bf16[1,2560,768]{2,1,0:T(8,128)(2,1)}, u32[]{:S(2)}) copy-start(bf16[1,2560,768]{2,1,0:T(8,128)(2,1)} %param.26) | copy-start | bytes 11796484
  241.4 5.0 %copy-start.11 = (f32[256,6]{0,1:T(8,128)S(1)}, f32[256,6]{0,1:T(8,128)}, u32[]{:S(2)}) copy-start(f32[256,6]{0,1:T(8,128)} %param.23) | copy-start | bytes 18436
  241.4 66.1 %all-to-all-start.6 = ((bf16[16,32,2560]{2,1,0:T(8,128)(2,1)}), bf16[16,32,2560]{2,1,0:T(8,128)(2,1)}, u32[]{:S(2)}, u32[]{:S(2)}) async-start(bf16[16,32,2560]{2,1,0:T(8,128)(2,1)} %bitcast.92), calls=%async_computation.6 | async-start | bytes 5242880 | tf_op jit(solution)/shard_map/all_to_all | solution.py:260
  246.4 1.5 copy-start.3
  310.5 1.2 copy-start.5
  317.0 7.0 %copy-start.2 = (bf16[512,1024]{1,0:T(8,128)(2,1)S(1)}, bf16[512,1024]{1,0:T(8,128)(2,1)}, u32[]{:S(2)}) copy-start(bf16[512,1024]{1,0:T(8,128)(2,1)} %copy-done.1) | copy-start | bytes 3145732
  317.0 40.8 %all-to-all-start.7 = ((f32[16,256,160]{1,2,0:T(8,128)}), f32[16,256,160]{1,2,0:T(8,128)}, u32[]{:S(2)}, u32[]{:S(2)}) async-start(f32[16,256,160]{1,2,0:T(8,128)} %bitcast.87), calls=%async_computation.7 | async-start | bytes 5242880 | tf_op jit(solution)/shard_map/all_to_all | solution.py:148

commit v6 on v5

--- a/solution.py
+++ b/solution.py
@@ -145,8 +145,10 @@
     count = lax.axis_size("blk")
     rows, width = values.shape
     pieces = values.reshape(rows, count, width // count).transpose(1, 0, 2)
-    received = lax.all_to_all(pieces, "blk", split_axis=0, concat_axis=0, tiled=True)
-    return jnp.sum(received, axis=0)
+    received = lax.all_to_all(
+        pieces.astype(jnp.bfloat16), "blk", split_axis=0, concat_axis=0, tiled=True
+    )
+    return jnp.sum(received.astype(jnp.float32), axis=0)
 
 
 def per_device(

time: 365 us -> 343 us (0.940); the launches traced: 360 us -> 342 us
  waiting for transfers between devices: 128 us -> 113 us
    all_to_all x1, waiting for transfers between devices: 31.4 us -> 16.4 us  [scatter_sum_blocks(): lax.all_to_all(pieces.astype(jnp.bfloat16), 'blk', split_axis=0, concat_a...]
  transfers between devices with their start and end apart: 4 -> 4, of which waited for: 4 -> 4; matrix products, arithmetic and copies ran while one was open for 2% -> 3% of each run, Pallas kernels for 0% -> 0%
where the time goes in v6:
time: 343 us; the launch traced here: 342 us
  blocking collectives  144 us (42%)
  waiting for transfers between devices  113 us (33%)
  starting transfers between devices  21.7 us (6%)
  Pallas kernels  17.6 us (5%)
  local copies, waits for them, and re-layouts  17.1 us (5%)
  other arithmetic  17 us (5%)
  matrix products  10.2 us (3%)
    all_to_all x1, blocking collectives, per_device(): lax.all_to_all(outgoing, 'exp', split_axis=0, concat_axis=0, tiled=True)  72.6 us
    all_to_all x1, waiting for transfers between devices, per_device(): lax.all_to_all(result.reshape(received.shape), 'exp', split_axis=0, conca...  58 us
    all_to_all x2, blocking collectives, gather_blocks(): lax.all_to_all(stacked, 'blk', split_axis=0, concat_axis=0, tiled=True)  47.3 us
    all_to_all x2, waiting for transfers between devices, gather_blocks(): lax.all_to_all(stacked, 'blk', split_axis=0, concat_axis=0, tiled=True)  38.4 us
    all_to_all x1, blocking collectives, per_device(): lax.all_to_all(payload, 'blk', split_axis=0, concat_axis=0, tiled=True)  24.3 us
    all_to_all x1, waiting for transfers between devices, scatter_sum_blocks(): lax.all_to_all(pieces.astype(jnp.bfloat16), 'blk', split_axis=0, concat_a...  16.4 us
    pallas_call x1, Pallas kernels, local_attention(): pl.pallas_call(attention_kernel, out_shape=jax.ShapeDtypeStruct((NEW, wid...  11.5 us
    all_to_all x2, starting transfers between devices, gather_blocks(): lax.all_to_all(stacked, 'blk', split_axis=0, concat_axis=0, tiled=True)  9.87 us
  transfers between devices with their start and end apart: 4, of which 4 were waited for; matrix products, arithmetic and copies ran while one was open for 3% of the time, Pallas kernels for 0%

profile of v6, /device:TPU:1, one launch (start us, length us, event | category | flops | bytes accessed | tf_op | source)
XLA Modules:
  0.0 342.2 jit_solution(12201829829922830524)
XLA Ops:
  0.6 1.1 broadcast_in_dim.40
  1.8 25.1 %all_to_all.40 = bf16[16,256,160]{1,2,0:T(8,128)(2,1)S(1)} all-to-all(bf16[16,256,160]{1,2,0:T(8,128)(2,1)S(1)} %broadcast_in_dim.40), channel_id=1, replica_groups=mesh['blk'=16,'exp'=16] {'blk'}, dimensions={0} | all-to-all | bytes 2621440 | tf_op jit(solution)/shard_map/all_to_all | solution.py:138
  29.0 1.4 broadcast_in_dim.41
  30.4 5.3 %all-to-all-start.1 = ((bf16[16,256,224]{1,2,0:T(8,128)(2,1)}), bf16[16,256,224]{1,2,0:T(8,128)(2,1)}, u32[]{:S(2)}, u32[]{:S(2)}) async-start(bf16[16,256,224]{1,2,0:T(8,128)(2,1)} %broadcast_in_dim.41), calls=%async_computation.1 | async-start | bytes 3670016 | tf_op jit(solution)/shard_map/all_to_all | solution.py:138
  37.9 0.8 pad_maximum_fusion.2
  39.4 21.4 %all-to-all-done.1 = bf16[16,256,224]{1,2,0:T(8,128)(2,1)} async-done(((bf16[16,256,224]{1,2,0:T(8,128)(2,1)}), bf16[16,256,224]{1,2,0:T(8,128)(2,1)}, u32[]{:S(2)}, u32[]{:S(2)}) %all-to-all-start.1) | async-done | bytes 1835040 | tf_op jit(solution)/shard_map/all_to_all | solution.py:138
  60.8 1.0 slice.42
  61.7 3.9 %copy.36.proj_ref = bf16[256,3584]{1,0:T(8,128)(2,1)} copy(bf16[256,3584]{0,1:T(8,128)(2,1)} %bitcast.3) | data formatting | bytes 3670016 | tf_op jit(solution)/shard_map/reshape | solution.py:141
  67.2 2.1 gather_fusion
  69.3 2.7 bitcast_select_fusion.slot_ref
  72.0 11.5 %shard_map.149 = bf16[256,2688]{1,0:T(8,128)(2,1)} custom-call(bf16[256,3584]{1,0:T(8,128)(2,1)} %copy.36.proj_ref, f32[256,128]{1,0:T(8,128)} %get-tuple-element.9.cos_ref, f32[256,128]{1,0:T(8,128)} %get-tuple-element.10.sin_ref, bf16[512,1024]{1,0:T(8,128)(2,1)} %bitcast_select_fusion.slot_ref, s32[256,1]{1,0:T(8,128)} %iota_add_fusion.qpos_ref, ...), custom_call_target="tpu_custom_call" | custom-call | flops 1342177280 | bytes 4259840 | tf_op jit(solution)/shard_map/pallas_call | solution.py:87
  83.5 24.3 %all_to_all.41.part_ref = bf16[16,16,2688]{2,1,0:T(8,128)(2,1)} all-to-all(bf16[16,16,2688]{2,1,0:T(8,128)(2,1)} %bitcast.96), channel_id=1, replica_groups=mesh['blk'=16,'exp'=16] {'blk'}, dimensions={0} | all-to-all | bytes 2752512 | tf_op jit(solution)/shard_map/all_to_all | solution.py:220
  107.8 6.1 %shard_map.150 = bf16[16,2560]{1,0:T(8,128)(2,1)} custom-call(bf16[16,16,2688]{2,1,0:T(8,128)(2,1)} %all_to_all.41.part_ref), custom_call_target="tpu_custom_call" | custom-call | flops 2064384 | bytes 1458176 | tf_op jit(solution)/shard_map/pallas_call | solution.py:123
  113.9 1.0 broadcast_in_dim.45
  115.0 22.2 %all_to_all.42 = bf16[16,16,2560]{2,1,0:T(8,128)(2,1)S(1)} all-to-all(bf16[16,16,2560]{2,1,0:T(8,128)(2,1)S(1)} %broadcast_in_dim.45), channel_id=1, replica_groups=mesh['blk'=16,'exp'=16] {'blk'}, dimensions={0} | all-to-all | bytes 2621440 | tf_op jit(solution)/shard_map/all_to_all | solution.py:138
  137.7 1.2 broadcast_in_dim.46
  138.9 4.6 %all-to-all-start.4 = ((bf16[16,256,160]{1,2,0:T(8,128)(2,1)}), bf16[16,256,160]{1,2,0:T(8,128)(2,1)S(1)}, u32[]{:S(2)}, u32[]{:S(2)}) async-start(bf16[16,256,160]{1,2,0:T(8,128)(2,1)} %broadcast_in_dim.46), calls=%async_computation.4 | async-start | bytes 2621440 | tf_op jit(solution)/shard_map/all_to_all | solution.py:138
  143.7 1.2 reduce-window.6
  145.3 17.0 %all-to-all-done.4 = bf16[16,256,160]{1,2,0:T(8,128)(2,1)S(1)} async-done(((bf16[16,256,160]{1,2,0:T(8,128)(2,1)}), bf16[16,256,160]{1,2,0:T(8,128)(2,1)S(1)}, u32[]{:S(2)}, u32[]{:S(2)}) %all-to-all-start.4) | async-done | bytes 1310752 | tf_op jit(solution)/shard_map/all_to_all | solution.py:138
  164.0 72.6 %all_to_all.43 = bf16[16,32,2560]{2,1,0:T(8,128)(2,1)S(1)} all-to-all(bf16[16,32,2560]{2,1,0:T(8,128)(2,1)S(1)} %bitcast.87), channel_id=1, replica_groups=mesh['blk'=16,'exp'=16] {'exp'}, dimensions={0} | all-to-all | bytes 5242880 | tf_op jit(solution)/shard_map/all_to_all | solution.py:255
  236.6 2.2 fusion.1
  238.8 3.1 convolution_convert_fusion
  241.9 4.9 %all-to-all-start.6 = ((bf16[16,32,2560]{2,1,0:T(8,128)(2,1)}), bf16[16,32,2560]{2,1,0:T(8,128)(2,1)}, u32[]{:S(2)}, u32[]{:S(2)}) async-start(bf16[16,32,2560]{2,1,0:T(8,128)(2,1)} %bitcast.92), calls=%async_computation.6 | async-start | bytes 5242880 | tf_op jit(solution)/shard_map/all_to_all | solution.py:262
  247.5 0.9 copy-done.3
  248.4 1.6 fusion.35
  250.0 58.0 %all-to-all-done.6 = bf16[16,32,2560]{2,1,0:T(8,128)(2,1)} async-done(((bf16[16,32,2560]{2,1,0:T(8,128)(2,1)}), bf16[16,32,2560]{2,1,0:T(8,128)(2,1)}, u32[]{:S(2)}, u32[]{:S(2)}) %all-to-all-start.6) | async-done | bytes 2621472 | tf_op jit(solution)/shard_map/all_to_all | solution.py:262
  308.0 2.3 convert_reduce_fusion
  312.8 1.4 copy.40
  314.3 6.9 %all-to-all-start.7 = ((bf16[16,256,160]{1,2,0:T(8,128)(2,1)}), bf16[16,256,160]{1,2,0:T(8,128)(2,1)}, u32[]{:S(2)}, u32[]{:S(2)}) async-start(bf16[16,256,160]{1,2,0:T(8,128)(2,1)} %bitcast.90), calls=%async_computation.7 | async-start | bytes 2621440 | tf_op jit(solution)/shard_map/all_to_all | solution.py:148
  321.3 2.4 broadcast_select_fusion
  323.7 16.4 %all-to-all-done.7 = bf16[16,256,160]{1,2,0:T(8,128)(2,1)} async-done(((bf16[16,256,160]{1,2,0:T(8,128)(2,1)}), bf16[16,256,160]{1,2,0:T(8,128)(2,1)}, u32[]{:S(2)}, u32[]{:S(2)}) %all-to-all-start.7) | async-done | bytes 1310752 | tf_op jit(solution)/shard_map/all_to_all | solution.py:148
  340.0 1.5 convert_reduce_fusion.1
  (78 shorter events, 12.3 us)
Async XLA Ops:
  0.6 238.2 %copy-start = (bf16[1,384,2560]{2,1,0:T(8,128)(2,1)S(1)}, bf16[1,384,2560]{2,1,0:T(8,128)(2,1)}, u32[]{:S(2)}) copy-start(bf16[1,384,2560]{2,1,0:T(8,128)(2,1)} %param.27) | copy-start | bytes 5898244
  1.8 25.5 %copy-start.11 = (f32[2560]{0:T(1024)S(1)}, f32[2560]{0:T(1024)}, u32[]{:S(2)}) copy-start(f32[2560]{0:T(1024)} %param.15) | copy-start | bytes 30724
  27.3 1.3 copy-start.4
  30.4 5.9 %copy-start.14 = (s32[1,64]{1,0:T(1,128)S(1)}, s32[1,64]{1,0:T(1,128)}, u32[]{:S(2)}) copy-start(s32[1,64]{1,0:T(1,128)} %param.19) | copy-start | bytes 772
  30.4 30.3 %all-to-all-start.1 = ((bf16[16,256,224]{1,2,0:T(8,128)(2,1)}), bf16[16,256,224]{1,2,0:T(8,128)(2,1)}, u32[]{:S(2)}, u32[]{:S(2)}) async-start(bf16[16,256,224]{1,2,0:T(8,128)(2,1)} %broadcast_in_dim.41), calls=%async_computation.1 | async-start | bytes 3670016 | tf_op jit(solution)/shard_map/all_to_all | solution.py:138
  66.2 1.0 slice-start
  69.3 2.8 copy-start.1
  114.9 22.2 %copy-start.7 = (bf16[2560,160]{0,1:T(8,128)(2,1)S(1)}, bf16[2560,160]{0,1:T(8,128)(2,1)}, u32[]{:S(2)}) copy-start(bf16[2560,160]{0,1:T(8,128)(2,1)} %param.17) | copy-start | bytes 2457604
  115.0 22.2 %copy-start.8 = (bf16[256,160]{0,1:T(8,128)(2,1)S(1)}, bf16[256,160]{0,1:T(8,128)(2,1)}, u32[]{:S(2)}) copy-start(bf16[256,160]{0,1:T(8,128)(2,1)} %param.14) | copy-start | bytes 245764
  138.9 4.6 %copy-start.10 = (s32[256,6]{0,1:T(8,128)S(1)}, s32[256,6]{0,1:T(8,128)}, u32[]{:S(2)}) copy-start(s32[256,6]{0,1:T(8,128)} %param.22) | copy-start | bytes 18436
  138.9 23.8 %copy-start.9 = (f32[2560]{0:T(1024)S(1)}, f32[2560]{0:T(1024)}, u32[]{:S(2)}) copy-start(f32[2560]{0:T(1024)} %param.21) | copy-start | bytes 30724
  138.9 23.4 %all-to-all-start.4 = ((bf16[16,256,160]{1,2,0:T(8,128)(2,1)}), bf16[16,256,160]{1,2,0:T(8,128)(2,1)S(1)}, u32[]{:S(2)}, u32[]{:S(2)}) async-start(bf16[16,256,160]{1,2,0:T(8,128)(2,1)} %broadcast_in_dim.46), calls=%async_computation.4 | async-start | bytes 2621440 | tf_op jit(solution)/shard_map/all_to_all | solution.py:138
  163.9 72.7 %copy-start.13 = (bf16[1,2560,768]{2,1,0:T(8,128)(2,1)S(1)}, bf16[1,2560,768]{2,1,0:T(8,128)(2,1)}, u32[]{:S(2)}) copy-start(bf16[1,2560,768]{2,1,0:T(8,128)(2,1)} %param.26) | copy-start | bytes 11796484
  241.9 5.0 %copy-start.12 = (f32[256,6]{0,1:T(8,128)S(1)}, f32[256,6]{0,1:T(8,128)}, u32[]{:S(2)}) copy-start(f32[256,6]{0,1:T(8,128)} %param.23) | copy-start | bytes 18436
  241.9 66.1 %all-to-all-start.6 = ((bf16[16,32,2560]{2,1,0:T(8,128)(2,1)}), bf16[16,32,2560]{2,1,0:T(8,128)(2,1)}, u32[]{:S(2)}, u32[]{:S(2)}) async-start(bf16[16,32,2560]{2,1,0:T(8,128)(2,1)} %bitcast.92), calls=%async_computation.6 | async-start | bytes 5242880 | tf_op jit(solution)/shard_map/all_to_all | solution.py:262
  246.8 1.5 copy-start.3
  310.9 1.0 copy-start.5
  310.9 1.3 copy-start.6
  314.3 7.0 %copy-start.2 = (bf16[512,1024]{1,0:T(8,128)(2,1)S(1)}, bf16[512,1024]{1,0:T(8,128)(2,1)}, u32[]{:S(2)}) copy-start(bf16[512,1024]{1,0:T(8,128)(2,1)} %copy-done.1) | copy-start | bytes 3145732
  314.3 25.7 %all-to-all-start.7 = ((bf16[16,256,160]{1,2,0:T(8,128)(2,1)}), bf16[16,256,160]{1,2,0:T(8,128)(2,1)}, u32[]{:S(2)}, u32[]{:S(2)}) async-start(bf16[16,256,160]{1,2,0:T(8,128)(2,1)} %bitcast.90), calls=%async_computation.7 | async-start | bytes 2621440 | tf_op jit(solution)/shard_map/all_to_all | solution.py:148

commit v7 on v6

--- a/solution.py
+++ b/solution.py
@@ -253,6 +253,7 @@
     ).astype(jnp.bfloat16)
     outgoing = jnp.repeat(outgoing, SPLIT, axis=0)
     received = lax.all_to_all(outgoing, "exp", split_axis=0, concat_axis=0, tiled=True)
+    received, shared_term = lax.optimization_barrier((received, shared_term))
     flat_rows = received.reshape(-1, model_width)
     expert_gu = jnp.dot(flat_rows, expert_gate_up[0], preferred_element_type=jnp.float32)
     activated = (jax.nn.silu(expert_gu[:, :FF_PART]) * expert_gu[:, FF_PART:]).astype(jnp.bfloat16)

time: 343 us -> 348 us (1.015)
  blocking collectives: 144 us -> 71.6 us
  waiting for transfers between devices: 113 us -> 173 us
  starting transfers between devices: 21.7 us -> 32.7 us
  matrix products: 10.2 us -> 13.9 us
    all_to_all x1 -> x0, blocking collectives: 72.6 us -> none  [per_device(): lax.all_to_all(outgoing, 'exp', split_axis=0, concat_axis=0, tiled=True)]
    all_to_all x0 -> x1, waiting for transfers between devices: none -> 56.8 us  [per_device(): lax.all_to_all(outgoing, 'exp', split_axis=0, concat_axis=0, tiled=True)]
    all_to_all x0 -> x1, starting transfers between devices: none -> 10.5 us  [per_device(): lax.all_to_all(outgoing, 'exp', split_axis=0, concat_axis=0, tiled=True)]
  transfers between devices with their start and end apart: 4 -> 5, of which waited for: 4 -> 5; matrix products, arithmetic and copies ran while one was open for 3% -> 3% of each run, Pallas kernels for 0% -> 0%
where the time goes in v7:
time: 348 us; the launch traced here: 347 us
  waiting for transfers between devices  173 us (50%)
  blocking collectives  71.6 us (21%)
  starting transfers between devices  32.7 us (9%)
  local copies, waits for them, and re-layouts  19.5 us (6%)
  Pallas kernels  17.6 us (5%)
  other arithmetic  17 us (5%)
  matrix products  13.9 us (4%)
    all_to_all x1, waiting for transfers between devices, per_device(): lax.all_to_all(result.reshape(received.shape), 'exp', split_axis=0, conca...  61.1 us
    all_to_all x1, waiting for transfers between devices, per_device(): lax.all_to_all(outgoing, 'exp', split_axis=0, concat_axis=0, tiled=True)  56.8 us
    all_to_all x2, blocking collectives, gather_blocks(): lax.all_to_all(stacked, 'blk', split_axis=0, concat_axis=0, tiled=True)  47.3 us
    all_to_all x2, waiting for transfers between devices, gather_blocks(): lax.all_to_all(stacked, 'blk', split_axis=0, concat_axis=0, tiled=True)  38.4 us
    all_to_all x1, blocking collectives, per_device(): lax.all_to_all(payload, 'blk', split_axis=0, concat_axis=0, tiled=True)  24.3 us
    all_to_all x1, waiting for transfers between devices, scatter_sum_blocks(): lax.all_to_all(pieces.astype(jnp.bfloat16), 'blk', split_axis=0, concat_a...  16.4 us
    pallas_call x1, Pallas kernels, local_attention(): pl.pallas_call(attention_kernel, out_shape=jax.ShapeDtypeStruct((NEW, wid...  11.5 us
    all_to_all x1, starting transfers between devices, per_device(): lax.all_to_all(outgoing, 'exp', split_axis=0, concat_axis=0, tiled=True)  10.5 us
  transfers between devices with their start and end apart: 5, of which 5 were waited for; matrix products, arithmetic and copies ran while one was open for 3% of the time, Pallas kernels for 0%

profile of v7, /device:TPU:1, one launch (start us, length us, event | category | flops | bytes accessed | tf_op | source)
XLA Modules:
  0.0 346.5 jit_solution(7972761863637267654)
XLA Ops:
  0.6 1.1 broadcast_in_dim.40
  1.8 25.1 %all_to_all.40 = bf16[16,256,160]{1,2,0:T(8,128)(2,1)S(1)} all-to-all(bf16[16,256,160]{1,2,0:T(8,128)(2,1)S(1)} %broadcast_in_dim.40), channel_id=1, replica_groups=mesh['blk'=16,'exp'=16] {'blk'}, dimensions={0} | all-to-all | bytes 2621440 | tf_op jit(solution)/shard_map/all_to_all | solution.py:138
  29.0 1.4 broadcast_in_dim.41
  30.4 5.3 %all-to-all-start.1 = ((bf16[16,256,224]{1,2,0:T(8,128)(2,1)}), bf16[16,256,224]{1,2,0:T(8,128)(2,1)}, u32[]{:S(2)}, u32[]{:S(2)}) async-start(bf16[16,256,224]{1,2,0:T(8,128)(2,1)} %broadcast_in_dim.41), calls=%async_computation.1 | async-start | bytes 3670016 | tf_op jit(solution)/shard_map/all_to_all | solution.py:138
  39.4 21.4 %all-to-all-done.1 = bf16[16,256,224]{1,2,0:T(8,128)(2,1)} async-done(((bf16[16,256,224]{1,2,0:T(8,128)(2,1)}), bf16[16,256,224]{1,2,0:T(8,128)(2,1)}, u32[]{:S(2)}, u32[]{:S(2)}) %all-to-all-start.1) | async-done | bytes 1835040 | tf_op jit(solution)/shard_map/all_to_all | solution.py:138
  60.8 3.8 %copy.36.proj_ref = bf16[256,3584]{1,0:T(8,128)(2,1)} copy(bf16[256,3584]{0,1:T(8,128)(2,1)} %bitcast.3) | data formatting | bytes 3670016 | tf_op jit(solution)/shard_map/reshape | solution.py:141
  67.1 2.1 gather_fusion
  69.2 2.7 bitcast_select_fusion.slot_ref
  71.9 11.5 %shard_map.149 = bf16[256,2688]{1,0:T(8,128)(2,1)} custom-call(bf16[256,3584]{1,0:T(8,128)(2,1)} %copy.36.proj_ref, f32[256,128]{1,0:T(8,128)} %get-tuple-element.13.cos_ref, f32[256,128]{1,0:T(8,128)} %get-tuple-element.14.sin_ref, bf16[512,1024]{1,0:T(8,128)(2,1)} %bitcast_select_fusion.slot_ref, s32[256,1]{1,0:T(8,128)} %iota_add_fusion.qpos_ref, ...), custom_call_target="tpu_custom_call" | custom-call | flops 1342177280 | bytes 4259840 | tf_op jit(solution)/shard_map/pallas_call | solution.py:87
  83.4 24.3 %all_to_all.41.part_ref = bf16[16,16,2688]{2,1,0:T(8,128)(2,1)} all-to-all(bf16[16,16,2688]{2,1,0:T(8,128)(2,1)} %bitcast.99), channel_id=1, replica_groups=mesh['blk'=16,'exp'=16] {'blk'}, dimensions={0} | all-to-all | bytes 2752512 | tf_op jit(solution)/shard_map/all_to_all | solution.py:220
  107.7 6.1 %shard_map.150 = bf16[16,2560]{1,0:T(8,128)(2,1)} custom-call(bf16[16,16,2688]{2,1,0:T(8,128)(2,1)} %all_to_all.41.part_ref), custom_call_target="tpu_custom_call" | custom-call | flops 2064384 | bytes 1458176 | tf_op jit(solution)/shard_map/pallas_call | solution.py:123
  114.9 22.2 %all_to_all.42 = bf16[16,16,2560]{2,1,0:T(8,128)(2,1)S(1)} all-to-all(bf16[16,16,2560]{2,1,0:T(8,128)(2,1)S(1)} %broadcast_in_dim.45), channel_id=1, replica_groups=mesh['blk'=16,'exp'=16] {'blk'}, dimensions={0} | all-to-all | bytes 2621440 | tf_op jit(solution)/shard_map/all_to_all | solution.py:138
  137.7 1.2 broadcast_in_dim.46
  138.9 4.6 %all-to-all-start.4 = ((bf16[16,256,160]{1,2,0:T(8,128)(2,1)}), bf16[16,256,160]{1,2,0:T(8,128)(2,1)S(1)}, u32[]{:S(2)}, u32[]{:S(2)}) async-start(bf16[16,256,160]{1,2,0:T(8,128)(2,1)} %broadcast_in_dim.46), calls=%async_computation.4 | async-start | bytes 2621440 | tf_op jit(solution)/shard_map/all_to_all | solution.py:138
  143.6 1.2 reduce-window.6
  145.2 17.0 %all-to-all-done.4 = bf16[16,256,160]{1,2,0:T(8,128)(2,1)S(1)} async-done(((bf16[16,256,160]{1,2,0:T(8,128)(2,1)}), bf16[16,256,160]{1,2,0:T(8,128)(2,1)S(1)}, u32[]{:S(2)}, u32[]{:S(2)}) %all-to-all-start.4) | async-done | bytes 1310752 | tf_op jit(solution)/shard_map/all_to_all | solution.py:138
  163.6 1.8 broadcast_in_dim.47
  165.4 10.5 %all-to-all-start.5 = ((bf16[16,32,2560]{2,1,0:T(8,128)(2,1)}), bf16[16,32,2560]{2,1,0:T(8,128)(2,1)}, u32[]{:S(2)}, u32[]{:S(2)}) async-start(bf16[16,32,2560]{2,1,0:T(8,128)(2,1)} %bitcast.91), calls=%async_computation.5 | async-start | bytes 5242880 | tf_op jit(solution)/shard_map/all_to_all | solution.py:255
  176.4 1.1 copy-done.4
  178.7 2.1 fusion.18
  180.8 56.8 %all-to-all-done.5 = bf16[16,32,2560]{2,1,0:T(8,128)(2,1)} async-done(((bf16[16,32,2560]{2,1,0:T(8,128)(2,1)}), bf16[16,32,2560]{2,1,0:T(8,128)(2,1)}, u32[]{:S(2)}, u32[]{:S(2)}) %all-to-all-start.5) | async-done | bytes 2621472 | tf_op jit(solution)/shard_map/all_to_all | solution.py:255
  237.6 5.1 %fusion.2 = f32[512,768]{1,0:T(8,128)S(1)} fusion(bf16[512,2560]{1,0:T(8,128)(2,1)} %bitcast.24, bf16[1,2560,768]{2,1,0:T(8,128)(2,1)} %param.26), kind=kOutput, calls=%fused_computation.7 | convolution fusion | flops 2013265920 | bytes 8126464 | tf_op jit(solution)/shard_map/dot_general | solution.py:258
  242.7 3.0 convolution_convert_fusion
  245.7 5.5 %all-to-all-start.6 = ((bf16[16,32,2560]{2,1,0:T(8,128)(2,1)}), bf16[16,32,2560]{2,1,0:T(8,128)(2,1)}, u32[]{:S(2)}, u32[]{:S(2)}) async-start(bf16[16,32,2560]{2,1,0:T(8,128)(2,1)} %bitcast.96), calls=%async_computation.6 | async-start | bytes 5242880 | tf_op jit(solution)/shard_map/all_to_all | solution.py:263
  251.4 61.1 %all-to-all-done.6 = bf16[16,32,2560]{2,1,0:T(8,128)(2,1)} async-done(((bf16[16,32,2560]{2,1,0:T(8,128)(2,1)}), bf16[16,32,2560]{2,1,0:T(8,128)(2,1)}, u32[]{:S(2)}, u32[]{:S(2)}) %all-to-all-start.6) | async-done | bytes 2621472 | tf_op jit(solution)/shard_map/all_to_all | solution.py:263
  312.5 2.3 convert_reduce_fusion
  315.4 1.1 copy-done.1
  317.2 1.4 copy.40
  318.6 6.9 %all-to-all-start.7 = ((bf16[16,256,160]{1,2,0:T(8,128)(2,1)}), bf16[16,256,160]{1,2,0:T(8,128)(2,1)}, u32[]{:S(2)}, u32[]{:S(2)}) async-start(bf16[16,256,160]{1,2,0:T(8,128)(2,1)} %bitcast.94), calls=%async_computation.7 | async-start | bytes 2621440 | tf_op jit(solution)/shard_map/all_to_all | solution.py:148
  325.6 2.4 broadcast_select_fusion
  328.0 16.4 %all-to-all-done.7 = bf16[16,256,160]{1,2,0:T(8,128)(2,1)} async-done(((bf16[16,256,160]{1,2,0:T(8,128)(2,1)}), bf16[16,256,160]{1,2,0:T(8,128)(2,1)}, u32[]{:S(2)}, u32[]{:S(2)}) %all-to-all-start.7) | async-done | bytes 1310752 | tf_op jit(solution)/shard_map/all_to_all | solution.py:148
  344.4 1.5 convert_reduce_fusion.1
  (77 shorter events, 14.8 us)
Async XLA Ops:
  0.6 242.0 %copy-start = (bf16[1,384,2560]{2,1,0:T(8,128)(2,1)S(1)}, bf16[1,384,2560]{2,1,0:T(8,128)(2,1)}, u32[]{:S(2)}) copy-start(bf16[1,384,2560]{2,1,0:T(8,128)(2,1)} %param.27) | copy-start | bytes 5898244
  1.8 25.5 %copy-start.11 = (f32[2560]{0:T(1024)S(1)}, f32[2560]{0:T(1024)}, u32[]{:S(2)}) copy-start(f32[2560]{0:T(1024)} %param.15) | copy-start | bytes 30724
  27.3 1.3 copy-start.5
  30.4 5.9 %copy-start.13 = (s32[1,64]{1,0:T(1,128)S(1)}, s32[1,64]{1,0:T(1,128)}, u32[]{:S(2)}) copy-start(s32[1,64]{1,0:T(1,128)} %param.19) | copy-start | bytes 772
  30.4 30.3 %all-to-all-start.1 = ((bf16[16,256,224]{1,2,0:T(8,128)(2,1)}), bf16[16,256,224]{1,2,0:T(8,128)(2,1)}, u32[]{:S(2)}, u32[]{:S(2)}) async-start(bf16[16,256,224]{1,2,0:T(8,128)(2,1)} %broadcast_in_dim.41), calls=%async_computation.1 | async-start | bytes 3670016 | tf_op jit(solution)/shard_map/all_to_all | solution.py:138
  66.1 1.0 slice-start
  69.2 2.8 copy-start.2
  114.9 22.2 %copy-start.7 = (bf16[2560,160]{0,1:T(8,128)(2,1)S(1)}, bf16[2560,160]{0,1:T(8,128)(2,1)}, u32[]{:S(2)}) copy-start(bf16[2560,160]{0,1:T(8,128)(2,1)} %param.17) | copy-start | bytes 2457604
  114.9 22.2 %copy-start.8 = (bf16[256,160]{0,1:T(8,128)(2,1)S(1)}, bf16[256,160]{0,1:T(8,128)(2,1)}, u32[]{:S(2)}) copy-start(bf16[256,160]{0,1:T(8,128)(2,1)} %param.14) | copy-start | bytes 245764
  138.9 4.6 %copy-start.10 = (s32[256,6]{0,1:T(8,128)S(1)}, s32[256,6]{0,1:T(8,128)}, u32[]{:S(2)}) copy-start(s32[256,6]{0,1:T(8,128)} %param.22) | copy-start | bytes 18436
  138.9 23.8 %copy-start.9 = (f32[2560]{0:T(1024)S(1)}, f32[2560]{0:T(1024)}, u32[]{:S(2)}) copy-start(f32[2560]{0:T(1024)} %param.21) | copy-start | bytes 30724
  138.9 23.4 %all-to-all-start.4 = ((bf16[16,256,160]{1,2,0:T(8,128)(2,1)}), bf16[16,256,160]{1,2,0:T(8,128)(2,1)S(1)}, u32[]{:S(2)}, u32[]{:S(2)}) async-start(bf16[16,256,160]{1,2,0:T(8,128)(2,1)} %broadcast_in_dim.46), calls=%async_computation.4 | async-start | bytes 2621440 | tf_op jit(solution)/shard_map/all_to_all | solution.py:138
  165.4 72.2 %all-to-all-start.5 = ((bf16[16,32,2560]{2,1,0:T(8,128)(2,1)}), bf16[16,32,2560]{2,1,0:T(8,128)(2,1)}, u32[]{:S(2)}, u32[]{:S(2)}) async-start(bf16[16,32,2560]{2,1,0:T(8,128)(2,1)} %bitcast.91), calls=%async_computation.5 | async-start | bytes 5242880 | tf_op jit(solution)/shard_map/all_to_all | solution.py:255
  176.0 1.5 copy-start.4
  177.5 1.2 copy-start.6
  245.7 5.5 %copy-start.12 = (f32[256,6]{0,1:T(8,128)S(1)}, f32[256,6]{0,1:T(8,128)}, u32[]{:S(2)}) copy-start(f32[256,6]{0,1:T(8,128)} %param.23) | copy-start | bytes 18436
  245.7 66.8 %all-to-all-start.6 = ((bf16[16,32,2560]{2,1,0:T(8,128)(2,1)}), bf16[16,32,2560]{2,1,0:T(8,128)(2,1)}, u32[]{:S(2)}, u32[]{:S(2)}) async-start(bf16[16,32,2560]{2,1,0:T(8,128)(2,1)} %bitcast.96), calls=%async_computation.6 | async-start | bytes 5242880 | tf_op jit(solution)/shard_map/all_to_all | solution.py:263
  314.8 1.7 copy-start.1
  318.6 7.0 %copy-start.3 = (bf16[512,1024]{1,0:T(8,128)(2,1)S(1)}, bf16[512,1024]{1,0:T(8,128)(2,1)}, u32[]{:S(2)}) copy-start(bf16[512,1024]{1,0:T(8,128)(2,1)} %copy-done.2) | copy-start | bytes 3145732
  318.6 25.7 %all-to-all-start.7 = ((bf16[16,256,160]{1,2,0:T(8,128)(2,1)}), bf16[16,256,160]{1,2,0:T(8,128)(2,1)}, u32[]{:S(2)}, u32[]{:S(2)}) async-start(bf16[16,256,160]{1,2,0:T(8,128)(2,1)} %bitcast.94), calls=%async_computation.7 | async-start | bytes 2621440 | tf_op jit(solution)/shard_map/all_to_all | solution.py:148

commit v8 on v6

--- a/solution.py
+++ b/solution.py
@@ -72,10 +72,11 @@
         ) * (1.0 / math.sqrt(HEAD_DIM))
         scores = jnp.where(allowed, scores, -1e30)
         peak = jnp.max(scores, axis=1, keepdims=True)
-        probs = jnp.where(allowed, jnp.exp(scores - peak), 0.0)
-        total = jnp.sum(probs, axis=1, keepdims=True)
-        out_ref[:, head * HEAD_DIM : (head + 1) * HEAD_DIM] = jnp.dot(
-            probs.astype(jnp.bfloat16), values, preferred_element_type=jnp.float32
+        probs = jnp.exp(scores - peak)
+        live = jnp.where(peak > -1e29, 1.0, 0.0)
+        total = jnp.sum(probs, axis=1, keepdims=True) * live
+        out_ref[:, head * HEAD_DIM : (head + 1) * HEAD_DIM] = (
+            jnp.dot(probs.astype(jnp.bfloat16), values, preferred_element_type=jnp.float32) * live
         ).astype(out_ref.dtype)
         for slot, value in enumerate(split_three(peak) + split_three(total)):
             stats = jnp.where(lane == slot * HEADS + head, value, stats)
@@ -99,16 +100,19 @@
 
 def combine_kernel(part_ref, out_ref):
     coded = part_ref[:, :, HEADS * HEAD_DIM :].astype(jnp.float32)
+    lane_count = coded.shape[2]
+
+    def shifted(piece):
+        return pltpu.roll(coded, lane_count - piece * HEADS, 2)
+
+    peak = (coded + shifted(1)) + shifted(2)
+    total = (shifted(3) + shifted(4)) + shifted(5)
+    factors = jnp.exp(peak - jnp.max(peak, axis=0, keepdims=True))
+    denominators = jnp.sum(factors * total, axis=0)
     lane = lax.broadcasted_iota(jnp.int32, coded.shape, 2)
-
-    def pick(slot):
-        return jnp.sum(jnp.where(lane == slot, coded, 0.0), axis=2, keepdims=True)
-
     for head in range(HEADS):
-        peak = (pick(head) + pick(HEADS + head)) + pick(2 * HEADS + head)
-        total = (pick(3 * HEADS + head) + pick(4 * HEADS + head)) + pick(5 * HEADS + head)
-        factor = jnp.exp(peak - jnp.max(peak, axis=0, keepdims=True))
-        denominator = jnp.sum(factor * total, axis=0)
+        factor = jnp.sum(jnp.where(lane == head, factors, 0.0), axis=2, keepdims=True)
+        denominator = jnp.sum(jnp.where(lane[0] == head, denominators, 0.0), axis=1, keepdims=True)
         numerator = jnp.sum(
             part_ref[:, :, head * HEAD_DIM : (head + 1) * HEAD_DIM].astype(jnp.float32) * factor,
             axis=0,
@@ -135,10 +139,8 @@
 def gather_blocks(values, axis):
     count = lax.axis_size("blk")
     stacked = jnp.broadcast_to(values[None], (count,) + values.shape)
-    received = lax.all_to_all(stacked, "blk", split_axis=0, concat_axis=0, tiled=True)
-    if axis == 0:
-        return received.reshape((count * values.shape[0],) + values.shape[1:])
-    return received.transpose(1, 0, 2).reshape(values.shape[0], count * values.shape[1])
+    received = lax.all_to_all(stacked, "blk", split_axis=0, concat_axis=axis + 1, tiled=True)
+    return received.reshape(received.shape[1:])
 
 
 def scatter_sum_blocks(values):

time: 343 us -> 340 us (level)
  Pallas kernels: 17.6 us -> 14 us
where the time goes in v8:
time: 340 us; the launch traced here: 339 us
  blocking collectives  144 us (42%)
  waiting for transfers between devices  113 us (33%)
  starting transfers between devices  21.7 us (6%)
  local copies, waits for them, and re-layouts  17.1 us (5%)
  other arithmetic  17 us (5%)
  Pallas kernels  14 us (4%)
  matrix products  10.2 us (3%)
    all_to_all x1, blocking collectives, per_device(): lax.all_to_all(outgoing, 'exp', split_axis=0, concat_axis=0, tiled=True)  72.6 us
    all_to_all x1, waiting for transfers between devices, per_device(): lax.all_to_all(result.reshape(received.shape), 'exp', split_axis=0, conca...  58 us
    all_to_all x2, blocking collectives, gather_blocks(): lax.all_to_all(stacked, 'blk', split_axis=0, concat_axis=axis + 1, tiled=...  47.3 us
    all_to_all x2, waiting for transfers between devices, gather_blocks(): lax.all_to_all(stacked, 'blk', split_axis=0, concat_axis=axis + 1, tiled=...  38.4 us
    all_to_all x1, blocking collectives, per_device(): lax.all_to_all(payload, 'blk', split_axis=0, concat_axis=0, tiled=True)  24.3 us
    all_to_all x1, waiting for transfers between devices, scatter_sum_blocks(): lax.all_to_all(pieces.astype(jnp.bfloat16), 'blk', split_axis=0, concat_a...  16.4 us
    pallas_call x1, Pallas kernels, local_attention(): pl.pallas_call(attention_kernel, out_shape=jax.ShapeDtypeStruct((NEW, wid...  11.1 us
    all_to_all x2, starting transfers between devices, gather_blocks(): lax.all_to_all(stacked, 'blk', split_axis=0, concat_axis=axis + 1, tiled=...  9.88 us
  transfers between devices with their start and end apart: 4, of which 4 were waited for; matrix products, arithmetic and copies ran while one was open for 3% of the time, Pallas kernels for 0%

profile of v8, /device:TPU:1, one launch (start us, length us, event | category | flops | bytes accessed | tf_op | source)
XLA Modules:
  0.0 338.6 jit_solution(15635221586538558434)
XLA Ops:
  0.6 1.1 broadcast_in_dim.40
  1.8 25.1 %all_to_all.62 = bf16[16,256,160]{1,2,0:T(8,128)(2,1)S(1)} all-to-all(bf16[16,256,160]{1,2,0:T(8,128)(2,1)S(1)} %broadcast_in_dim.40), channel_id=1, replica_groups=mesh['blk'=16,'exp'=16] {'blk'}, dimensions={0} | all-to-all | bytes 2621440 | tf_op jit(solution)/shard_map/all_to_all | solution.py:142
  29.0 1.4 broadcast_in_dim.41
  30.4 5.3 %all-to-all-start.1 = ((bf16[16,256,224]{1,2,0:T(8,128)(2,1)}), bf16[16,256,224]{1,2,0:T(8,128)(2,1)}, u32[]{:S(2)}, u32[]{:S(2)}) async-start(bf16[16,256,224]{1,2,0:T(8,128)(2,1)} %broadcast_in_dim.41), calls=%async_computation.1 | async-start | bytes 3670016 | tf_op jit(solution)/shard_map/all_to_all | solution.py:142
  37.9 0.8 pad_maximum_fusion.2
  39.4 21.4 %all-to-all-done.1 = bf16[16,256,224]{1,2,0:T(8,128)(2,1)} async-done(((bf16[16,256,224]{1,2,0:T(8,128)(2,1)}), bf16[16,256,224]{1,2,0:T(8,128)(2,1)}, u32[]{:S(2)}, u32[]{:S(2)}) %all-to-all-start.1) | async-done | bytes 1835040 | tf_op jit(solution)/shard_map/all_to_all | solution.py:142
  60.8 1.0 slice.42
  61.7 3.9 %copy.36.proj_ref = bf16[256,3584]{1,0:T(8,128)(2,1)} copy(bf16[256,3584]{0,1:T(8,128)(2,1)} %bitcast.5) | data formatting | bytes 3670016 | tf_op jit(solution)/shard_map/reshape | solution.py:143
  67.2 2.1 gather_fusion
  69.3 2.7 bitcast_select_fusion.slot_ref
  72.0 11.1 %shard_map.149 = bf16[256,2688]{1,0:T(8,128)(2,1)} custom-call(bf16[256,3584]{1,0:T(8,128)(2,1)} %copy.36.proj_ref, f32[256,128]{1,0:T(8,128)} %get-tuple-element.9.cos_ref, f32[256,128]{1,0:T(8,128)} %get-tuple-element.10.sin_ref, bf16[512,1024]{1,0:T(8,128)(2,1)} %bitcast_select_fusion.slot_ref, s32[256,1]{1,0:T(8,128)} %iota_add_fusion.qpos_ref, ...), custom_call_target="tpu_custom_call" | custom-call | flops 1342177280 | bytes 4259840 | tf_op jit(solution)/shard_map/pallas_call | solution.py:88
  83.1 24.3 %all_to_all.63.part_ref = bf16[16,16,2688]{2,1,0:T(8,128)(2,1)} all-to-all(bf16[16,16,2688]{2,1,0:T(8,128)(2,1)} %bitcast.105), channel_id=1, replica_groups=mesh['blk'=16,'exp'=16] {'blk'}, dimensions={0} | all-to-all | bytes 2752512 | tf_op jit(solution)/shard_map/all_to_all | solution.py:222
  107.4 2.9 shard_map.150
  110.3 1.0 broadcast_in_dim.45
  111.4 22.2 %all_to_all.64 = bf16[16,16,2560]{2,1,0:T(8,128)(2,1)S(1)} all-to-all(bf16[16,16,2560]{2,1,0:T(8,128)(2,1)S(1)} %broadcast_in_dim.45), channel_id=1, replica_groups=mesh['blk'=16,'exp'=16] {'blk'}, dimensions={0} | all-to-all | bytes 2621440 | tf_op jit(solution)/shard_map/all_to_all | solution.py:142
  134.1 1.2 broadcast_in_dim.46
  135.3 4.6 %all-to-all-start.4 = ((bf16[16,256,160]{1,2,0:T(8,128)(2,1)}), bf16[16,256,160]{1,2,0:T(8,128)(2,1)S(1)}, u32[]{:S(2)}, u32[]{:S(2)}) async-start(bf16[16,256,160]{1,2,0:T(8,128)(2,1)} %broadcast_in_dim.46), calls=%async_computation.4 | async-start | bytes 2621440 | tf_op jit(solution)/shard_map/all_to_all | solution.py:142
  140.1 1.2 reduce-window.6
  141.7 17.0 %all-to-all-done.4 = bf16[16,256,160]{1,2,0:T(8,128)(2,1)S(1)} async-done(((bf16[16,256,160]{1,2,0:T(8,128)(2,1)}), bf16[16,256,160]{1,2,0:T(8,128)(2,1)S(1)}, u32[]{:S(2)}, u32[]{:S(2)}) %all-to-all-start.4) | async-done | bytes 1310752 | tf_op jit(solution)/shard_map/all_to_all | solution.py:142
  160.4 72.6 %all_to_all.65 = bf16[16,32,2560]{2,1,0:T(8,128)(2,1)S(1)} all-to-all(bf16[16,32,2560]{2,1,0:T(8,128)(2,1)S(1)} %bitcast.96), channel_id=1, replica_groups=mesh['blk'=16,'exp'=16] {'exp'}, dimensions={0} | all-to-all | bytes 5242880 | tf_op jit(solution)/shard_map/all_to_all | solution.py:257
  233.0 2.2 fusion.1
  235.2 3.1 convolution_convert_fusion
  238.3 4.9 %all-to-all-start.6 = ((bf16[16,32,2560]{2,1,0:T(8,128)(2,1)}), bf16[16,32,2560]{2,1,0:T(8,128)(2,1)}, u32[]{:S(2)}, u32[]{:S(2)}) async-start(bf16[16,32,2560]{2,1,0:T(8,128)(2,1)} %bitcast.101), calls=%async_computation.6 | async-start | bytes 5242880 | tf_op jit(solution)/shard_map/all_to_all | solution.py:264
  243.8 0.9 copy-done.3
  244.8 1.6 fusion.35
  246.4 58.0 %all-to-all-done.6 = bf16[16,32,2560]{2,1,0:T(8,128)(2,1)} async-done(((bf16[16,32,2560]{2,1,0:T(8,128)(2,1)}), bf16[16,32,2560]{2,1,0:T(8,128)(2,1)}, u32[]{:S(2)}, u32[]{:S(2)}) %all-to-all-start.6) | async-done | bytes 2621472 | tf_op jit(solution)/shard_map/all_to_all | solution.py:264
  304.4 2.3 convert_reduce_fusion
  309.2 1.4 copy.40
  310.7 6.9 %all-to-all-start.7 = ((bf16[16,256,160]{1,2,0:T(8,128)(2,1)}), bf16[16,256,160]{1,2,0:T(8,128)(2,1)}, u32[]{:S(2)}, u32[]{:S(2)}) async-start(bf16[16,256,160]{1,2,0:T(8,128)(2,1)} %bitcast.99), calls=%async_computation.7 | async-start | bytes 2621440 | tf_op jit(solution)/shard_map/all_to_all | solution.py:150
  317.7 2.4 broadcast_select_fusion
  320.1 16.4 %all-to-all-done.7 = bf16[16,256,160]{1,2,0:T(8,128)(2,1)} async-done(((bf16[16,256,160]{1,2,0:T(8,128)(2,1)}), bf16[16,256,160]{1,2,0:T(8,128)(2,1)}, u32[]{:S(2)}, u32[]{:S(2)}) %all-to-all-start.7) | async-done | bytes 1310752 | tf_op jit(solution)/shard_map/all_to_all | solution.py:150
  336.4 1.5 convert_reduce_fusion.1
  (78 shorter events, 12.3 us)
Async XLA Ops:
  0.6 234.6 %copy-start = (bf16[1,384,2560]{2,1,0:T(8,128)(2,1)S(1)}, bf16[1,384,2560]{2,1,0:T(8,128)(2,1)}, u32[]{:S(2)}) copy-start(bf16[1,384,2560]{2,1,0:T(8,128)(2,1)} %param.27) | copy-start | bytes 5898244
  1.8 25.5 %copy-start.11 = (f32[2560]{0:T(1024)S(1)}, f32[2560]{0:T(1024)}, u32[]{:S(2)}) copy-start(f32[2560]{0:T(1024)} %param.15) | copy-start | bytes 30724
  27.3 1.3 copy-start.4
  30.4 5.9 %copy-start.14 = (s32[1,64]{1,0:T(1,128)S(1)}, s32[1,64]{1,0:T(1,128)}, u32[]{:S(2)}) copy-start(s32[1,64]{1,0:T(1,128)} %param.19) | copy-start | bytes 772
  30.4 30.3 %all-to-all-start.1 = ((bf16[16,256,224]{1,2,0:T(8,128)(2,1)}), bf16[16,256,224]{1,2,0:T(8,128)(2,1)}, u32[]{:S(2)}, u32[]{:S(2)}) async-start(bf16[16,256,224]{1,2,0:T(8,128)(2,1)} %broadcast_in_dim.41), calls=%async_computation.1 | async-start | bytes 3670016 | tf_op jit(solution)/shard_map/all_to_all | solution.py:142
  66.2 1.0 slice-start
  69.3 2.8 copy-start.1
  111.3 22.2 %copy-start.7 = (bf16[2560,160]{0,1:T(8,128)(2,1)S(1)}, bf16[2560,160]{0,1:T(8,128)(2,1)}, u32[]{:S(2)}) copy-start(bf16[2560,160]{0,1:T(8,128)(2,1)} %param.17) | copy-start | bytes 2457604
  111.4 22.2 %copy-start.8 = (bf16[256,160]{0,1:T(8,128)(2,1)S(1)}, bf16[256,160]{0,1:T(8,128)(2,1)}, u32[]{:S(2)}) copy-start(bf16[256,160]{0,1:T(8,128)(2,1)} %param.14) | copy-start | bytes 245764
  135.3 4.6 %copy-start.10 = (s32[256,6]{0,1:T(8,128)S(1)}, s32[256,6]{0,1:T(8,128)}, u32[]{:S(2)}) copy-start(s32[256,6]{0,1:T(8,128)} %param.22) | copy-start | bytes 18436
  135.3 23.8 %copy-start.9 = (f32[2560]{0:T(1024)S(1)}, f32[2560]{0:T(1024)}, u32[]{:S(2)}) copy-start(f32[2560]{0:T(1024)} %param.21) | copy-start | bytes 30724
  135.3 23.4 %all-to-all-start.4 = ((bf16[16,256,160]{1,2,0:T(8,128)(2,1)}), bf16[16,256,160]{1,2,0:T(8,128)(2,1)S(1)}, u32[]{:S(2)}, u32[]{:S(2)}) async-start(bf16[16,256,160]{1,2,0:T(8,128)(2,1)} %broadcast_in_dim.46), calls=%async_computation.4 | async-start | bytes 2621440 | tf_op jit(solution)/shard_map/all_to_all | solution.py:142
  160.3 72.7 %copy-start.13 = (bf16[1,2560,768]{2,1,0:T(8,128)(2,1)S(1)}, bf16[1,2560,768]{2,1,0:T(8,128)(2,1)}, u32[]{:S(2)}) copy-start(bf16[1,2560,768]{2,1,0:T(8,128)(2,1)} %param.26) | copy-start | bytes 11796484
  238.3 4.9 %copy-start.12 = (f32[256,6]{0,1:T(8,128)S(1)}, f32[256,6]{0,1:T(8,128)}, u32[]{:S(2)}) copy-start(f32[256,6]{0,1:T(8,128)} %param.23) | copy-start | bytes 18436
  238.3 66.1 %all-to-all-start.6 = ((bf16[16,32,2560]{2,1,0:T(8,128)(2,1)}), bf16[16,32,2560]{2,1,0:T(8,128)(2,1)}, u32[]{:S(2)}, u32[]{:S(2)}) async-start(bf16[16,32,2560]{2,1,0:T(8,128)(2,1)} %bitcast.101), calls=%async_computation.6 | async-start | bytes 5242880 | tf_op jit(solution)/shard_map/all_to_all | solution.py:264
  243.2 1.5 copy-start.3
  307.3 1.0 copy-start.5
  307.3 1.3 copy-start.6
  310.7 7.0 %copy-start.2 = (bf16[512,1024]{1,0:T(8,128)(2,1)S(1)}, bf16[512,1024]{1,0:T(8,128)(2,1)}, u32[]{:S(2)}) copy-start(bf16[512,1024]{1,0:T(8,128)(2,1)} %copy-done.1) | copy-start | bytes 3145732
  310.7 25.7 %all-to-all-start.7 = ((bf16[16,256,160]{1,2,0:T(8,128)(2,1)}), bf16[16,256,160]{1,2,0:T(8,128)(2,1)}, u32[]{:S(2)}, u32[]{:S(2)}) async-start(bf16[16,256,160]{1,2,0:T(8,128)(2,1)} %bitcast.99), calls=%async_computation.7 | async-start | bytes 2621440 | tf_op jit(solution)/shard_map/all_to_all | solution.py:150

commit v9 on v8

--- a/solution.py
+++ b/solution.py
@@ -239,6 +239,7 @@
         jnp.bfloat16
     )
     shared_term = jnp.dot(shared_act, shared_down, preferred_element_type=jnp.float32)
+    shared_sum = lax.psum_scatter(shared_term, "blk", scatter_dimension=1, tiled=True)
     row_experts = groups // SPLIT
     expert_count = row_experts * blocks
     capacity = NEW * TOPK * 4 // (expert_count * 3)
@@ -261,22 +262,31 @@
     result = jnp.dot(activated, expert_down[0], preferred_element_type=jnp.float32).astype(
         jnp.bfloat16
     )
-    returned = lax.all_to_all(
-        result.reshape(received.shape), "exp", split_axis=0, concat_axis=0, tiled=True
-    )
+    column_width = model_width // blocks
+    sent_back = (
+        result.reshape(groups, capacity, blocks, column_width)
+        .transpose(2, 0, 1, 3)
+        .reshape(blocks * groups, capacity, column_width)
+    )
+    returned = lax.all_to_all(sent_back, ("blk", "exp"), split_axis=0, concat_axis=0, tiled=True)
     summed = jnp.sum(
-        returned.reshape(row_experts, SPLIT, capacity, model_width).astype(jnp.float32), axis=1
-    )
-    slot_weight = jnp.sum(placed.astype(jnp.float32) * route_share.T[:, None, :], axis=2)
+        returned.reshape(expert_count, SPLIT, capacity, column_width).astype(jnp.float32), axis=1
+    )
+    every_expert = jnp.arange(expert_count, dtype=jnp.int32)
+    all_hits = route_ids[:, :, None] == every_expert[None, None, :]
+    all_chosen = jnp.any(all_hits, axis=1)
+    all_share = jnp.sum(jnp.where(all_hits, route_weights[:, :, None], 0.0), axis=1)
+    all_rank = jnp.cumsum(all_chosen.astype(jnp.int32), axis=0) - 1
+    all_placed = all_chosen.T[:, None, :] & (all_rank.T[:, None, :] == slot_ids[None, :, None])
+    all_selector = all_placed.astype(jnp.bfloat16)
+    slot_weight = jnp.sum(all_placed.astype(jnp.float32) * all_share.T[:, None, :], axis=2)
     slot_values = summed * slot_weight[:, :, None]
     upper_part = slot_values.astype(jnp.bfloat16)
     lower_part = (slot_values - upper_part.astype(jnp.float32)).astype(jnp.bfloat16)
-    routed = jnp.einsum(
-        "ect,ecd->td", selector, upper_part, preferred_element_type=jnp.float32
-    ) + jnp.einsum("ect,ecd->td", selector, lower_part, preferred_element_type=jnp.float32)
-    layer_term = shared_term + routed
-    summed_cols = scatter_sum_blocks(layer_term)
-    hidden_out = (mixed_cols.astype(jnp.float32) + summed_cols).astype(jnp.bfloat16)
+    routed_cols = jnp.einsum(
+        "ect,ecd->td", all_selector, upper_part, preferred_element_type=jnp.float32
+    ) + jnp.einsum("ect,ecd->td", all_selector, lower_part, preferred_element_type=jnp.float32)
+    hidden_out = (mixed_cols.astype(jnp.float32) + shared_sum + routed_cols).astype(jnp.bfloat16)
     return (hidden_out, pool_out[None])
 
 

time: 340 us -> 387 us (1.14)
  waiting for transfers between devices: 113 us -> 187 us
  blocking collectives: 144 us -> 71.5 us
  local copies, waits for them, and re-layouts: 17.1 us -> 32 us
  between operations: 1.62 us -> 15 us
  starting transfers between devices: 21.7 us -> 31.3 us
  matrix products: 10.2 us -> 17.5 us
    all_to_all x2, waiting for transfers between devices: 74.4 us -> 148 us  [the longest x1 86.6 us: per_device(): lax.all_to_all(sent_back, ('blk', 'exp'), split_axis=0, concat_axis=0, ti...]
    all_to_all x1 -> x0, blocking collectives: 72.6 us -> none  [per_device(): lax.all_to_all(outgoing, 'exp', split_axis=0, concat_axis=0, tiled=True)]
    reshape x0 -> x2, local copies, waits for them, and re-layouts: none -> 13.9 us  [per_device(): result.reshape(groups, capacity, blocks, column_width).transpose(2, 0, 1, 3)]
    all_to_all x2, starting transfers between devices: 11.8 us -> 21.1 us  [the longest x1 10.6 us: per_device(): lax.all_to_all(sent_back, ('blk', 'exp'), split_axis=0, concat_axis=0, ti...]
  transfers between devices with their start and end apart: 4 -> 5, of which waited for: 4 -> 4; matrix products, arithmetic and copies ran while one was open for 3% -> 5% of each run, Pallas kernels for 0% -> 0%
where the time goes in v9:
time: 387 us; the launch traced here: 385 us
  waiting for transfers between devices  187 us (48%)
  blocking collectives  71.5 us (18%)
  local copies, waits for them, and re-layouts  32 us (8%)
  starting transfers between devices  31.3 us (8%)
  other arithmetic  17.5 us (5%)
  matrix products  17.5 us (5%)
  between operations  15 us (4%)
  Pallas kernels  14 us (4%)
    all_to_all x1, waiting for transfers between devices, per_device(): lax.all_to_all(sent_back, ('blk', 'exp'), split_axis=0, concat_axis=0, ti...  86.6 us
    all_to_all x1, waiting for transfers between devices, per_device(): lax.all_to_all(outgoing, 'exp', split_axis=0, concat_axis=0, tiled=True)  61.6 us
    all_to_all x2, blocking collectives, gather_blocks(): lax.all_to_all(stacked, 'blk', split_axis=0, concat_axis=axis + 1, tiled=...  47.2 us
    all_to_all x2, waiting for transfers between devices, gather_blocks(): lax.all_to_all(stacked, 'blk', split_axis=0, concat_axis=axis + 1, tiled=...  38.4 us
    all_to_all x1, blocking collectives, per_device(): lax.all_to_all(payload, 'blk', split_axis=0, concat_axis=0, tiled=True)  24.3 us
    reshape x2, local copies, waits for them, and re-layouts, per_device(): result.reshape(groups, capacity, blocks, column_width).transpose(2, 0, 1, 3)  13.9 us
    pallas_call x1, Pallas kernels, local_attention(): pl.pallas_call(attention_kernel, out_shape=jax.ShapeDtypeStruct((NEW, wid...  11.1 us
    all_to_all x1, starting transfers between devices, per_device(): lax.all_to_all(sent_back, ('blk', 'exp'), split_axis=0, concat_axis=0, ti...  10.6 us
  transfers between devices with their start and end apart: 5, of which 4 were waited for; matrix products, arithmetic and copies ran while one was open for 5% of the time, Pallas kernels for 0%

profile of v9, /device:TPU:1, one launch (start us, length us, event | category | flops | bytes accessed | tf_op | source)
XLA Modules:
  0.0 385.3 jit_solution(2697429138453168429)
XLA Ops:
  7.2 1.1 broadcast_in_dim.40
  8.3 25.1 %all_to_all.57 = bf16[16,256,160]{1,2,0:T(8,128)(2,1)S(1)} all-to-all(bf16[16,256,160]{1,2,0:T(8,128)(2,1)S(1)} %broadcast_in_dim.40), channel_id=1, replica_groups=mesh['blk'=16,'exp'=16] {'blk'}, dimensions={0} | all-to-all | bytes 2621440 | tf_op jit(solution)/shard_map/all_to_all | solution.py:142
  35.2 1.4 broadcast_in_dim.41
  36.6 5.3 %all-to-all-start.1 = ((bf16[16,256,224]{1,2,0:T(8,128)(2,1)}), bf16[16,256,224]{1,2,0:T(8,128)(2,1)}, u32[]{:S(2)}, u32[]{:S(2)}) async-start(bf16[16,256,224]{1,2,0:T(8,128)(2,1)} %broadcast_in_dim.41), calls=%async_computation.1 | async-start | bytes 3670016 | tf_op jit(solution)/shard_map/all_to_all | solution.py:142
  45.6 21.4 %all-to-all-done.1 = bf16[16,256,224]{1,2,0:T(8,128)(2,1)} async-done(((bf16[16,256,224]{1,2,0:T(8,128)(2,1)}), bf16[16,256,224]{1,2,0:T(8,128)(2,1)}, u32[]{:S(2)}, u32[]{:S(2)}) %all-to-all-start.1) | async-done | bytes 1835040 | tf_op jit(solution)/shard_map/all_to_all | solution.py:142
  67.9 3.9 %copy.71.proj_ref = bf16[256,3584]{1,0:T(8,128)(2,1)} copy(bf16[256,3584]{0,1:T(8,128)(2,1)} %bitcast.5) | data formatting | bytes 3670016 | tf_op jit(solution)/shard_map/reshape | solution.py:143
  72.8 1.2 copy.83
  74.8 2.1 gather_fusion
  76.9 2.7 bitcast_select_fusion.slot_ref
  79.6 11.1 %shard_map.149 = bf16[256,2688]{1,0:T(8,128)(2,1)} custom-call(bf16[256,3584]{1,0:T(8,128)(2,1)} %copy.71.proj_ref, f32[256,128]{1,0:T(8,128)} %get-tuple-element.11.cos_ref, f32[256,128]{1,0:T(8,128)} %get-tuple-element.12.sin_ref, bf16[512,1024]{1,0:T(8,128)(2,1)} %bitcast_select_fusion.slot_ref, s32[256,1]{1,0:T(8,128)} %iota_add_fusion.qpos_ref, ...), custom_call_target="tpu_custom_call" | custom-call | flops 1342177280 | bytes 4259840 | tf_op jit(solution)/shard_map/pallas_call | solution.py:88
  90.8 24.3 %all_to_all.58.part_ref = bf16[16,16,2688]{2,1,0:T(8,128)(2,1)} all-to-all(bf16[16,16,2688]{2,1,0:T(8,128)(2,1)} %bitcast.119), channel_id=1, replica_groups=mesh['blk'=16,'exp'=16] {'blk'}, dimensions={0} | all-to-all | bytes 2752512 | tf_op jit(solution)/shard_map/all_to_all | solution.py:222
  115.1 2.9 shard_map.150
  119.0 22.1 %all_to_all.59 = bf16[16,16,2560]{2,1,0:T(8,128)(2,1)S(1)} all-to-all(bf16[16,16,2560]{2,1,0:T(8,128)(2,1)S(1)} %broadcast_in_dim.45), channel_id=1, replica_groups=mesh['blk'=16,'exp'=16] {'blk'}, dimensions={0} | all-to-all | bytes 2621440 | tf_op jit(solution)/shard_map/all_to_all | solution.py:142
  141.7 1.2 broadcast_in_dim.46
  142.9 4.6 %all-to-all-start.4 = ((bf16[16,256,160]{1,2,0:T(8,128)(2,1)}), bf16[16,256,160]{1,2,0:T(8,128)(2,1)S(1)}, u32[]{:S(2)}, u32[]{:S(2)}) async-start(bf16[16,256,160]{1,2,0:T(8,128)(2,1)} %broadcast_in_dim.46), calls=%async_computation.4 | async-start | bytes 2621440 | tf_op jit(solution)/shard_map/all_to_all | solution.py:142
  147.6 1.2 reduce-window.16
  149.3 17.0 %all-to-all-done.4 = bf16[16,256,160]{1,2,0:T(8,128)(2,1)S(1)} async-done(((bf16[16,256,160]{1,2,0:T(8,128)(2,1)}), bf16[16,256,160]{1,2,0:T(8,128)(2,1)S(1)}, u32[]{:S(2)}, u32[]{:S(2)}) %all-to-all-start.4) | async-done | bytes 1310752 | tf_op jit(solution)/shard_map/all_to_all | solution.py:142
  167.7 1.8 broadcast_in_dim.47
  169.4 10.5 %all-to-all-start.5 = ((bf16[16,32,2560]{2,1,0:T(8,128)(2,1)}), bf16[16,32,2560]{2,1,0:T(8,128)(2,1)}, u32[]{:S(2)}, u32[]{:S(2)}) async-start(bf16[16,32,2560]{2,1,0:T(8,128)(2,1)} %bitcast.113), calls=%async_computation.6 | async-start | bytes 5242880 | tf_op jit(solution)/shard_map/all_to_all | solution.py:258
  180.0 61.6 %all-to-all-done.5 = bf16[16,32,2560]{2,1,0:T(8,128)(2,1)} async-done(((bf16[16,32,2560]{2,1,0:T(8,128)(2,1)}), bf16[16,32,2560]{2,1,0:T(8,128)(2,1)}, u32[]{:S(2)}, u32[]{:S(2)}) %all-to-all-start.5) | async-done | bytes 2621472 | tf_op jit(solution)/shard_map/all_to_all | solution.py:258
  241.6 5.1 %fusion = f32[512,768]{1,0:T(8,128)S(1)} fusion(bf16[512,2560]{1,0:T(8,128)(2,1)} %bitcast.30, bf16[1,2560,768]{2,1,0:T(8,128)(2,1)} %param.26), kind=kOutput, calls=%fused_computation.3 | convolution fusion | flops 2013265920 | bytes 8126464 | tf_op jit(solution)/shard_map/dot_general | solution.py:260
  246.7 3.0 convolution_convert_fusion
  249.8 8.3 %reshape.315 = bf16[16,32,16,160]{3,2,1,0:T(8,128)(2,1)} reshape(bf16[512,2560]{1,0:T(8,128)(2,1)} %convolution_convert_fusion) | data formatting | bytes 5242880 | tf_op jit(solution)/shard_map/reshape | solution.py:267
  258.1 5.6 %copy.77 = bf16[16,32,16,160]{3,1,0,2:T(8,128)(2,1)} copy(bf16[16,32,16,160]{3,2,1,0:T(8,128)(2,1)} %reshape.315) | data formatting | bytes 5242880 | tf_op jit(solution)/shard_map/reshape | solution.py:267
  263.7 10.6 %all-to-all-start.6 = ((bf16[256,32,160]{2,1,0:T(8,128)(2,1)}), bf16[256,32,160]{2,1,0:T(8,128)(2,1)}, u32[]{:S(2)}, u32[]{:S(2)}) async-start(bf16[256,32,160]{2,1,0:T(8,128)(2,1)} %bitcast.112), calls=%async_computation.7 | async-start | bytes 8388608 | tf_op jit(solution)/shard_map/all_to_all | solution.py:271
  275.0 1.1 copy-done.3
  277.0 2.3 fusion.40
  281.1 2.4 broadcast_select_fusion
  283.5 86.6 %all-to-all-done.6 = bf16[256,32,160]{2,1,0:T(8,128)(2,1)} async-done(((bf16[256,32,160]{2,1,0:T(8,128)(2,1)}), bf16[256,32,160]{2,1,0:T(8,128)(2,1)}, u32[]{:S(2)}, u32[]{:S(2)}) %all-to-all-start.6) | async-done | bytes 2621472 | tf_op jit(solution)/shard_map/all_to_all | solution.py:271
  370.1 3.5 convert_reduce_fusion
  373.9 1.5 fusion.13
  375.5 3.0 fusion.25
  (84 shorter events, 14.7 us)
Async XLA Ops:
  7.2 239.6 %copy-start = (bf16[1,384,2560]{2,1,0:T(8,128)(2,1)S(1)}, bf16[1,384,2560]{2,1,0:T(8,128)(2,1)}, u32[]{:S(2)}) copy-start(bf16[1,384,2560]{2,1,0:T(8,128)(2,1)} %param.27) | copy-start | bytes 5898244
  8.3 25.5 %copy-start.10 = (f32[2560]{0:T(1024)S(1)}, f32[2560]{0:T(1024)}, u32[]{:S(2)}) copy-start(f32[2560]{0:T(1024)} %param.15) | copy-start | bytes 30724
  33.5 1.3 copy-start.4
  36.6 5.9 %copy-start.12 = (s32[1,64]{1,0:T(1,128)S(1)}, s32[1,64]{1,0:T(1,128)}, u32[]{:S(2)}) copy-start(s32[1,64]{1,0:T(1,128)} %param.19) | copy-start | bytes 772
  36.6 30.3 %all-to-all-start.1 = ((bf16[16,256,224]{1,2,0:T(8,128)(2,1)}), bf16[16,256,224]{1,2,0:T(8,128)(2,1)}, u32[]{:S(2)}, u32[]{:S(2)}) async-start(bf16[16,256,224]{1,2,0:T(8,128)(2,1)} %broadcast_in_dim.41), calls=%async_computation.1 | async-start | bytes 3670016 | tf_op jit(solution)/shard_map/all_to_all | solution.py:142
  72.8 1.9 slice-start
  76.9 13.9 %copy-start.1 = (bf16[512,1024]{1,0:T(8,128)(2,1)}, bf16[512,1024]{1,0:T(8,128)(2,1)S(1)}, u32[]{:S(2)}) copy-start(bf16[512,1024]{1,0:T(8,128)(2,1)S(1)} %gather_fusion) | copy-start | bytes 3145732
  118.0 23.2 %copy-start.6 = (bf16[2560,160]{0,1:T(8,128)(2,1)S(1)}, bf16[2560,160]{0,1:T(8,128)(2,1)}, u32[]{:S(2)}) copy-start(bf16[2560,160]{0,1:T(8,128)(2,1)} %param.17) | copy-start | bytes 2457604
  118.0 23.2 %copy-start.7 = (bf16[256,160]{0,1:T(8,128)(2,1)S(1)}, bf16[256,160]{0,1:T(8,128)(2,1)}, u32[]{:S(2)}) copy-start(bf16[256,160]{0,1:T(8,128)(2,1)} %param.14) | copy-start | bytes 245764
  141.7 5.8 %copy-start.8 = (s32[256,6]{0,1:T(8,128)S(1)}, s32[256,6]{0,1:T(8,128)}, u32[]{:S(2)}) copy-start(s32[256,6]{0,1:T(8,128)} %param.22) | copy-start | bytes 18436
  142.9 23.8 %copy-start.9 = (f32[2560]{0:T(1024)S(1)}, f32[2560]{0:T(1024)}, u32[]{:S(2)}) copy-start(f32[2560]{0:T(1024)} %param.21) | copy-start | bytes 30724
  142.9 23.4 %all-to-all-start.4 = ((bf16[16,256,160]{1,2,0:T(8,128)(2,1)}), bf16[16,256,160]{1,2,0:T(8,128)(2,1)S(1)}, u32[]{:S(2)}, u32[]{:S(2)}) async-start(bf16[16,256,160]{1,2,0:T(8,128)(2,1)} %broadcast_in_dim.46), calls=%async_computation.4 | async-start | bytes 2621440 | tf_op jit(solution)/shard_map/all_to_all | solution.py:142
  169.4 72.2 %all-to-all-start.5 = ((bf16[16,32,2560]{2,1,0:T(8,128)(2,1)}), bf16[16,32,2560]{2,1,0:T(8,128)(2,1)}, u32[]{:S(2)}, u32[]{:S(2)}) async-start(bf16[16,32,2560]{2,1,0:T(8,128)(2,1)} %bitcast.113), calls=%async_computation.6 | async-start | bytes 5242880 | tf_op jit(solution)/shard_map/all_to_all | solution.py:258
  263.7 106.4 %all-to-all-start.6 = ((bf16[256,32,160]{2,1,0:T(8,128)(2,1)}), bf16[256,32,160]{2,1,0:T(8,128)(2,1)}, u32[]{:S(2)}, u32[]{:S(2)}) async-start(bf16[256,32,160]{2,1,0:T(8,128)(2,1)} %bitcast.112), calls=%async_computation.7 | async-start | bytes 8388608 | tf_op jit(solution)/shard_map/all_to_all | solution.py:271
  274.3 101.1 %reduce-scatter.2.cloned.1.call-start = ((), (), s32[]{:S(2)}) async-start(), calls=%async_computation.8 | async-start | bytes 2785280 | tf_op jit(solution)/shard_map/reduce_scatter | solution.py:242
  274.6 1.5 copy-start.3
  275.0 2.0 copy-start.5
  279.4 0.9 copy-start.11
  279.4 1.7 copy-start.2
Sparse Core Ops, SparseCore 0:
  279.5 72.6 reduce-scatter.1

commit v10 on v8

--- a/solution.py
+++ b/solution.py
@@ -56,30 +56,41 @@
     key_width = KV_HEADS * HEAD_DIM
     group_size = HEADS // KV_HEADS
     allowed = kpos_ref[...] <= qpos_ref[...]
+    group_allowed = jnp.concatenate([allowed] * group_size, axis=0)
     cosine = cos_ref[...]
     sine_signed = sin_ref[...]
     lane = lax.broadcasted_iota(jnp.int32, (NEW, 128), 1)
     stats = jnp.zeros((NEW, 128), jnp.float32)
-    for head in range(HEADS):
-        kv = head // group_size
-        raw = proj_ref[:, head * HEAD_DIM : (head + 1) * HEAD_DIM].astype(jnp.float32)
-        swapped = pltpu.roll(raw, HEAD_DIM // 2, 1)
-        query = (raw * cosine + swapped * sine_signed).astype(jnp.bfloat16)
+    for kv in range(KV_HEADS):
+        rotated = []
+        for member in range(group_size):
+            head = kv * group_size + member
+            raw = proj_ref[:, head * HEAD_DIM : (head + 1) * HEAD_DIM].astype(jnp.float32)
+            swapped = pltpu.roll(raw, HEAD_DIM // 2, 1)
+            rotated.append((raw * cosine + swapped * sine_signed).astype(jnp.bfloat16))
+        query = jnp.concatenate(rotated, axis=0)
         keys = slot_ref[:, kv * HEAD_DIM : (kv + 1) * HEAD_DIM]
         values = slot_ref[:, key_width + kv * HEAD_DIM : key_width + (kv + 1) * HEAD_DIM]
         scores = lax.dot_general(
             query, keys, (((1,), (1,)), ((), ())), preferred_element_type=jnp.float32
         ) * (1.0 / math.sqrt(HEAD_DIM))
-        scores = jnp.where(allowed, scores, -1e30)
+        scores = jnp.where(group_allowed, scores, -1e30)
         peak = jnp.max(scores, axis=1, keepdims=True)
         probs = jnp.exp(scores - peak)
         live = jnp.where(peak > -1e29, 1.0, 0.0)
         total = jnp.sum(probs, axis=1, keepdims=True) * live
-        out_ref[:, head * HEAD_DIM : (head + 1) * HEAD_DIM] = (
+        weighted = (
             jnp.dot(probs.astype(jnp.bfloat16), values, preferred_element_type=jnp.float32) * live
-        ).astype(out_ref.dtype)
-        for slot, value in enumerate(split_three(peak) + split_three(total)):
-            stats = jnp.where(lane == slot * HEADS + head, value, stats)
+        )
+        for member in range(group_size):
+            head = kv * group_size + member
+            rows = slice(member * NEW, (member + 1) * NEW)
+            out_ref[:, head * HEAD_DIM : (head + 1) * HEAD_DIM] = weighted[rows].astype(
+                out_ref.dtype
+            )
+            pieces = split_three(peak[rows]) + split_three(total[rows])
+            for slot, value in enumerate(pieces):
+                stats = jnp.where(lane == slot * HEADS + head, value, stats)
     out_ref[:, HEADS * HEAD_DIM :] = stats.astype(out_ref.dtype)
 
 

time: 340 us -> 338 us (level)
  no operation moved by 1% of the time
where the time goes in v10:
time: 338 us; the launch traced here: 337 us
  blocking collectives  144 us (43%)
  waiting for transfers between devices  113 us (33%)
  starting transfers between devices  21.9 us (6%)
  local copies, waits for them, and re-layouts  17.1 us (5%)
  other arithmetic  17 us (5%)
  Pallas kernels  12.6 us (4%)
  matrix products  10.2 us (3%)
    all_to_all x1, blocking collectives, per_device(): lax.all_to_all(outgoing, 'exp', split_axis=0, concat_axis=0, tiled=True)  72.6 us
    all_to_all x1, waiting for transfers between devices, per_device(): lax.all_to_all(result.reshape(received.shape), 'exp', split_axis=0, conca...  58 us
    all_to_all x2, blocking collectives, gather_blocks(): lax.all_to_all(stacked, 'blk', split_axis=0, concat_axis=axis + 1, tiled=...  47.3 us
    all_to_all x2, waiting for transfers between devices, gather_blocks(): lax.all_to_all(stacked, 'blk', split_axis=0, concat_axis=axis + 1, tiled=...  38.4 us
    all_to_all x1, blocking collectives, per_device(): lax.all_to_all(payload, 'blk', split_axis=0, concat_axis=0, tiled=True)  24.3 us
    all_to_all x1, waiting for transfers between devices, scatter_sum_blocks(): lax.all_to_all(pieces.astype(jnp.bfloat16), 'blk', split_axis=0, concat_a...  16.4 us
    all_to_all x2, starting transfers between devices, gather_blocks(): lax.all_to_all(stacked, 'blk', split_axis=0, concat_axis=axis + 1, tiled=...  10.1 us
    pallas_call x1, Pallas kernels, local_attention(): pl.pallas_call(attention_kernel, out_shape=jax.ShapeDtypeStruct((NEW, wid...  9.72 us
  transfers between devices with their start and end apart: 4, of which 4 were waited for; matrix products, arithmetic and copies ran while one was open for 3% of the time, Pallas kernels for 0%

profile of v10, /device:TPU:1, one launch (start us, length us, event | category | flops | bytes accessed | tf_op | source)
XLA Modules:
  0.0 337.4 jit_solution(5784764203485230264)
XLA Ops:
  0.6 1.1 broadcast_in_dim.40
  1.8 25.1 %all_to_all.62 = bf16[16,256,160]{1,2,0:T(8,128)(2,1)S(1)} all-to-all(bf16[16,256,160]{1,2,0:T(8,128)(2,1)S(1)} %broadcast_in_dim.40), channel_id=1, replica_groups=mesh['blk'=16,'exp'=16] {'blk'}, dimensions={0} | all-to-all | bytes 2621440 | tf_op jit(solution)/shard_map/all_to_all | solution.py:153
  29.0 1.4 broadcast_in_dim.41
  30.4 5.3 %all-to-all-start.1 = ((bf16[16,256,224]{1,2,0:T(8,128)(2,1)}), bf16[16,256,224]{1,2,0:T(8,128)(2,1)}, u32[]{:S(2)}, u32[]{:S(2)}) async-start(bf16[16,256,224]{1,2,0:T(8,128)(2,1)} %broadcast_in_dim.41), calls=%async_computation.1 | async-start | bytes 3670016 | tf_op jit(solution)/shard_map/all_to_all | solution.py:153
  37.9 0.8 pad_maximum_fusion.2
  39.4 21.4 %all-to-all-done.1 = bf16[16,256,224]{1,2,0:T(8,128)(2,1)} async-done(((bf16[16,256,224]{1,2,0:T(8,128)(2,1)}), bf16[16,256,224]{1,2,0:T(8,128)(2,1)}, u32[]{:S(2)}, u32[]{:S(2)}) %all-to-all-start.1) | async-done | bytes 1835040 | tf_op jit(solution)/shard_map/all_to_all | solution.py:153
  60.8 1.0 slice.42
  61.7 3.9 %copy.36.proj_ref = bf16[256,3584]{1,0:T(8,128)(2,1)} copy(bf16[256,3584]{0,1:T(8,128)(2,1)} %bitcast.5) | data formatting | bytes 3670016 | tf_op jit(solution)/shard_map/reshape | solution.py:154
  67.2 2.1 gather_fusion
  69.3 2.7 bitcast_select_fusion.slot_ref
  72.0 9.7 %shard_map.149 = bf16[256,2688]{1,0:T(8,128)(2,1)} custom-call(bf16[256,3584]{1,0:T(8,128)(2,1)} %copy.36.proj_ref, f32[256,128]{1,0:T(8,128)} %get-tuple-element.9.cos_ref, f32[256,128]{1,0:T(8,128)} %get-tuple-element.10.sin_ref, bf16[512,1024]{1,0:T(8,128)(2,1)} %bitcast_select_fusion.slot_ref, s32[256,1]{1,0:T(8,128)} %iota_add_fusion.qpos_ref, ...), custom_call_target="tpu_custom_call" | custom-call | flops 1342177280 | bytes 4259840 | tf_op jit(solution)/shard_map/pallas_call | solution.py:99
  81.7 24.3 %all_to_all.63.part_ref = bf16[16,16,2688]{2,1,0:T(8,128)(2,1)} all-to-all(bf16[16,16,2688]{2,1,0:T(8,128)(2,1)} %bitcast.105), channel_id=1, replica_groups=mesh['blk'=16,'exp'=16] {'blk'}, dimensions={0} | all-to-all | bytes 2752512 | tf_op jit(solution)/shard_map/all_to_all | solution.py:233
  106.0 2.9 shard_map.150
  108.9 1.0 broadcast_in_dim.45
  110.0 22.2 %all_to_all.64 = bf16[16,16,2560]{2,1,0:T(8,128)(2,1)S(1)} all-to-all(bf16[16,16,2560]{2,1,0:T(8,128)(2,1)S(1)} %broadcast_in_dim.45), channel_id=1, replica_groups=mesh['blk'=16,'exp'=16] {'blk'}, dimensions={0} | all-to-all | bytes 2621440 | tf_op jit(solution)/shard_map/all_to_all | solution.py:153
  132.8 1.2 broadcast_in_dim.46
  134.0 4.8 %all-to-all-start.4 = ((bf16[16,256,160]{1,2,0:T(8,128)(2,1)}), bf16[16,256,160]{1,2,0:T(8,128)(2,1)S(1)}, u32[]{:S(2)}, u32[]{:S(2)}) async-start(bf16[16,256,160]{1,2,0:T(8,128)(2,1)} %broadcast_in_dim.46), calls=%async_computation.4 | async-start | bytes 2621440 | tf_op jit(solution)/shard_map/all_to_all | solution.py:153
  138.9 1.2 reduce-window.6
  140.5 17.0 %all-to-all-done.4 = bf16[16,256,160]{1,2,0:T(8,128)(2,1)S(1)} async-done(((bf16[16,256,160]{1,2,0:T(8,128)(2,1)}), bf16[16,256,160]{1,2,0:T(8,128)(2,1)S(1)}, u32[]{:S(2)}, u32[]{:S(2)}) %all-to-all-start.4) | async-done | bytes 1310752 | tf_op jit(solution)/shard_map/all_to_all | solution.py:153
  159.1 72.6 %all_to_all.65 = bf16[16,32,2560]{2,1,0:T(8,128)(2,1)S(1)} all-to-all(bf16[16,32,2560]{2,1,0:T(8,128)(2,1)S(1)} %bitcast.96), channel_id=1, replica_groups=mesh['blk'=16,'exp'=16] {'exp'}, dimensions={0} | all-to-all | bytes 5242880 | tf_op jit(solution)/shard_map/all_to_all | solution.py:268
  231.8 2.2 fusion.1
  234.0 3.1 convolution_convert_fusion
  237.1 4.9 %all-to-all-start.6 = ((bf16[16,32,2560]{2,1,0:T(8,128)(2,1)}), bf16[16,32,2560]{2,1,0:T(8,128)(2,1)}, u32[]{:S(2)}, u32[]{:S(2)}) async-start(bf16[16,32,2560]{2,1,0:T(8,128)(2,1)} %bitcast.101), calls=%async_computation.6 | async-start | bytes 5242880 | tf_op jit(solution)/shard_map/all_to_all | solution.py:275
  242.6 0.9 copy-done.3
  243.6 1.6 fusion.35
  245.2 58.0 %all-to-all-done.6 = bf16[16,32,2560]{2,1,0:T(8,128)(2,1)} async-done(((bf16[16,32,2560]{2,1,0:T(8,128)(2,1)}), bf16[16,32,2560]{2,1,0:T(8,128)(2,1)}, u32[]{:S(2)}, u32[]{:S(2)}) %all-to-all-start.6) | async-done | bytes 2621472 | tf_op jit(solution)/shard_map/all_to_all | solution.py:275
  303.2 2.3 convert_reduce_fusion
  308.0 1.4 copy.40
  309.5 6.9 %all-to-all-start.7 = ((bf16[16,256,160]{1,2,0:T(8,128)(2,1)}), bf16[16,256,160]{1,2,0:T(8,128)(2,1)}, u32[]{:S(2)}, u32[]{:S(2)}) async-start(bf16[16,256,160]{1,2,0:T(8,128)(2,1)} %bitcast.99), calls=%async_computation.7 | async-start | bytes 2621440 | tf_op jit(solution)/shard_map/all_to_all | solution.py:161
  316.5 2.4 broadcast_select_fusion
  318.8 16.4 %all-to-all-done.7 = bf16[16,256,160]{1,2,0:T(8,128)(2,1)} async-done(((bf16[16,256,160]{1,2,0:T(8,128)(2,1)}), bf16[16,256,160]{1,2,0:T(8,128)(2,1)}, u32[]{:S(2)}, u32[]{:S(2)}) %all-to-all-start.7) | async-done | bytes 1310752 | tf_op jit(solution)/shard_map/all_to_all | solution.py:161
  335.2 1.5 convert_reduce_fusion.1
  (78 shorter events, 12.3 us)
Async XLA Ops:
  0.6 233.4 %copy-start = (bf16[1,384,2560]{2,1,0:T(8,128)(2,1)S(1)}, bf16[1,384,2560]{2,1,0:T(8,128)(2,1)}, u32[]{:S(2)}) copy-start(bf16[1,384,2560]{2,1,0:T(8,128)(2,1)} %param.27) | copy-start | bytes 5898244
  1.8 25.5 %copy-start.11 = (f32[2560]{0:T(1024)S(1)}, f32[2560]{0:T(1024)}, u32[]{:S(2)}) copy-start(f32[2560]{0:T(1024)} %param.15) | copy-start | bytes 30724
  27.3 1.3 copy-start.4
  30.4 5.9 %copy-start.14 = (s32[1,64]{1,0:T(1,128)S(1)}, s32[1,64]{1,0:T(1,128)}, u32[]{:S(2)}) copy-start(s32[1,64]{1,0:T(1,128)} %param.19) | copy-start | bytes 772
  30.4 30.3 %all-to-all-start.1 = ((bf16[16,256,224]{1,2,0:T(8,128)(2,1)}), bf16[16,256,224]{1,2,0:T(8,128)(2,1)}, u32[]{:S(2)}, u32[]{:S(2)}) async-start(bf16[16,256,224]{1,2,0:T(8,128)(2,1)} %broadcast_in_dim.41), calls=%async_computation.1 | async-start | bytes 3670016 | tf_op jit(solution)/shard_map/all_to_all | solution.py:153
  66.2 1.0 slice-start
  69.3 2.8 copy-start.1
  110.0 22.2 %copy-start.7 = (bf16[2560,160]{0,1:T(8,128)(2,1)S(1)}, bf16[2560,160]{0,1:T(8,128)(2,1)}, u32[]{:S(2)}) copy-start(bf16[2560,160]{0,1:T(8,128)(2,1)} %param.17) | copy-start | bytes 2457604
  110.0 22.2 %copy-start.8 = (bf16[256,160]{0,1:T(8,128)(2,1)S(1)}, bf16[256,160]{0,1:T(8,128)(2,1)}, u32[]{:S(2)}) copy-start(bf16[256,160]{0,1:T(8,128)(2,1)} %param.14) | copy-start | bytes 245764
  133.9 4.8 %copy-start.10 = (s32[256,6]{0,1:T(8,128)S(1)}, s32[256,6]{0,1:T(8,128)}, u32[]{:S(2)}) copy-start(s32[256,6]{0,1:T(8,128)} %param.22) | copy-start | bytes 18436
  133.9 23.9 %copy-start.9 = (f32[2560]{0:T(1024)S(1)}, f32[2560]{0:T(1024)}, u32[]{:S(2)}) copy-start(f32[2560]{0:T(1024)} %param.21) | copy-start | bytes 30724
  134.0 23.6 %all-to-all-start.4 = ((bf16[16,256,160]{1,2,0:T(8,128)(2,1)}), bf16[16,256,160]{1,2,0:T(8,128)(2,1)S(1)}, u32[]{:S(2)}, u32[]{:S(2)}) async-start(bf16[16,256,160]{1,2,0:T(8,128)(2,1)} %broadcast_in_dim.46), calls=%async_computation.4 | async-start | bytes 2621440 | tf_op jit(solution)/shard_map/all_to_all | solution.py:153
  159.1 72.7 %copy-start.13 = (bf16[1,2560,768]{2,1,0:T(8,128)(2,1)S(1)}, bf16[1,2560,768]{2,1,0:T(8,128)(2,1)}, u32[]{:S(2)}) copy-start(bf16[1,2560,768]{2,1,0:T(8,128)(2,1)} %param.26) | copy-start | bytes 11796484
  237.1 4.9 %copy-start.12 = (f32[256,6]{0,1:T(8,128)S(1)}, f32[256,6]{0,1:T(8,128)}, u32[]{:S(2)}) copy-start(f32[256,6]{0,1:T(8,128)} %param.23) | copy-start | bytes 18436
  237.1 66.1 %all-to-all-start.6 = ((bf16[16,32,2560]{2,1,0:T(8,128)(2,1)}), bf16[16,32,2560]{2,1,0:T(8,128)(2,1)}, u32[]{:S(2)}, u32[]{:S(2)}) async-start(bf16[16,32,2560]{2,1,0:T(8,128)(2,1)} %bitcast.101), calls=%async_computation.6 | async-start | bytes 5242880 | tf_op jit(solution)/shard_map/all_to_all | solution.py:275
  242.0 1.5 copy-start.3
  306.1 1.0 copy-start.5
  306.1 1.3 copy-start.6
  309.5 7.0 %copy-start.2 = (bf16[512,1024]{1,0:T(8,128)(2,1)S(1)}, bf16[512,1024]{1,0:T(8,128)(2,1)}, u32[]{:S(2)}) copy-start(bf16[512,1024]{1,0:T(8,128)(2,1)} %copy-done.1) | copy-start | bytes 3145732
  309.5 25.7 %all-to-all-start.7 = ((bf16[16,256,160]{1,2,0:T(8,128)(2,1)}), bf16[16,256,160]{1,2,0:T(8,128)(2,1)}, u32[]{:S(2)}, u32[]{:S(2)}) async-start(bf16[16,256,160]{1,2,0:T(8,128)(2,1)} %bitcast.99), calls=%async_computation.7 | async-start | bytes 2621440 | tf_op jit(solution)/shard_map/all_to_all | solution.py:161

commit v11 on v10

--- a/solution.py
+++ b/solution.py
@@ -157,11 +157,11 @@
 def scatter_sum_blocks(values):
     count = lax.axis_size("blk")
     rows, width = values.shape
-    pieces = values.reshape(rows, count, width // count).transpose(1, 0, 2)
+    pieces = values.reshape(rows, count, width // count)
     received = lax.all_to_all(
-        pieces.astype(jnp.bfloat16), "blk", split_axis=0, concat_axis=0, tiled=True
-    )
-    return jnp.sum(received.astype(jnp.float32), axis=0)
+        pieces.astype(jnp.bfloat16), "blk", split_axis=1, concat_axis=1, tiled=True
+    )
+    return jnp.sum(received.astype(jnp.float32), axis=1)
 
 
 def per_device(
@@ -217,7 +217,15 @@
     local_pos = local_logical[:, None] * PAGE + slot_offsets[None, :]
     offset = local_pos - length
     written = (offset >= 0) & (offset < NEW)
-    picked = appended[jnp.clip(offset, 0, NEW - 1)]
+    padding = jnp.zeros((PAGE, 2 * key_width), appended.dtype)
+    padded = jnp.concatenate([padding, appended, padding], axis=0)
+    starts = jnp.clip(local_logical * PAGE - length + PAGE, 0, NEW + PAGE)
+    picked = jnp.stack(
+        [
+            lax.dynamic_slice_in_dim(padded, starts[page], PAGE, 0)
+            for page in range(local_pages)
+        ]
+    )
     pool_out = jnp.where(written[:, :, None], picked, kv_pool[0])
     half_dim = HEAD_DIM // 2
     frequency = rope_base ** (-(jnp.arange(half_dim).astype(jnp.float32) * 2.0 / HEAD_DIM))

time: 338 us -> 341 us (level)
  waiting for transfers between devices: 113 us -> 91.2 us
  local copies, waits for them, and re-layouts: 17.1 us -> 27.7 us
  between operations: 1.62 us -> 9.34 us
  other arithmetic: 17 us -> 23 us
    all_to_all x2, waiting for transfers between devices: 38.4 us -> 19.8 us  [gather_blocks(): lax.all_to_all(stacked, 'blk', split_axis=0, concat_axis=axis + 1, tiled=...]
    dynamic_slice x0 -> x5, local copies, waits for them, and re-layouts: none -> 6.29 us  [per_device(): lax.dynamic_slice_in_dim(padded, starts[page], PAGE, 0)]
    another operation x5 -> x6, other arithmetic: 1.95 us -> 6.37 us
    another operation x3, local copies, waits for them, and re-layouts: 0.12 us -> 3.75 us
  transfers between devices with their start and end apart: 4 -> 4, of which waited for: 4 -> 4; matrix products, arithmetic and copies ran while one was open for 3% -> 7% of each run, Pallas kernels for 0% -> 0%
where the time goes in v11:
time: 341 us; the launch traced here: 340 us
  blocking collectives  144 us (42%)
  waiting for transfers between devices  91.2 us (27%)
  local copies, waits for them, and re-layouts  27.7 us (8%)
  other arithmetic  23 us (7%)
  starting transfers between devices  21.5 us (6%)
  Pallas kernels  12.6 us (4%)
  matrix products  10.2 us (3%)
  between operations  9.34 us (3%)
    all_to_all x1, blocking collectives, per_device(): lax.all_to_all(outgoing, 'exp', split_axis=0, concat_axis=0, tiled=True)  72.6 us
    all_to_all x1, waiting for transfers between devices, per_device(): lax.all_to_all(result.reshape(received.shape), 'exp', split_axis=0, conca...  55.4 us
    all_to_all x2, blocking collectives, gather_blocks(): lax.all_to_all(stacked, 'blk', split_axis=0, concat_axis=axis + 1, tiled=...  47.2 us
    all_to_all x1, blocking collectives, per_device(): lax.all_to_all(payload, 'blk', split_axis=0, concat_axis=0, tiled=True)  24.3 us
    all_to_all x2, waiting for transfers between devices, gather_blocks(): lax.all_to_all(stacked, 'blk', split_axis=0, concat_axis=axis + 1, tiled=...  19.8 us
    all_to_all x1, waiting for transfers between devices, scatter_sum_blocks(): lax.all_to_all(pieces.astype(jnp.bfloat16), 'blk', split_axis=1, concat_a...  16 us
    all_to_all x2, starting transfers between devices, gather_blocks(): lax.all_to_all(stacked, 'blk', split_axis=0, concat_axis=axis + 1, tiled=...  9.87 us
    pallas_call x1, Pallas kernels, local_attention(): pl.pallas_call(attention_kernel, out_shape=jax.ShapeDtypeStruct((NEW, wid...  9.72 us
  transfers between devices with their start and end apart: 4, of which 4 were waited for; matrix products, arithmetic and copies ran while one was open for 7% of the time, Pallas kernels for 0%

profile of v11, /device:TPU:1, one launch (start us, length us, event | category | flops | bytes accessed | tf_op | source)
XLA Modules:
  0.0 339.7 jit_solution(7972104481582529238)
XLA Ops:
  1.8 25.1 %all_to_all.62 = bf16[16,256,160]{1,2,0:T(8,128)(2,1)S(1)} all-to-all(bf16[16,256,160]{1,2,0:T(8,128)(2,1)S(1)} %broadcast_in_dim.42), channel_id=1, replica_groups=mesh['blk'=16,'exp'=16] {'blk'}, dimensions={0} | all-to-all | bytes 2621440 | tf_op jit(solution)/shard_map/all_to_all | solution.py:153
  28.7 1.4 broadcast_in_dim.43
  30.1 5.3 %all-to-all-start.1 = ((bf16[16,256,224]{1,2,0:T(8,128)(2,1)}), bf16[16,256,224]{1,2,0:T(8,128)(2,1)}, u32[]{:S(2)}, u32[]{:S(2)}) async-start(bf16[16,256,224]{1,2,0:T(8,128)(2,1)} %broadcast_in_dim.43), calls=%async_computation.1 | async-start | bytes 3670016 | tf_op jit(solution)/shard_map/all_to_all | solution.py:153
  47.5 12.9 %all-to-all-done.1 = bf16[16,256,224]{1,2,0:T(8,128)(2,1)} async-done(((bf16[16,256,224]{1,2,0:T(8,128)(2,1)}), bf16[16,256,224]{1,2,0:T(8,128)(2,1)}, u32[]{:S(2)}, u32[]{:S(2)}) %all-to-all-start.1) | async-done | bytes 1835040 | tf_op jit(solution)/shard_map/all_to_all | solution.py:153
  61.5 3.8 %copy.71.proj_ref = bf16[256,3584]{1,0:T(8,128)(2,1)} copy(bf16[256,3584]{0,1:T(8,128)(2,1)} %bitcast.5) | data formatting | bytes 3670016 | tf_op jit(solution)/shard_map/reshape | solution.py:154
  65.6 1.3 constant_dynamic-slice_fusion.3
  68.3 1.9 copy.69
  70.2 1.8 copy.70
  73.1 1.3 bitcast_select_fusion.slot_ref
  74.5 9.7 %shard_map.149 = bf16[256,2688]{1,0:T(8,128)(2,1)} custom-call(bf16[256,3584]{1,0:T(8,128)(2,1)} %copy.71.proj_ref, f32[256,128]{1,0:T(8,128)} %get-tuple-element.19.cos_ref, f32[256,128]{1,0:T(8,128)} %get-tuple-element.20.sin_ref, bf16[512,1024]{1,0:T(8,128)(2,1)} %bitcast_select_fusion.slot_ref, s32[256,1]{1,0:T(8,128)} %iota_add_fusion.qpos_ref, ...), custom_call_target="tpu_custom_call" | custom-call | flops 1342177280 | bytes 4259840 | tf_op jit(solution)/shard_map/pallas_call | solution.py:99
  84.2 24.3 %all_to_all.63.part_ref = bf16[16,16,2688]{2,1,0:T(8,128)(2,1)} all-to-all(bf16[16,16,2688]{2,1,0:T(8,128)(2,1)} %bitcast.117), channel_id=1, replica_groups=mesh['blk'=16,'exp'=16] {'blk'}, dimensions={0} | all-to-all | bytes 2752512 | tf_op jit(solution)/shard_map/all_to_all | solution.py:241
  108.5 2.9 shard_map.150
  112.5 22.1 %all_to_all.64 = bf16[16,16,2560]{2,1,0:T(8,128)(2,1)S(1)} all-to-all(bf16[16,16,2560]{2,1,0:T(8,128)(2,1)S(1)} %broadcast_in_dim.48), channel_id=1, replica_groups=mesh['blk'=16,'exp'=16] {'blk'}, dimensions={0} | all-to-all | bytes 2621440 | tf_op jit(solution)/shard_map/all_to_all | solution.py:153
  137.0 4.6 %all-to-all-start.4 = ((bf16[16,256,160]{1,2,0:T(8,128)(2,1)}), bf16[16,256,160]{1,2,0:T(8,128)(2,1)S(1)}, u32[]{:S(2)}, u32[]{:S(2)}) async-start(bf16[16,256,160]{1,2,0:T(8,128)(2,1)} %broadcast_in_dim.49), calls=%async_computation.4 | async-start | bytes 2621440 | tf_op jit(solution)/shard_map/all_to_all | solution.py:153
  143.6 1.3 reshape.267
  144.9 2.3 reduce-window.6
  147.8 1.3 copy.72
  151.5 1.3 copy.73
  153.5 6.9 %all-to-all-done.4 = bf16[16,256,160]{1,2,0:T(8,128)(2,1)S(1)} async-done(((bf16[16,256,160]{1,2,0:T(8,128)(2,1)}), bf16[16,256,160]{1,2,0:T(8,128)(2,1)S(1)}, u32[]{:S(2)}, u32[]{:S(2)}) %all-to-all-start.4) | async-done | bytes 1310752 | tf_op jit(solution)/shard_map/all_to_all | solution.py:153
  162.1 72.6 %all_to_all.65 = bf16[16,32,2560]{2,1,0:T(8,128)(2,1)S(1)} all-to-all(bf16[16,32,2560]{2,1,0:T(8,128)(2,1)S(1)} %bitcast.102), channel_id=1, replica_groups=mesh['blk'=16,'exp'=16] {'exp'}, dimensions={0} | all-to-all | bytes 5242880 | tf_op jit(solution)/shard_map/all_to_all | solution.py:276
  234.8 2.2 fusion.1
  237.0 3.1 convolution_convert_fusion
  240.0 4.7 %all-to-all-start.6 = ((bf16[16,32,2560]{2,1,0:T(8,128)(2,1)}), bf16[16,32,2560]{2,1,0:T(8,128)(2,1)}, u32[]{:S(2)}, u32[]{:S(2)}) async-start(bf16[16,32,2560]{2,1,0:T(8,128)(2,1)} %bitcast.106), calls=%async_computation.6 | async-start | bytes 5242880 | tf_op jit(solution)/shard_map/all_to_all | solution.py:283
  246.5 1.4 select_reduce_fusion
  249.0 1.6 fusion.35
  250.6 55.4 %all-to-all-done.6 = bf16[16,32,2560]{2,1,0:T(8,128)(2,1)} async-done(((bf16[16,32,2560]{2,1,0:T(8,128)(2,1)}), bf16[16,32,2560]{2,1,0:T(8,128)(2,1)}, u32[]{:S(2)}, u32[]{:S(2)}) %all-to-all-start.6) | async-done | bytes 2621472 | tf_op jit(solution)/shard_map/all_to_all | solution.py:283
  306.0 2.3 convert_reduce_fusion
  310.9 1.4 copy.75
  312.3 6.9 %all-to-all-start.7 = ((bf16[256,16,160]{0,2,1:T(8,128)(2,1)}), bf16[256,16,160]{0,2,1:T(8,128)(2,1)S(1)}, u32[]{:S(2)}, u32[]{:S(2)}) async-start(bf16[256,16,160]{0,2,1:T(8,128)(2,1)} %bitcast.104), calls=%async_computation.7 | async-start | bytes 2621440 | tf_op jit(solution)/shard_map/all_to_all | solution.py:161
  319.3 2.6 maximum_select_fusion
  321.9 16.0 %all-to-all-done.7 = bf16[256,16,160]{0,2,1:T(8,128)(2,1)S(1)} async-done(((bf16[256,16,160]{0,2,1:T(8,128)(2,1)}), bf16[256,16,160]{0,2,1:T(8,128)(2,1)S(1)}, u32[]{:S(2)}, u32[]{:S(2)}) %all-to-all-start.7) | async-done | bytes 1310752 | tf_op jit(solution)/shard_map/all_to_all | solution.py:161
  338.1 1.5 add_convert_fusion.1
  (98 shorter events, 27.1 us)
Async XLA Ops:
  0.6 236.4 %copy-start = (bf16[1,384,2560]{2,1,0:T(8,128)(2,1)S(1)}, bf16[1,384,2560]{2,1,0:T(8,128)(2,1)}, u32[]{:S(2)}) copy-start(bf16[1,384,2560]{2,1,0:T(8,128)(2,1)} %param.27) | copy-start | bytes 5898244
  1.8 25.5 %copy-start.16 = (f32[2560]{0:T(1024)S(1)}, f32[2560]{0:T(1024)}, u32[]{:S(2)}) copy-start(f32[2560]{0:T(1024)} %param.15) | copy-start | bytes 30724
  26.9 1.3 copy-start.4
  30.1 5.9 %copy-start.23 = (s32[1,64]{1,0:T(1,128)S(1)}, s32[1,64]{1,0:T(1,128)}, u32[]{:S(2)}) copy-start(s32[1,64]{1,0:T(1,128)} %param.19) | copy-start | bytes 772
  30.1 30.3 %all-to-all-start.1 = ((bf16[16,256,224]{1,2,0:T(8,128)(2,1)}), bf16[16,256,224]{1,2,0:T(8,128)(2,1)}, u32[]{:S(2)}, u32[]{:S(2)}) async-start(bf16[16,256,224]{1,2,0:T(8,128)(2,1)} %broadcast_in_dim.43), calls=%async_computation.1 | async-start | bytes 3670016 | tf_op jit(solution)/shard_map/all_to_all | solution.py:153
  36.2 24.2 %copy-start.19 = (s32[4]{0:T(128)}, s32[4]{0:T(128)S(1)}, u32[]{:S(2)}) copy-start(s32[4]{0:T(128)S(1)} %get-tuple-element.3) | copy-start | bytes 52
  67.1 6.1 %copy-start.1 = (bf16[1,4,128,1024]{3,2,1,0:T(8,128)(2,1)S(1)}, bf16[1,4,128,1024]{3,2,1,0:T(8,128)(2,1)}, u32[]{:S(2)}) copy-start(bf16[1,4,128,1024]{3,2,1,0:T(8,128)(2,1)} %param.18) | copy-start | bytes 3145732
  68.3 6.2 %copy-start.2 = (bf16[128,1024]{1,0:T(8,128)(2,1)}, bf16[128,1024]{1,0:T(8,128)(2,1)S(1)}, u32[]{:S(2)}) copy-start(bf16[128,1024]{1,0:T(8,128)(2,1)S(1)} %copy.68) | copy-start | bytes 786436
  111.4 23.2 %copy-start.7 = (bf16[2560,160]{0,1:T(8,128)(2,1)S(1)}, bf16[2560,160]{0,1:T(8,128)(2,1)}, u32[]{:S(2)}) copy-start(bf16[2560,160]{0,1:T(8,128)(2,1)} %param.17) | copy-start | bytes 2457604
  111.4 23.2 %copy-start.9 = (bf16[256,160]{0,1:T(8,128)(2,1)S(1)}, bf16[256,160]{0,1:T(8,128)(2,1)}, u32[]{:S(2)}) copy-start(bf16[256,160]{0,1:T(8,128)(2,1)} %param.14) | copy-start | bytes 245764
  135.1 0.6 copy-start.8
  137.0 23.8 %copy-start.12 = (f32[2560]{0:T(1024)S(1)}, f32[2560]{0:T(1024)}, u32[]{:S(2)}) copy-start(f32[2560]{0:T(1024)} %param.21) | copy-start | bytes 30724
  137.0 23.4 %all-to-all-start.4 = ((bf16[16,256,160]{1,2,0:T(8,128)(2,1)}), bf16[16,256,160]{1,2,0:T(8,128)(2,1)S(1)}, u32[]{:S(2)}, u32[]{:S(2)}) async-start(bf16[16,256,160]{1,2,0:T(8,128)(2,1)} %broadcast_in_dim.49), calls=%async_computation.4 | async-start | bytes 2621440 | tf_op jit(solution)/shard_map/all_to_all | solution.py:153
  141.6 0.6 copy-start.21
  143.0 0.6 copy-start.13
  153.5 7.7 %copy-start.10 = (s32[1,4,2,128]{3,1,2,0:T(4,128)}, s32[1,4,2,128]{3,1,2,0:T(4,128)S(1)}, u32[]{:S(2)}) copy-start(s32[1,4,2,128]{3,1,2,0:T(4,128)S(1)} %copy.84) | copy-start | bytes 12292
  160.3 1.0 copy-start.14
  160.7 0.6 copy-start.17
  162.1 72.7 %copy-start.22 = (bf16[1,2560,768]{2,1,0:T(8,128)(2,1)S(1)}, bf16[1,2560,768]{2,1,0:T(8,128)(2,1)}, u32[]{:S(2)}) copy-start(bf16[1,2560,768]{2,1,0:T(8,128)(2,1)} %param.26) | copy-start | bytes 11796484
  240.0 66.0 %all-to-all-start.6 = ((bf16[16,32,2560]{2,1,0:T(8,128)(2,1)}), bf16[16,32,2560]{2,1,0:T(8,128)(2,1)}, u32[]{:S(2)}, u32[]{:S(2)}) async-start(bf16[16,32,2560]{2,1,0:T(8,128)(2,1)} %bitcast.106), calls=%async_computation.6 | async-start | bytes 5242880 | tf_op jit(solution)/shard_map/all_to_all | solution.py:283
  245.6 3.4 %copy-start.3 = (bf16[2560,2,192]{0,2,1:T(8,128)(2,1)S(1)}, bf16[2560,2,192]{0,2,1:T(8,128)(2,1)}, u32[]{:S(2)}) copy-start(bf16[2560,2,192]{0,2,1:T(8,128)(2,1)} %param.24) | copy-start | bytes 5898244
  250.6 57.7 %copy-start.11 = (s32[1,4,2,128]{3,1,2,0:T(4,128)S(1)}, s32[1,4,2,128]{3,1,2,0:T(4,128)}, u32[]{:S(2)}) copy-start(s32[1,4,2,128]{3,1,2,0:T(4,128)} %copy-done.10) | copy-start | bytes 12292
  250.6 57.8 %copy-start.15 = (pred[256,4]{0,1:T(4,128)(4,1)S(1)}, pred[256,4]{0,1:T(4,128)(4,1)}, u32[]{:S(2)}) copy-start(pred[256,4]{0,1:T(4,128)(4,1)} %copy-done.13) | copy-start | bytes 3076
  250.6 57.8 %copy-start.18 = (f32[4,32]{1,0:T(4,128)S(1)}, f32[4,32]{1,0:T(4,128)}, u32[]{:S(2)}) copy-start(f32[4,32]{1,0:T(4,128)} %select_reduce_fusion) | copy-start | bytes 1540
  309.0 1.0 copy-start.5
  309.0 1.3 copy-start.6
  312.3 6.9 %copy-start.20 = (s32[4]{0:T(128)S(1)}, s32[4]{0:T(128)}, u32[]{:S(2)}) copy-start(s32[4]{0:T(128)} %copy-done.19) | copy-start | bytes 52
  312.3 25.6 %all-to-all-start.7 = ((bf16[256,16,160]{0,2,1:T(8,128)(2,1)}), bf16[256,16,160]{0,2,1:T(8,128)(2,1)S(1)}, u32[]{:S(2)}, u32[]{:S(2)}) async-start(bf16[256,16,160]{0,2,1:T(8,128)(2,1)} %bitcast.104), calls=%async_computation.7 | async-start | bytes 2621440 | tf_op jit(solution)/shard_map/all_to_all | solution.py:161

commit v12 on v10

--- a/solution.py
+++ b/solution.py
@@ -266,6 +266,8 @@
     ).astype(jnp.bfloat16)
     outgoing = jnp.repeat(outgoing, SPLIT, axis=0)
     received = lax.all_to_all(outgoing, "exp", split_axis=0, concat_axis=0, tiled=True)
+    slot_weight = jnp.sum(placed.astype(jnp.float32) * route_share.T[:, None, :], axis=2)
+    received, slot_weight = lax.optimization_barrier((received, slot_weight))
     flat_rows = received.reshape(-1, model_width)
     expert_gu = jnp.dot(flat_rows, expert_gate_up[0], preferred_element_type=jnp.float32)
     activated = (jax.nn.silu(expert_gu[:, :FF_PART]) * expert_gu[:, FF_PART:]).astype(jnp.bfloat16)
@@ -278,7 +280,6 @@
     summed = jnp.sum(
         returned.reshape(row_experts, SPLIT, capacity, model_width).astype(jnp.float32), axis=1
     )
-    slot_weight = jnp.sum(placed.astype(jnp.float32) * route_share.T[:, None, :], axis=2)
     slot_values = summed * slot_weight[:, :, None]
     upper_part = slot_values.astype(jnp.bfloat16)
     lower_part = (slot_values - upper_part.astype(jnp.float32)).astype(jnp.bfloat16)

time: 338 us -> 343 us (1.015)
  blocking collectives: 144 us -> 71.6 us
  waiting for transfers between devices: 113 us -> 174 us
  starting transfers between devices: 21.9 us -> 32.9 us
    all_to_all x1 -> x0, blocking collectives: 72.6 us -> none  [per_device(): lax.all_to_all(outgoing, 'exp', split_axis=0, concat_axis=0, tiled=True)]
    all_to_all x0 -> x1, waiting for transfers between devices: none -> 61.5 us  [per_device(): lax.all_to_all(outgoing, 'exp', split_axis=0, concat_axis=0, tiled=True)]
    all_to_all x0 -> x1, starting transfers between devices: none -> 10.6 us  [per_device(): lax.all_to_all(outgoing, 'exp', split_axis=0, concat_axis=0, tiled=True)]
  transfers between devices with their start and end apart: 4 -> 5, of which waited for: 4 -> 5; matrix products, arithmetic and copies ran while one was open for 3% -> 3% of each run, Pallas kernels for 0% -> 0%
where the time goes in v12:
time: 343 us; the launch traced here: 342 us
  waiting for transfers between devices  174 us (51%)
  blocking collectives  71.6 us (21%)
  starting transfers between devices  32.9 us (10%)
  local copies, waits for them, and re-layouts  18.7 us (5%)
  other arithmetic  17 us (5%)
  matrix products  13.1 us (4%)
  Pallas kernels  12.6 us (4%)
    all_to_all x1, waiting for transfers between devices, per_device(): lax.all_to_all(outgoing, 'exp', split_axis=0, concat_axis=0, tiled=True)  61.5 us
    all_to_all x1, waiting for transfers between devices, per_device(): lax.all_to_all(result.reshape(received.shape), 'exp', split_axis=0, conca...  58.1 us
    all_to_all x2, blocking collectives, gather_blocks(): lax.all_to_all(stacked, 'blk', split_axis=0, concat_axis=axis + 1, tiled=...  47.3 us
    all_to_all x2, waiting for transfers between devices, gather_blocks(): lax.all_to_all(stacked, 'blk', split_axis=0, concat_axis=axis + 1, tiled=...  38.4 us
    all_to_all x1, blocking collectives, per_device(): lax.all_to_all(payload, 'blk', split_axis=0, concat_axis=0, tiled=True)  24.3 us
    all_to_all x1, waiting for transfers between devices, scatter_sum_blocks(): lax.all_to_all(pieces.astype(jnp.bfloat16), 'blk', split_axis=0, concat_a...  16.4 us
    all_to_all x1, starting transfers between devices, per_device(): lax.all_to_all(outgoing, 'exp', split_axis=0, concat_axis=0, tiled=True)  10.6 us
    all_to_all x2, starting transfers between devices, gather_blocks(): lax.all_to_all(stacked, 'blk', split_axis=0, concat_axis=axis + 1, tiled=...  10.1 us
  transfers between devices with their start and end apart: 5, of which 5 were waited for; matrix products, arithmetic and copies ran while one was open for 3% of the time, Pallas kernels for 0%

profile of v12, /device:TPU:1, one launch (start us, length us, event | category | flops | bytes accessed | tf_op | source)
XLA Modules:
  0.0 341.9 jit_solution(16768915161580497821)
XLA Ops:
  0.6 1.1 broadcast_in_dim.40
  1.8 25.1 %all_to_all.62 = bf16[16,256,160]{1,2,0:T(8,128)(2,1)S(1)} all-to-all(bf16[16,256,160]{1,2,0:T(8,128)(2,1)S(1)} %broadcast_in_dim.40), channel_id=1, replica_groups=mesh['blk'=16,'exp'=16] {'blk'}, dimensions={0} | all-to-all | bytes 2621440 | tf_op jit(solution)/shard_map/all_to_all | solution.py:153
  29.0 1.4 broadcast_in_dim.41
  30.4 5.3 %all-to-all-start.1 = ((bf16[16,256,224]{1,2,0:T(8,128)(2,1)}), bf16[16,256,224]{1,2,0:T(8,128)(2,1)}, u32[]{:S(2)}, u32[]{:S(2)}) async-start(bf16[16,256,224]{1,2,0:T(8,128)(2,1)} %broadcast_in_dim.41), calls=%async_computation.1 | async-start | bytes 3670016 | tf_op jit(solution)/shard_map/all_to_all | solution.py:153
  39.4 21.4 %all-to-all-done.1 = bf16[16,256,224]{1,2,0:T(8,128)(2,1)} async-done(((bf16[16,256,224]{1,2,0:T(8,128)(2,1)}), bf16[16,256,224]{1,2,0:T(8,128)(2,1)}, u32[]{:S(2)}, u32[]{:S(2)}) %all-to-all-start.1) | async-done | bytes 1835040 | tf_op jit(solution)/shard_map/all_to_all | solution.py:153
  61.7 3.9 %copy.36.proj_ref = bf16[256,3584]{1,0:T(8,128)(2,1)} copy(bf16[256,3584]{0,1:T(8,128)(2,1)} %bitcast.5) | data formatting | bytes 3670016 | tf_op jit(solution)/shard_map/reshape | solution.py:154
  67.1 2.1 gather_fusion
  69.2 2.7 bitcast_select_fusion.slot_ref
  72.0 9.7 %shard_map.149 = bf16[256,2688]{1,0:T(8,128)(2,1)} custom-call(bf16[256,3584]{1,0:T(8,128)(2,1)} %copy.36.proj_ref, f32[256,128]{1,0:T(8,128)} %get-tuple-element.13.cos_ref, f32[256,128]{1,0:T(8,128)} %get-tuple-element.14.sin_ref, bf16[512,1024]{1,0:T(8,128)(2,1)} %bitcast_select_fusion.slot_ref, s32[256,1]{1,0:T(8,128)} %iota_add_fusion.qpos_ref, ...), custom_call_target="tpu_custom_call" | custom-call | flops 1342177280 | bytes 4259840 | tf_op jit(solution)/shard_map/pallas_call | solution.py:99
  81.7 24.3 %all_to_all.63.part_ref = bf16[16,16,2688]{2,1,0:T(8,128)(2,1)} all-to-all(bf16[16,16,2688]{2,1,0:T(8,128)(2,1)} %bitcast.104), channel_id=1, replica_groups=mesh['blk'=16,'exp'=16] {'blk'}, dimensions={0} | all-to-all | bytes 2752512 | tf_op jit(solution)/shard_map/all_to_all | solution.py:233
  106.0 2.9 shard_map.150
  108.9 1.0 broadcast_in_dim.45
  109.9 22.2 %all_to_all.64 = bf16[16,16,2560]{2,1,0:T(8,128)(2,1)S(1)} all-to-all(bf16[16,16,2560]{2,1,0:T(8,128)(2,1)S(1)} %broadcast_in_dim.45), channel_id=1, replica_groups=mesh['blk'=16,'exp'=16] {'blk'}, dimensions={0} | all-to-all | bytes 2621440 | tf_op jit(solution)/shard_map/all_to_all | solution.py:153
  132.7 1.2 broadcast_in_dim.46
  133.9 4.8 %all-to-all-start.4 = ((bf16[16,256,160]{1,2,0:T(8,128)(2,1)}), bf16[16,256,160]{1,2,0:T(8,128)(2,1)S(1)}, u32[]{:S(2)}, u32[]{:S(2)}) async-start(bf16[16,256,160]{1,2,0:T(8,128)(2,1)} %broadcast_in_dim.46), calls=%async_computation.4 | async-start | bytes 2621440 | tf_op jit(solution)/shard_map/all_to_all | solution.py:153
  138.8 1.2 reduce-window.6
  140.5 17.0 %all-to-all-done.4 = bf16[16,256,160]{1,2,0:T(8,128)(2,1)S(1)} async-done(((bf16[16,256,160]{1,2,0:T(8,128)(2,1)}), bf16[16,256,160]{1,2,0:T(8,128)(2,1)S(1)}, u32[]{:S(2)}, u32[]{:S(2)}) %all-to-all-start.4) | async-done | bytes 1310752 | tf_op jit(solution)/shard_map/all_to_all | solution.py:153
  158.8 1.8 broadcast_in_dim.47
  160.6 10.6 %all-to-all-start.5 = ((bf16[16,32,2560]{2,1,0:T(8,128)(2,1)}), bf16[16,32,2560]{2,1,0:T(8,128)(2,1)}, u32[]{:S(2)}, u32[]{:S(2)}) async-start(bf16[16,32,2560]{2,1,0:T(8,128)(2,1)} %bitcast.96), calls=%async_computation.5 | async-start | bytes 5242880 | tf_op jit(solution)/shard_map/all_to_all | solution.py:268
  171.5 61.5 %all-to-all-done.5 = bf16[16,32,2560]{2,1,0:T(8,128)(2,1)} async-done(((bf16[16,32,2560]{2,1,0:T(8,128)(2,1)}), bf16[16,32,2560]{2,1,0:T(8,128)(2,1)}, u32[]{:S(2)}, u32[]{:S(2)}) %all-to-all-start.5) | async-done | bytes 2621472 | tf_op jit(solution)/shard_map/all_to_all | solution.py:268
  232.9 5.1 %fusion.1 = f32[512,768]{1,0:T(8,128)S(1)} fusion(bf16[512,2560]{1,0:T(8,128)(2,1)} %bitcast.30, bf16[1,2560,768]{2,1,0:T(8,128)(2,1)} %param.26), kind=kOutput, calls=%fused_computation.7 | convolution fusion | flops 2013265920 | bytes 8126464 | tf_op jit(solution)/shard_map/dot_general | solution.py:272
  238.0 3.1 convolution_convert_fusion
  241.1 5.3 %all-to-all-start.6 = ((bf16[16,32,2560]{2,1,0:T(8,128)(2,1)}), bf16[16,32,2560]{2,1,0:T(8,128)(2,1)}, u32[]{:S(2)}, u32[]{:S(2)}) async-start(bf16[16,32,2560]{2,1,0:T(8,128)(2,1)} %bitcast.101), calls=%async_computation.6 | async-start | bytes 5242880 | tf_op jit(solution)/shard_map/all_to_all | solution.py:277
  246.9 1.1 copy-done.3
  248.1 1.6 fusion.35
  249.7 58.1 %all-to-all-done.6 = bf16[16,32,2560]{2,1,0:T(8,128)(2,1)} async-done(((bf16[16,32,2560]{2,1,0:T(8,128)(2,1)}), bf16[16,32,2560]{2,1,0:T(8,128)(2,1)}, u32[]{:S(2)}, u32[]{:S(2)}) %all-to-all-start.6) | async-done | bytes 2621472 | tf_op jit(solution)/shard_map/all_to_all | solution.py:277
  307.8 2.3 convert_reduce_fusion
  312.6 1.4 copy.40
  314.0 6.9 %all-to-all-start.7 = ((bf16[16,256,160]{1,2,0:T(8,128)(2,1)}), bf16[16,256,160]{1,2,0:T(8,128)(2,1)}, u32[]{:S(2)}, u32[]{:S(2)}) async-start(bf16[16,256,160]{1,2,0:T(8,128)(2,1)} %bitcast.99), calls=%async_computation.7 | async-start | bytes 2621440 | tf_op jit(solution)/shard_map/all_to_all | solution.py:161
  321.0 2.4 broadcast_select_fusion
  323.3 16.4 %all-to-all-done.7 = bf16[16,256,160]{1,2,0:T(8,128)(2,1)} async-done(((bf16[16,256,160]{1,2,0:T(8,128)(2,1)}), bf16[16,256,160]{1,2,0:T(8,128)(2,1)}, u32[]{:S(2)}, u32[]{:S(2)}) %all-to-all-start.7) | async-done | bytes 1310752 | tf_op jit(solution)/shard_map/all_to_all | solution.py:161
  339.8 1.5 convert_reduce_fusion.1
  (77 shorter events, 13.9 us)
Async XLA Ops:
  0.6 237.4 %copy-start = (bf16[1,384,2560]{2,1,0:T(8,128)(2,1)S(1)}, bf16[1,384,2560]{2,1,0:T(8,128)(2,1)}, u32[]{:S(2)}) copy-start(bf16[1,384,2560]{2,1,0:T(8,128)(2,1)} %param.27) | copy-start | bytes 5898244
  1.8 25.5 %copy-start.11 = (f32[2560]{0:T(1024)S(1)}, f32[2560]{0:T(1024)}, u32[]{:S(2)}) copy-start(f32[2560]{0:T(1024)} %param.15) | copy-start | bytes 30724
  27.3 1.3 copy-start.4
  30.4 5.9 %copy-start.13 = (s32[1,64]{1,0:T(1,128)S(1)}, s32[1,64]{1,0:T(1,128)}, u32[]{:S(2)}) copy-start(s32[1,64]{1,0:T(1,128)} %param.19) | copy-start | bytes 772
  30.4 30.3 %all-to-all-start.1 = ((bf16[16,256,224]{1,2,0:T(8,128)(2,1)}), bf16[16,256,224]{1,2,0:T(8,128)(2,1)}, u32[]{:S(2)}, u32[]{:S(2)}) async-start(bf16[16,256,224]{1,2,0:T(8,128)(2,1)} %broadcast_in_dim.41), calls=%async_computation.1 | async-start | bytes 3670016 | tf_op jit(solution)/shard_map/all_to_all | solution.py:153
  66.1 1.0 slice-start
  69.2 2.8 copy-start.1
  109.9 22.2 %copy-start.7 = (bf16[2560,160]{0,1:T(8,128)(2,1)S(1)}, bf16[2560,160]{0,1:T(8,128)(2,1)}, u32[]{:S(2)}) copy-start(bf16[2560,160]{0,1:T(8,128)(2,1)} %param.17) | copy-start | bytes 2457604
  109.9 22.2 %copy-start.8 = (bf16[256,160]{0,1:T(8,128)(2,1)S(1)}, bf16[256,160]{0,1:T(8,128)(2,1)}, u32[]{:S(2)}) copy-start(bf16[256,160]{0,1:T(8,128)(2,1)} %param.14) | copy-start | bytes 245764
  133.9 4.8 %copy-start.10 = (s32[256,6]{0,1:T(8,128)S(1)}, s32[256,6]{0,1:T(8,128)}, u32[]{:S(2)}) copy-start(s32[256,6]{0,1:T(8,128)} %param.22) | copy-start | bytes 18436
  133.9 23.9 %copy-start.9 = (f32[2560]{0:T(1024)S(1)}, f32[2560]{0:T(1024)}, u32[]{:S(2)}) copy-start(f32[2560]{0:T(1024)} %param.21) | copy-start | bytes 30724
  133.9 23.5 %all-to-all-start.4 = ((bf16[16,256,160]{1,2,0:T(8,128)(2,1)}), bf16[16,256,160]{1,2,0:T(8,128)(2,1)S(1)}, u32[]{:S(2)}, u32[]{:S(2)}) async-start(bf16[16,256,160]{1,2,0:T(8,128)(2,1)} %broadcast_in_dim.46), calls=%async_computation.4 | async-start | bytes 2621440 | tf_op jit(solution)/shard_map/all_to_all | solution.py:153
  160.6 10.6 %copy-start.12 = (f32[256,6]{0,1:T(8,128)S(1)}, f32[256,6]{0,1:T(8,128)}, u32[]{:S(2)}) copy-start(f32[256,6]{0,1:T(8,128)} %param.23) | copy-start | bytes 18436
  160.6 72.3 %all-to-all-start.5 = ((bf16[16,32,2560]{2,1,0:T(8,128)(2,1)}), bf16[16,32,2560]{2,1,0:T(8,128)(2,1)}, u32[]{:S(2)}, u32[]{:S(2)}) async-start(bf16[16,32,2560]{2,1,0:T(8,128)(2,1)} %bitcast.96), calls=%async_computation.5 | async-start | bytes 5242880 | tf_op jit(solution)/shard_map/all_to_all | solution.py:268
  241.1 66.6 %all-to-all-start.6 = ((bf16[16,32,2560]{2,1,0:T(8,128)(2,1)}), bf16[16,32,2560]{2,1,0:T(8,128)(2,1)}, u32[]{:S(2)}, u32[]{:S(2)}) async-start(bf16[16,32,2560]{2,1,0:T(8,128)(2,1)} %bitcast.101), calls=%async_computation.6 | async-start | bytes 5242880 | tf_op jit(solution)/shard_map/all_to_all | solution.py:277
  246.5 1.5 copy-start.3
  310.7 1.0 copy-start.5
  310.7 1.3 copy-start.6
  314.0 7.0 %copy-start.2 = (bf16[512,1024]{1,0:T(8,128)(2,1)S(1)}, bf16[512,1024]{1,0:T(8,128)(2,1)}, u32[]{:S(2)}) copy-start(bf16[512,1024]{1,0:T(8,128)(2,1)} %copy-done.1) | copy-start | bytes 3145732
  314.0 25.7 %all-to-all-start.7 = ((bf16[16,256,160]{1,2,0:T(8,128)(2,1)}), bf16[16,256,160]{1,2,0:T(8,128)(2,1)}, u32[]{:S(2)}, u32[]{:S(2)}) async-start(bf16[16,256,160]{1,2,0:T(8,128)(2,1)} %bitcast.99), calls=%async_computation.7 | async-start | bytes 2621440 | tf_op jit(solution)/shard_map/all_to_all | solution.py:161

commit v13 on v10

--- a/solution.py
+++ b/solution.py
@@ -52,7 +52,15 @@
     return [high, middle, low]
 
 
-def attention_kernel(proj_ref, cos_ref, sin_ref, slot_ref, qpos_ref, kpos_ref, out_ref):
+def attention_kernel(
+    proj_ref, cos_ref, sin_ref, cache_ref, fresh_ref, offset_ref, qpos_ref, kpos_ref, out_ref, slot_ref
+):
+    offsets = offset_ref[...]
+    columns = lax.broadcasted_iota(jnp.int32, (offsets.shape[0], NEW), 1)
+    chooser = jnp.where(offsets == columns, 1.0, 0.0).astype(jnp.bfloat16)
+    picked = jnp.dot(chooser, fresh_ref[...], preferred_element_type=jnp.float32)
+    written = (offsets >= 0) & (offsets < NEW)
+    slot_ref[...] = jnp.where(written, picked.astype(slot_ref.dtype), cache_ref[...])
     key_width = KV_HEADS * HEAD_DIM
     group_size = HEADS // KV_HEADS
     allowed = kpos_ref[...] <= qpos_ref[...]
@@ -94,19 +102,31 @@
     out_ref[:, HEADS * HEAD_DIM :] = stats.astype(out_ref.dtype)
 
 
-def local_attention(projected_all, cosine, sine_signed, slot_rows, positions, key_pos):
+def local_attention(projected_all, cosine, sine_signed, cache_rows, fresh, offsets, positions, key_pos):
     width = HEADS * HEAD_DIM + 128
     return pl.pallas_call(
         attention_kernel,
-        out_shape=jax.ShapeDtypeStruct((NEW, width), jnp.bfloat16),
-        in_specs=[pl.BlockSpec(memory_space=pltpu.VMEM)] * 6,
-        out_specs=pl.BlockSpec(memory_space=pltpu.VMEM),
+        out_shape=(
+            jax.ShapeDtypeStruct((NEW, width), jnp.bfloat16),
+            jax.ShapeDtypeStruct(cache_rows.shape, cache_rows.dtype),
+        ),
+        in_specs=[pl.BlockSpec(memory_space=pltpu.VMEM)] * 8,
+        out_specs=(pl.BlockSpec(memory_space=pltpu.VMEM), pl.BlockSpec(memory_space=pltpu.VMEM)),
         cost_estimate=pl.CostEstimate(
-            flops=4 * NEW * slot_rows.shape[0] * HEAD_DIM * HEADS,
-            transcendentals=NEW * slot_rows.shape[0] * HEADS,
-            bytes_accessed=NEW * width * 2 + slot_rows.size * 2 + projected_all.size * 2,
+            flops=4 * NEW * cache_rows.shape[0] * HEAD_DIM * HEADS,
+            transcendentals=NEW * cache_rows.shape[0] * HEADS,
+            bytes_accessed=NEW * width * 2 + cache_rows.size * 4 + projected_all.size * 2,
         ),
-    )(projected_all, cosine, sine_signed, slot_rows, positions[:, None], key_pos[None, :])
+    )(
+        projected_all,
+        cosine,
+        sine_signed,
+        cache_rows,
+        fresh,
+        offsets[:, None],
+        positions[:, None],
+        key_pos[None, :],
+    )
 
 
 def combine_kernel(part_ref, out_ref):
@@ -217,8 +237,6 @@
     local_pos = local_logical[:, None] * PAGE + slot_offsets[None, :]
     offset = local_pos - length
     written = (offset >= 0) & (offset < NEW)
-    picked = appended[jnp.clip(offset, 0, NEW - 1)]
-    pool_out = jnp.where(written[:, :, None], picked, kv_pool[0])
     half_dim = HEAD_DIM // 2
     frequency = rope_base ** (-(jnp.arange(half_dim).astype(jnp.float32) * 2.0 / HEAD_DIM))
     angles = positions.astype(jnp.float32)[:, None] * frequency[None, :]
@@ -226,10 +244,18 @@
     sine_vals = jnp.sin(angles)
     cosine_full = jnp.concatenate([cosine, cosine], axis=1)
     sine_signed = jnp.concatenate([-sine_vals, sine_vals], axis=1)
-    slot_rows = pool_out.reshape(local_pages * PAGE, 2 * key_width)
-    payload = local_attention(
-        projected_all, cosine_full, sine_signed, slot_rows, positions, local_pos.reshape(-1)
-    ).reshape(blocks, own_rows, query_width + 128)
+    payload, slot_rows = local_attention(
+        projected_all,
+        cosine_full,
+        sine_signed,
+        kv_pool[0].reshape(local_pages * PAGE, 2 * key_width),
+        appended,
+        offset.reshape(-1),
+        positions,
+        local_pos.reshape(-1),
+    )
+    pool_out = slot_rows.reshape(local_pages, PAGE, 2 * key_width)
+    payload = payload.reshape(blocks, own_rows, query_width + 128)
     gathered = lax.all_to_all(payload, "blk", split_axis=0, concat_axis=0, tiled=True)
     own_attention = combine_attention(gathered)
     attended = jnp.dot(

time: 338 us -> 335 us (level)
  blocking collectives: 144 us -> 169 us
  waiting for transfers between devices: 113 us -> 95.6 us
  starting transfers between devices: 21.9 us -> 14.7 us
  other arithmetic: 17 us -> 11.2 us
    all_to_all x0 -> x1, blocking collectives: none -> 25.2 us  [scatter_sum_blocks(): lax.all_to_all(pieces.astype(jnp.bfloat16), 'blk', split_axis=0, concat_a...]
    all_to_all x1 -> x0, waiting for transfers between devices: 16.4 us -> none  [scatter_sum_blocks(): lax.all_to_all(pieces.astype(jnp.bfloat16), 'blk', split_axis=0, concat_a...]
    all_to_all x1 -> x0, starting transfers between devices: 6.94 us -> none  [scatter_sum_blocks(): lax.all_to_all(pieces.astype(jnp.bfloat16), 'blk', split_axis=0, concat_a...]
    select_n x3 -> x0, other arithmetic: 5.19 us -> none  [the longest x2 5.12 us: per_device(): pool_out = jnp.where(written[:, :, None], picked, kv_pool[0])]
  transfers between devices with their start and end apart: 4 -> 3, of which waited for: 4 -> 3; matrix products, arithmetic and copies ran while one was open for 3% -> 2% of each run, Pallas kernels for 0% -> 0%
where the time goes in v13:
time: 335 us; the launch traced here: 334 us
  blocking collectives  169 us (50%)
  waiting for transfers between devices  95.6 us (29%)
  local copies, waits for them, and re-layouts  17.5 us (5%)
  starting transfers between devices  14.7 us (4%)
  Pallas kernels  13.2 us (4%)
  other arithmetic  11.2 us (3%)
  matrix products  10.2 us (3%)
    all_to_all x1, blocking collectives, per_device(): lax.all_to_all(outgoing, 'exp', split_axis=0, concat_axis=0, tiled=True)  72.6 us
    all_to_all x1, waiting for transfers between devices, per_device(): lax.all_to_all(result.reshape(received.shape), 'exp', split_axis=0, conca...  58 us
    all_to_all x2, blocking collectives, gather_blocks(): lax.all_to_all(stacked, 'blk', split_axis=0, concat_axis=axis + 1, tiled=...  47.3 us
    all_to_all x2, waiting for transfers between devices, gather_blocks(): lax.all_to_all(stacked, 'blk', split_axis=0, concat_axis=axis + 1, tiled=...  37.7 us
    all_to_all x1, blocking collectives, scatter_sum_blocks(): lax.all_to_all(pieces.astype(jnp.bfloat16), 'blk', split_axis=0, concat_a...  25.2 us
    all_to_all x1, blocking collectives, per_device(): lax.all_to_all(payload, 'blk', split_axis=0, concat_axis=0, tiled=True)  24.3 us
    pallas_call x1, Pallas kernels, local_attention(): pl.pallas_call(attention_kernel, out_shape=(jax.ShapeDtypeStruct((NEW, wi...  10.3 us
    all_to_all x2, starting transfers between devices, gather_blocks(): lax.all_to_all(stacked, 'blk', split_axis=0, concat_axis=axis + 1, tiled=...  9.89 us
  transfers between devices with their start and end apart: 3, of which 3 were waited for; matrix products, arithmetic and copies ran while one was open for 2% of the time, Pallas kernels for 0%

profile of v13, /device:TPU:1, one launch (start us, length us, event | category | flops | bytes accessed | tf_op | source)
XLA Modules:
  0.0 333.5 jit_solution(3949251204755208888)
XLA Ops:
  0.6 1.1 broadcast_in_dim.30
  1.8 25.1 %all_to_all.62 = bf16[16,256,160]{1,2,0:T(8,128)(2,1)S(1)} all-to-all(bf16[16,256,160]{1,2,0:T(8,128)(2,1)S(1)} %broadcast_in_dim.30), channel_id=1, replica_groups=mesh['blk'=16,'exp'=16] {'blk'}, dimensions={0} | all-to-all | bytes 2621440 | tf_op jit(solution)/shard_map/all_to_all | solution.py:173
  27.7 0.8 copy-done.2
  29.0 1.4 broadcast_in_dim.31
  30.5 5.3 %all-to-all-start.1 = ((bf16[16,256,224]{1,2,0:T(8,128)(2,1)}), bf16[16,256,224]{1,2,0:T(8,128)(2,1)}, u32[]{:S(2)}, u32[]{:S(2)}) async-start(bf16[16,256,224]{1,2,0:T(8,128)(2,1)} %broadcast_in_dim.31), calls=%async_computation.1 | async-start | bytes 3670016 | tf_op jit(solution)/shard_map/all_to_all | solution.py:173
  37.2 0.9 copy.38.offset_ref
  39.3 0.8 pad_maximum_fusion.2
  40.2 20.6 %all-to-all-done.1 = bf16[16,256,224]{1,2,0:T(8,128)(2,1)} async-done(((bf16[16,256,224]{1,2,0:T(8,128)(2,1)}), bf16[16,256,224]{1,2,0:T(8,128)(2,1)}, u32[]{:S(2)}, u32[]{:S(2)}) %all-to-all-start.1) | async-done | bytes 1835040 | tf_op jit(solution)/shard_map/all_to_all | solution.py:173
  60.8 1.0 slice.40
  61.8 3.8 %copy.37.proj_ref = bf16[256,3584]{1,0:T(8,128)(2,1)} copy(bf16[256,3584]{0,1:T(8,128)(2,1)} %bitcast.5) | data formatting | bytes 3670016 | tf_op jit(solution)/shard_map/reshape | solution.py:174
  65.6 0.7 fusion.33
  66.6 1.2 copy.46
  68.7 0.9 pad_maximum_fusion.fresh_ref
  69.6 10.3 %shard_map.149 = (bf16[256,2688]{1,0:T(8,128)(2,1)}, bf16[512,1024]{1,0:T(8,128)(2,1)}) custom-call(bf16[256,3584]{1,0:T(8,128)(2,1)} %copy.37.proj_ref, f32[256,128]{1,0:T(8,128)} %get-tuple-element.15.cos_ref, f32[256,128]{1,0:T(8,128)} %get-tuple-element.16.sin_ref, bf16[512,1024]{1,0:T(8,128)(2,1)} %bitcast.113, ...), custom_call_target="tpu_custom_call" | custom-call | flops 1342177280 | bytes 5308416 | tf_op jit(solution)/shard_map/pallas_call | solution.py:107
  79.9 24.3 %all_to_all.63.part_ref = bf16[16,16,2688]{2,1,0:T(8,128)(2,1)} all-to-all(bf16[16,16,2688]{2,1,0:T(8,128)(2,1)} %bitcast.98), channel_id=1, replica_groups=mesh['blk'=16,'exp'=16] {'blk'}, dimensions={0} | all-to-all | bytes 2752512 | tf_op jit(solution)/shard_map/all_to_all | solution.py:259
  104.3 2.9 shard_map.150
  107.1 1.0 broadcast_in_dim.34
  108.2 22.2 %all_to_all.64 = bf16[16,16,2560]{2,1,0:T(8,128)(2,1)S(1)} all-to-all(bf16[16,16,2560]{2,1,0:T(8,128)(2,1)S(1)} %broadcast_in_dim.34), channel_id=1, replica_groups=mesh['blk'=16,'exp'=16] {'blk'}, dimensions={0} | all-to-all | bytes 2621440 | tf_op jit(solution)/shard_map/all_to_all | solution.py:173
  131.0 1.2 broadcast_in_dim.35
  132.2 4.6 %all-to-all-start.4 = ((bf16[16,256,160]{1,2,0:T(8,128)(2,1)}), bf16[16,256,160]{1,2,0:T(8,128)(2,1)S(1)}, u32[]{:S(2)}, u32[]{:S(2)}) async-start(bf16[16,256,160]{1,2,0:T(8,128)(2,1)} %broadcast_in_dim.35), calls=%async_computation.4 | async-start | bytes 2621440 | tf_op jit(solution)/shard_map/all_to_all | solution.py:173
  136.9 1.2 reduce-window.6
  138.5 17.0 %all-to-all-done.4 = bf16[16,256,160]{1,2,0:T(8,128)(2,1)S(1)} async-done(((bf16[16,256,160]{1,2,0:T(8,128)(2,1)}), bf16[16,256,160]{1,2,0:T(8,128)(2,1)S(1)}, u32[]{:S(2)}, u32[]{:S(2)}) %all-to-all-start.4) | async-done | bytes 1310752 | tf_op jit(solution)/shard_map/all_to_all | solution.py:173
  157.2 72.6 %all_to_all.65 = bf16[16,32,2560]{2,1,0:T(8,128)(2,1)S(1)} all-to-all(bf16[16,32,2560]{2,1,0:T(8,128)(2,1)S(1)} %bitcast.90), channel_id=1, replica_groups=mesh['blk'=16,'exp'=16] {'exp'}, dimensions={0} | all-to-all | bytes 5242880 | tf_op jit(solution)/shard_map/all_to_all | solution.py:294
  229.8 2.2 fusion.1
  232.0 3.1 convolution_convert_fusion
  235.1 4.8 %all-to-all-start.6 = ((bf16[16,32,2560]{2,1,0:T(8,128)(2,1)}), bf16[16,32,2560]{2,1,0:T(8,128)(2,1)}, u32[]{:S(2)}, u32[]{:S(2)}) async-start(bf16[16,32,2560]{2,1,0:T(8,128)(2,1)} %bitcast.94), calls=%async_computation.6 | async-start | bytes 5242880 | tf_op jit(solution)/shard_map/all_to_all | solution.py:301
  240.7 0.9 copy-done.1
  241.6 1.6 fusion.34
  243.2 58.0 %all-to-all-done.6 = bf16[16,32,2560]{2,1,0:T(8,128)(2,1)} async-done(((bf16[16,32,2560]{2,1,0:T(8,128)(2,1)}), bf16[16,32,2560]{2,1,0:T(8,128)(2,1)}, u32[]{:S(2)}, u32[]{:S(2)}) %all-to-all-start.6) | async-done | bytes 2621472 | tf_op jit(solution)/shard_map/all_to_all | solution.py:301
  301.2 2.3 convert_reduce_fusion
  306.0 1.5 copy.42
  307.5 25.2 %all_to_all.66 = bf16[16,256,160]{1,2,0:T(8,128)(2,1)S(1)} all-to-all(bf16[16,256,160]{1,2,0:T(8,128)(2,1)} %bitcast.93), channel_id=1, replica_groups=mesh['blk'=16,'exp'=16] {'blk'}, dimensions={0} | all-to-all | bytes 2621440 | tf_op jit(solution)/shard_map/all_to_all | solution.py:181
  (67 shorter events, 11.1 us)
Async XLA Ops:
  0.6 231.4 %copy-start = (bf16[1,384,2560]{2,1,0:T(8,128)(2,1)S(1)}, bf16[1,384,2560]{2,1,0:T(8,128)(2,1)}, u32[]{:S(2)}) copy-start(bf16[1,384,2560]{2,1,0:T(8,128)(2,1)} %param.27) | copy-start | bytes 5898244
  1.8 25.5 %copy-start.9 = (f32[2560]{0:T(1024)S(1)}, f32[2560]{0:T(1024)}, u32[]{:S(2)}) copy-start(f32[2560]{0:T(1024)} %param.15) | copy-start | bytes 30724
  27.3 1.3 copy-start.2
  30.5 5.9 %copy-start.12 = (s32[1,64]{1,0:T(1,128)S(1)}, s32[1,64]{1,0:T(1,128)}, u32[]{:S(2)}) copy-start(s32[1,64]{1,0:T(1,128)} %param.19) | copy-start | bytes 772
  30.5 30.3 %all-to-all-start.1 = ((bf16[16,256,224]{1,2,0:T(8,128)(2,1)}), bf16[16,256,224]{1,2,0:T(8,128)(2,1)}, u32[]{:S(2)}, u32[]{:S(2)}) async-start(bf16[16,256,224]{1,2,0:T(8,128)(2,1)} %broadcast_in_dim.31), calls=%async_computation.1 | async-start | bytes 3670016 | tf_op jit(solution)/shard_map/all_to_all | solution.py:173
  67.8 1.0 slice-start
  108.2 22.2 %copy-start.5 = (bf16[2560,160]{0,1:T(8,128)(2,1)S(1)}, bf16[2560,160]{0,1:T(8,128)(2,1)}, u32[]{:S(2)}) copy-start(bf16[2560,160]{0,1:T(8,128)(2,1)} %param.17) | copy-start | bytes 2457604
  108.2 22.2 %copy-start.6 = (bf16[256,160]{0,1:T(8,128)(2,1)S(1)}, bf16[256,160]{0,1:T(8,128)(2,1)}, u32[]{:S(2)}) copy-start(bf16[256,160]{0,1:T(8,128)(2,1)} %param.14) | copy-start | bytes 245764
  132.2 4.6 %copy-start.8 = (s32[256,6]{0,1:T(8,128)S(1)}, s32[256,6]{0,1:T(8,128)}, u32[]{:S(2)}) copy-start(s32[256,6]{0,1:T(8,128)} %param.22) | copy-start | bytes 18436
  132.2 23.8 %copy-start.7 = (f32[2560]{0:T(1024)S(1)}, f32[2560]{0:T(1024)}, u32[]{:S(2)}) copy-start(f32[2560]{0:T(1024)} %param.21) | copy-start | bytes 30724
  132.2 23.4 %all-to-all-start.4 = ((bf16[16,256,160]{1,2,0:T(8,128)(2,1)}), bf16[16,256,160]{1,2,0:T(8,128)(2,1)S(1)}, u32[]{:S(2)}, u32[]{:S(2)}) async-start(bf16[16,256,160]{1,2,0:T(8,128)(2,1)} %broadcast_in_dim.35), calls=%async_computation.4 | async-start | bytes 2621440 | tf_op jit(solution)/shard_map/all_to_all | solution.py:173
  157.2 72.7 %copy-start.11 = (bf16[1,2560,768]{2,1,0:T(8,128)(2,1)S(1)}, bf16[1,2560,768]{2,1,0:T(8,128)(2,1)}, u32[]{:S(2)}) copy-start(bf16[1,2560,768]{2,1,0:T(8,128)(2,1)} %param.26) | copy-start | bytes 11796484
  235.1 4.9 %copy-start.10 = (f32[256,6]{0,1:T(8,128)S(1)}, f32[256,6]{0,1:T(8,128)}, u32[]{:S(2)}) copy-start(f32[256,6]{0,1:T(8,128)} %param.23) | copy-start | bytes 18436
  235.1 66.1 %all-to-all-start.6 = ((bf16[16,32,2560]{2,1,0:T(8,128)(2,1)}), bf16[16,32,2560]{2,1,0:T(8,128)(2,1)}, u32[]{:S(2)}, u32[]{:S(2)}) async-start(bf16[16,32,2560]{2,1,0:T(8,128)(2,1)} %bitcast.94), calls=%async_computation.6 | async-start | bytes 5242880 | tf_op jit(solution)/shard_map/all_to_all | solution.py:301
  240.1 1.5 copy-start.1
  304.1 1.0 copy-start.3
  304.2 1.3 copy-start.4

commit v14 on v13

--- a/solution.py
+++ b/solution.py
@@ -50,6 +50,19 @@
     middle = rest.astype(jnp.bfloat16).astype(jnp.float32)
     low = (rest - middle).astype(jnp.bfloat16).astype(jnp.float32)
     return [high, middle, low]
+
+
+def query_columns(proj_ref, head):
+    width = proj_ref.shape[2]
+    first = head * HEAD_DIM
+    last = first + HEAD_DIM
+    pieces = []
+    while first < last:
+        source = first // width
+        stop = min(last, (source + 1) * width)
+        pieces.append(proj_ref[source, :, first - source * width : stop - source * width])
+        first = stop
+    return pieces[0] if len(pieces) == 1 else jnp.concatenate(pieces, axis=1)
 
 
 def attention_kernel(
@@ -73,7 +86,7 @@
         rotated = []
         for member in range(group_size):
             head = kv * group_size + member
-            raw = proj_ref[:, head * HEAD_DIM : (head + 1) * HEAD_DIM].astype(jnp.float32)
+            raw = query_columns(proj_ref, head).astype(jnp.float32)
             swapped = pltpu.roll(raw, HEAD_DIM // 2, 1)
             rotated.append((raw * cosine + swapped * sine_signed).astype(jnp.bfloat16))
         query = jnp.concatenate(rotated, axis=0)
@@ -213,7 +226,11 @@
     projected = jnp.dot(attn_in, qkv_weight, preferred_element_type=jnp.float32).astype(
         jnp.bfloat16
     )
-    projected_all = gather_blocks(projected, 1)
+    projected_blocks = lax.all_to_all(
+        jnp.broadcast_to(projected[None], (blocks,) + projected.shape),
+        "blk", split_axis=0, concat_axis=0, tiled=True,
+    )
+    projected_all = projected_blocks.transpose(1, 0, 2).reshape(NEW, -1)
     length = cache_lens[0]
     positions = length + jnp.arange(NEW, dtype=jnp.int32)
     fresh_keys = rotate(
@@ -245,7 +262,7 @@
     cosine_full = jnp.concatenate([cosine, cosine], axis=1)
     sine_signed = jnp.concatenate([-sine_vals, sine_vals], axis=1)
     payload, slot_rows = local_attention(
-        projected_all,
+        projected_blocks,
         cosine_full,
         sine_signed,
         kv_pool[0].reshape(local_pages * PAGE, 2 * key_width),

time: 335 us -> 337 us (level)
    all_to_all x2 -> x1, waiting for transfers between devices: 37.7 us -> 17 us  [gather_blocks(): lax.all_to_all(stacked, 'blk', split_axis=0, concat_axis=axis + 1, tiled=...]
    all_to_all x0 -> x1, waiting for transfers between devices: none -> 20.6 us  [per_device(): lax.all_to_all(jnp.broadcast_to(projected[None], (blocks,) + projected.sh...]
    all_to_all x0 -> x1, starting transfers between devices: none -> 5.28 us  [per_device(): lax.all_to_all(jnp.broadcast_to(projected[None], (blocks,) + projected.sh...]
    all_to_all x2 -> x1, starting transfers between devices: 9.89 us -> 4.62 us  [gather_blocks(): lax.all_to_all(stacked, 'blk', split_axis=0, concat_axis=axis + 1, tiled=...]
    reshape x1 -> x0, local copies, waits for them, and re-layouts: 3.84 us -> none  [gather_blocks(): return received.reshape(received.shape[1:])]
    all_to_all x0 -> x1, local copies, waits for them, and re-layouts: none -> 3.82 us  [per_device(): lax.all_to_all(jnp.broadcast_to(projected[None], (blocks,) + projected.sh...]
where the time goes in v14:
time: 337 us; the launch traced here: 336 us
  blocking collectives  169 us (50%)
  waiting for transfers between devices  95.6 us (28%)
  local copies, waits for them, and re-layouts  16.7 us (5%)
  Pallas kernels  16.2 us (5%)
  starting transfers between devices  14.7 us (4%)
  other arithmetic  11.2 us (3%)
  matrix products  10.2 us (3%)
    all_to_all x1, blocking collectives, per_device(): lax.all_to_all(outgoing, 'exp', split_axis=0, concat_axis=0, tiled=True)  72.6 us
    all_to_all x1, waiting for transfers between devices, per_device(): lax.all_to_all(result.reshape(received.shape), 'exp', split_axis=0, conca...  58 us
    all_to_all x2, blocking collectives, gather_blocks(): lax.all_to_all(stacked, 'blk', split_axis=0, concat_axis=axis + 1, tiled=...  47.3 us
    all_to_all x1, blocking collectives, scatter_sum_blocks(): lax.all_to_all(pieces.astype(jnp.bfloat16), 'blk', split_axis=0, concat_a...  25.2 us
    all_to_all x1, blocking collectives, per_device(): lax.all_to_all(payload, 'blk', split_axis=0, concat_axis=0, tiled=True)  24.3 us
    all_to_all x1, waiting for transfers between devices, per_device(): lax.all_to_all(jnp.broadcast_to(projected[None], (blocks,) + projected.sh...  20.6 us
    all_to_all x1, waiting for transfers between devices, gather_blocks(): lax.all_to_all(stacked, 'blk', split_axis=0, concat_axis=axis + 1, tiled=...  17 us
    pallas_call x1, Pallas kernels, local_attention(): pl.pallas_call(attention_kernel, out_shape=(jax.ShapeDtypeStruct((NEW, wi...  13.3 us
  transfers between devices with their start and end apart: 3, of which 3 were waited for; matrix products, arithmetic and copies ran while one was open for 2% of the time, Pallas kernels for 0%

profile of v14, /device:TPU:1, one launch (start us, length us, event | category | flops | bytes accessed | tf_op | source)
XLA Modules:
  0.0 335.8 jit_solution(5325528248780099725)
XLA Ops:
  0.6 1.1 broadcast_in_dim.30
  1.8 25.1 %all_to_all.52 = bf16[16,256,160]{1,2,0:T(8,128)(2,1)S(1)} all-to-all(bf16[16,256,160]{1,2,0:T(8,128)(2,1)S(1)} %broadcast_in_dim.30), channel_id=1, replica_groups=mesh['blk'=16,'exp'=16] {'blk'}, dimensions={0} | all-to-all | bytes 2621440 | tf_op jit(solution)/shard_map/all_to_all | solution.py:186
  27.7 0.8 copy-done.2
  29.0 1.4 broadcast_in_dim.31
  30.5 5.3 %all-to-all-start.1 = ((bf16[16,256,224]{1,2,0:T(8,128)(2,1)}), bf16[16,256,224]{1,2,0:T(8,128)(2,1)}, u32[]{:S(2)}, u32[]{:S(2)}) async-start(bf16[16,256,224]{1,2,0:T(8,128)(2,1)} %broadcast_in_dim.31), calls=%async_computation.1 | async-start | bytes 3670016 | tf_op jit(solution)/shard_map/all_to_all | solution.py:229
  36.6 0.7 iota_add_fusion.1
  37.3 0.9 copy.51.offset_ref
  38.1 0.7 iota_add_fusion.qpos_ref
  39.3 0.8 pad_maximum_fusion.2
  40.2 20.6 %all-to-all-done.1 = bf16[16,256,224]{1,2,0:T(8,128)(2,1)} async-done(((bf16[16,256,224]{1,2,0:T(8,128)(2,1)}), bf16[16,256,224]{1,2,0:T(8,128)(2,1)}, u32[]{:S(2)}, u32[]{:S(2)}) %all-to-all-start.1) | async-done | bytes 1835040 | tf_op jit(solution)/shard_map/all_to_all | solution.py:229
  60.8 1.8 fusion.33
  64.2 0.9 pad_maximum_fusion.fresh_ref
  65.1 3.8 %copy.50.proj_ref = bf16[16,256,224]{2,1,0:T(8,128)(2,1)} copy(bf16[16,256,224]{1,2,0:T(8,128)(2,1)} %all-to-all-done.1) | data formatting | bytes 3670016 | tf_op jit(solution)/shard_map/all_to_all | solution.py:229
  68.9 13.3 %shard_map.149 = (bf16[256,2688]{1,0:T(8,128)(2,1)}, bf16[512,1024]{1,0:T(8,128)(2,1)}) custom-call(bf16[16,256,224]{2,1,0:T(8,128)(2,1)} %copy.50.proj_ref, f32[256,128]{1,0:T(8,128)} %get-tuple-element.17.cos_ref, f32[256,128]{1,0:T(8,128)} %get-tuple-element.18.sin_ref, bf16[512,1024]{1,0:T(8,128)(2,1)} %bitcast.111, ...), custom_call_target="tpu_custom_call" | custom-call | flops 1342177280 | bytes 5308416 | tf_op jit(solution)/shard_map/pallas_call | solution.py:120
  82.2 24.3 %all_to_all.53.part_ref = bf16[16,16,2688]{2,1,0:T(8,128)(2,1)} all-to-all(bf16[16,16,2688]{2,1,0:T(8,128)(2,1)} %bitcast.96), channel_id=1, replica_groups=mesh['blk'=16,'exp'=16] {'blk'}, dimensions={0} | all-to-all | bytes 2752512 | tf_op jit(solution)/shard_map/all_to_all | solution.py:276
  106.5 2.9 shard_map.150
  109.4 1.0 broadcast_in_dim.34
  110.4 22.2 %all_to_all.54 = bf16[16,16,2560]{2,1,0:T(8,128)(2,1)S(1)} all-to-all(bf16[16,16,2560]{2,1,0:T(8,128)(2,1)S(1)} %broadcast_in_dim.34), channel_id=1, replica_groups=mesh['blk'=16,'exp'=16] {'blk'}, dimensions={0} | all-to-all | bytes 2621440 | tf_op jit(solution)/shard_map/all_to_all | solution.py:186
  133.2 1.2 broadcast_in_dim.35
  134.4 4.6 %all-to-all-start.4 = ((bf16[16,256,160]{1,2,0:T(8,128)(2,1)}), bf16[16,256,160]{1,2,0:T(8,128)(2,1)S(1)}, u32[]{:S(2)}, u32[]{:S(2)}) async-start(bf16[16,256,160]{1,2,0:T(8,128)(2,1)} %broadcast_in_dim.35), calls=%async_computation.4 | async-start | bytes 2621440 | tf_op jit(solution)/shard_map/all_to_all | solution.py:186
  139.2 1.2 reduce-window.6
  140.8 17.0 %all-to-all-done.4 = bf16[16,256,160]{1,2,0:T(8,128)(2,1)S(1)} async-done(((bf16[16,256,160]{1,2,0:T(8,128)(2,1)}), bf16[16,256,160]{1,2,0:T(8,128)(2,1)S(1)}, u32[]{:S(2)}, u32[]{:S(2)}) %all-to-all-start.4) | async-done | bytes 1310752 | tf_op jit(solution)/shard_map/all_to_all | solution.py:186
  159.4 72.6 %all_to_all.55 = bf16[16,32,2560]{2,1,0:T(8,128)(2,1)S(1)} all-to-all(bf16[16,32,2560]{2,1,0:T(8,128)(2,1)S(1)} %bitcast.88), channel_id=1, replica_groups=mesh['blk'=16,'exp'=16] {'exp'}, dimensions={0} | all-to-all | bytes 5242880 | tf_op jit(solution)/shard_map/all_to_all | solution.py:311
  232.1 2.2 fusion.1
  234.3 3.1 convolution_convert_fusion
  237.4 4.8 %all-to-all-start.6 = ((bf16[16,32,2560]{2,1,0:T(8,128)(2,1)}), bf16[16,32,2560]{2,1,0:T(8,128)(2,1)}, u32[]{:S(2)}, u32[]{:S(2)}) async-start(bf16[16,32,2560]{2,1,0:T(8,128)(2,1)} %bitcast.92), calls=%async_computation.6 | async-start | bytes 5242880 | tf_op jit(solution)/shard_map/all_to_all | solution.py:318
  242.9 0.9 copy-done.1
  243.9 1.6 fusion.35
  245.5 58.0 %all-to-all-done.6 = bf16[16,32,2560]{2,1,0:T(8,128)(2,1)} async-done(((bf16[16,32,2560]{2,1,0:T(8,128)(2,1)}), bf16[16,32,2560]{2,1,0:T(8,128)(2,1)}, u32[]{:S(2)}, u32[]{:S(2)}) %all-to-all-start.6) | async-done | bytes 2621472 | tf_op jit(solution)/shard_map/all_to_all | solution.py:318
  303.5 2.3 convert_reduce_fusion
  308.3 1.5 copy.55
  309.8 25.2 %all_to_all.56 = bf16[16,256,160]{1,2,0:T(8,128)(2,1)S(1)} all-to-all(bf16[16,256,160]{1,2,0:T(8,128)(2,1)} %bitcast.91), channel_id=1, replica_groups=mesh['blk'=16,'exp'=16] {'blk'}, dimensions={0} | all-to-all | bytes 2621440 | tf_op jit(solution)/shard_map/all_to_all | solution.py:194
  (68 shorter events, 10.2 us)
Async XLA Ops:
  0.6 233.7 %copy-start = (bf16[1,384,2560]{2,1,0:T(8,128)(2,1)S(1)}, bf16[1,384,2560]{2,1,0:T(8,128)(2,1)}, u32[]{:S(2)}) copy-start(bf16[1,384,2560]{2,1,0:T(8,128)(2,1)} %param.27) | copy-start | bytes 5898244
  1.8 25.5 %copy-start.10 = (f32[2560]{0:T(1024)S(1)}, f32[2560]{0:T(1024)}, u32[]{:S(2)}) copy-start(f32[2560]{0:T(1024)} %param.15) | copy-start | bytes 30724
  27.3 1.3 copy-start.2
  30.5 5.9 %copy-start.13 = (s32[1,64]{1,0:T(1,128)S(1)}, s32[1,64]{1,0:T(1,128)}, u32[]{:S(2)}) copy-start(s32[1,64]{1,0:T(1,128)} %param.19) | copy-start | bytes 772
  30.5 30.4 %all-to-all-start.1 = ((bf16[16,256,224]{1,2,0:T(8,128)(2,1)}), bf16[16,256,224]{1,2,0:T(8,128)(2,1)}, u32[]{:S(2)}, u32[]{:S(2)}) async-start(bf16[16,256,224]{1,2,0:T(8,128)(2,1)} %broadcast_in_dim.31), calls=%async_computation.1 | async-start | bytes 3670016 | tf_op jit(solution)/shard_map/all_to_all | solution.py:229
  63.1 1.0 copy-start.4
  110.4 22.2 %copy-start.6 = (bf16[2560,160]{0,1:T(8,128)(2,1)S(1)}, bf16[2560,160]{0,1:T(8,128)(2,1)}, u32[]{:S(2)}) copy-start(bf16[2560,160]{0,1:T(8,128)(2,1)} %param.17) | copy-start | bytes 2457604
  110.4 22.2 %copy-start.7 = (bf16[256,160]{0,1:T(8,128)(2,1)S(1)}, bf16[256,160]{0,1:T(8,128)(2,1)}, u32[]{:S(2)}) copy-start(bf16[256,160]{0,1:T(8,128)(2,1)} %param.14) | copy-start | bytes 245764
  134.4 4.6 %copy-start.9 = (s32[256,6]{0,1:T(8,128)S(1)}, s32[256,6]{0,1:T(8,128)}, u32[]{:S(2)}) copy-start(s32[256,6]{0,1:T(8,128)} %param.22) | copy-start | bytes 18436
  134.4 23.8 %copy-start.8 = (f32[2560]{0:T(1024)S(1)}, f32[2560]{0:T(1024)}, u32[]{:S(2)}) copy-start(f32[2560]{0:T(1024)} %param.21) | copy-start | bytes 30724
  134.4 23.4 %all-to-all-start.4 = ((bf16[16,256,160]{1,2,0:T(8,128)(2,1)}), bf16[16,256,160]{1,2,0:T(8,128)(2,1)S(1)}, u32[]{:S(2)}, u32[]{:S(2)}) async-start(bf16[16,256,160]{1,2,0:T(8,128)(2,1)} %broadcast_in_dim.35), calls=%async_computation.4 | async-start | bytes 2621440 | tf_op jit(solution)/shard_map/all_to_all | solution.py:186
  159.4 72.7 %copy-start.12 = (bf16[1,2560,768]{2,1,0:T(8,128)(2,1)S(1)}, bf16[1,2560,768]{2,1,0:T(8,128)(2,1)}, u32[]{:S(2)}) copy-start(bf16[1,2560,768]{2,1,0:T(8,128)(2,1)} %param.26) | copy-start | bytes 11796484
  237.4 4.9 %copy-start.11 = (f32[256,6]{0,1:T(8,128)S(1)}, f32[256,6]{0,1:T(8,128)}, u32[]{:S(2)}) copy-start(f32[256,6]{0,1:T(8,128)} %param.23) | copy-start | bytes 18436
  237.4 66.1 %all-to-all-start.6 = ((bf16[16,32,2560]{2,1,0:T(8,128)(2,1)}), bf16[16,32,2560]{2,1,0:T(8,128)(2,1)}, u32[]{:S(2)}, u32[]{:S(2)}) async-start(bf16[16,32,2560]{2,1,0:T(8,128)(2,1)} %bitcast.92), calls=%async_computation.6 | async-start | bytes 5242880 | tf_op jit(solution)/shard_map/all_to_all | solution.py:318
  242.3 1.5 copy-start.1
  306.4 1.0 copy-start.3
  306.4 1.3 copy-start.5

commit v15 on v13

--- a/solution.py
+++ b/solution.py
@@ -148,21 +148,22 @@
             part_ref[:, :, head * HEAD_DIM : (head + 1) * HEAD_DIM].astype(jnp.float32) * factor,
             axis=0,
         )
-        out_ref[:, head * HEAD_DIM : (head + 1) * HEAD_DIM] = (
-            numerator / denominator
-        ).astype(out_ref.dtype)
+        result = (numerator / denominator).astype(out_ref.dtype)
+        out_ref[:, :, head * HEAD_DIM : (head + 1) * HEAD_DIM] = jnp.broadcast_to(
+            result[None], (out_ref.shape[0],) + result.shape
+        )
 
 
 def combine_attention(parts):
     sources, rows, width = parts.shape
     return pl.pallas_call(
         combine_kernel,
-        out_shape=jax.ShapeDtypeStruct((rows, HEADS * HEAD_DIM), jnp.bfloat16),
+        out_shape=jax.ShapeDtypeStruct((sources, rows, HEADS * HEAD_DIM), jnp.bfloat16),
         in_specs=[pl.BlockSpec(memory_space=pltpu.VMEM)],
         out_specs=pl.BlockSpec(memory_space=pltpu.VMEM),
         cost_estimate=pl.CostEstimate(
             flops=3 * parts.size, transcendentals=sources * rows * 128,
-            bytes_accessed=parts.size * 2 + rows * HEADS * HEAD_DIM * 2,
+            bytes_accessed=parts.size * 2 + sources * rows * HEADS * HEAD_DIM * 2,
         ),
     )(parts)
 
@@ -259,7 +260,7 @@
     gathered = lax.all_to_all(payload, "blk", split_axis=0, concat_axis=0, tiled=True)
     own_attention = combine_attention(gathered)
     attended = jnp.dot(
-        gather_blocks(own_attention, 0),
+        lax.all_to_all(own_attention, "blk", split_axis=0, concat_axis=0, tiled=True).reshape(NEW, query_width),
         out_weight,
         preferred_element_type=jnp.float32,
     )

time: 335 us -> 335 us (level)
    all_to_all x0 -> x1, blocking collectives: none -> 23.2 us  [per_device(): lax.all_to_all(own_attention, 'blk', split_axis=0, concat_axis=0, tiled=T...]
    all_to_all x2 -> x1, blocking collectives: 47.3 us -> 25.1 us  [gather_blocks(): lax.all_to_all(stacked, 'blk', split_axis=0, concat_axis=axis + 1, tiled=...]
where the time goes in v15:
time: 335 us; the launch traced here: 334 us
  blocking collectives  171 us (51%)
  waiting for transfers between devices  95.6 us (29%)
  local copies, waits for them, and re-layouts  16.5 us (5%)
  starting transfers between devices  14.7 us (4%)
  Pallas kernels  13.8 us (4%)
  other arithmetic  11.2 us (3%)
  matrix products  10.2 us (3%)
    all_to_all x1, blocking collectives, per_device(): lax.all_to_all(outgoing, 'exp', split_axis=0, concat_axis=0, tiled=True)  72.6 us
    all_to_all x1, waiting for transfers between devices, per_device(): lax.all_to_all(result.reshape(received.shape), 'exp', split_axis=0, conca...  58 us
    all_to_all x2, waiting for transfers between devices, gather_blocks(): lax.all_to_all(stacked, 'blk', split_axis=0, concat_axis=axis + 1, tiled=...  37.7 us
    all_to_all x1, blocking collectives, scatter_sum_blocks(): lax.all_to_all(pieces.astype(jnp.bfloat16), 'blk', split_axis=0, concat_a...  25.2 us
    all_to_all x1, blocking collectives, gather_blocks(): lax.all_to_all(stacked, 'blk', split_axis=0, concat_axis=axis + 1, tiled=...  25.1 us
    all_to_all x1, blocking collectives, per_device(): lax.all_to_all(payload, 'blk', split_axis=0, concat_axis=0, tiled=True)  24.3 us
    all_to_all x1, blocking collectives, per_device(): lax.all_to_all(own_attention, 'blk', split_axis=0, concat_axis=0, tiled=T...  23.2 us
    pallas_call x1, Pallas kernels, local_attention(): pl.pallas_call(attention_kernel, out_shape=(jax.ShapeDtypeStruct((NEW, wi...  10.3 us
  transfers between devices with their start and end apart: 3, of which 3 were waited for; matrix products, arithmetic and copies ran while one was open for 2% of the time, Pallas kernels for 0%

profile of v15, /device:TPU:1, one launch (start us, length us, event | category | flops | bytes accessed | tf_op | source)
XLA Modules:
  0.0 334.1 jit_solution(6343289101754501426)
XLA Ops:
  0.6 1.1 broadcast_in_dim.28
  1.8 25.1 %all_to_all.58 = bf16[16,256,160]{1,2,0:T(8,128)(2,1)S(1)} all-to-all(bf16[16,256,160]{1,2,0:T(8,128)(2,1)S(1)} %broadcast_in_dim.28), channel_id=1, replica_groups=mesh['blk'=16,'exp'=16] {'blk'}, dimensions={0} | all-to-all | bytes 2621440 | tf_op jit(solution)/shard_map/all_to_all | solution.py:174
  27.7 0.8 copy-done.2
  29.0 1.4 broadcast_in_dim.29
  30.5 5.3 %all-to-all-start.1 = ((bf16[16,256,224]{1,2,0:T(8,128)(2,1)}), bf16[16,256,224]{1,2,0:T(8,128)(2,1)}, u32[]{:S(2)}, u32[]{:S(2)}) async-start(bf16[16,256,224]{1,2,0:T(8,128)(2,1)} %broadcast_in_dim.29), calls=%async_computation.1 | async-start | bytes 3670016 | tf_op jit(solution)/shard_map/all_to_all | solution.py:174
  37.2 0.9 copy.38.offset_ref
  38.1 0.7 iota_add_fusion.qpos_ref
  39.3 0.8 pad_maximum_fusion.2
  40.2 20.6 %all-to-all-done.1 = bf16[16,256,224]{1,2,0:T(8,128)(2,1)} async-done(((bf16[16,256,224]{1,2,0:T(8,128)(2,1)}), bf16[16,256,224]{1,2,0:T(8,128)(2,1)}, u32[]{:S(2)}, u32[]{:S(2)}) %all-to-all-start.1) | async-done | bytes 1835040 | tf_op jit(solution)/shard_map/all_to_all | solution.py:174
  60.8 1.0 slice.40
  61.8 3.8 %copy.37.proj_ref = bf16[256,3584]{1,0:T(8,128)(2,1)} copy(bf16[256,3584]{0,1:T(8,128)(2,1)} %bitcast.5) | data formatting | bytes 3670016 | tf_op jit(solution)/shard_map/reshape | solution.py:175
  65.6 0.7 fusion.33
  66.6 1.2 copy.46
  68.7 0.9 pad_maximum_fusion.fresh_ref
  69.6 10.3 %shard_map.149 = (bf16[256,2688]{1,0:T(8,128)(2,1)}, bf16[512,1024]{1,0:T(8,128)(2,1)}) custom-call(bf16[256,3584]{1,0:T(8,128)(2,1)} %copy.37.proj_ref, f32[256,128]{1,0:T(8,128)} %get-tuple-element.15.cos_ref, f32[256,128]{1,0:T(8,128)} %get-tuple-element.16.sin_ref, bf16[512,1024]{1,0:T(8,128)(2,1)} %bitcast.113, ...), custom_call_target="tpu_custom_call" | custom-call | flops 1342177280 | bytes 5308416 | tf_op jit(solution)/shard_map/pallas_call | solution.py:107
  79.9 24.3 %all_to_all.59.part_ref = bf16[16,16,2688]{2,1,0:T(8,128)(2,1)} all-to-all(bf16[16,16,2688]{2,1,0:T(8,128)(2,1)} %bitcast.98), channel_id=1, replica_groups=mesh['blk'=16,'exp'=16] {'blk'}, dimensions={0} | all-to-all | bytes 2752512 | tf_op jit(solution)/shard_map/all_to_all | solution.py:260
  104.3 3.4 %shard_map.150 = bf16[16,16,2560]{2,1,0:T(8,128)(2,1)} custom-call(bf16[16,16,2688]{2,1,0:T(8,128)(2,1)} %all_to_all.59.part_ref), custom_call_target="tpu_custom_call" | custom-call | flops 2064384 | bytes 2686976 | tf_op jit(solution)/shard_map/pallas_call | solution.py:159
  107.7 23.2 %all_to_all.60 = bf16[16,16,2560]{2,1,0:T(8,128)(2,1)S(1)} all-to-all(bf16[16,16,2560]{2,1,0:T(8,128)(2,1)} %shard_map.150), channel_id=1, replica_groups=mesh['blk'=16,'exp'=16] {'blk'}, dimensions={0} | all-to-all | bytes 2621440 | tf_op jit(solution)/shard_map/all_to_all | solution.py:263
  131.5 1.2 broadcast_in_dim.32
  132.7 4.6 %all-to-all-start.4 = ((bf16[16,256,160]{1,2,0:T(8,128)(2,1)}), bf16[16,256,160]{1,2,0:T(8,128)(2,1)S(1)}, u32[]{:S(2)}, u32[]{:S(2)}) async-start(bf16[16,256,160]{1,2,0:T(8,128)(2,1)} %broadcast_in_dim.32), calls=%async_computation.4 | async-start | bytes 2621440 | tf_op jit(solution)/shard_map/all_to_all | solution.py:174
  137.5 1.2 reduce-window.6
  139.1 17.0 %all-to-all-done.4 = bf16[16,256,160]{1,2,0:T(8,128)(2,1)S(1)} async-done(((bf16[16,256,160]{1,2,0:T(8,128)(2,1)}), bf16[16,256,160]{1,2,0:T(8,128)(2,1)S(1)}, u32[]{:S(2)}, u32[]{:S(2)}) %all-to-all-start.4) | async-done | bytes 1310752 | tf_op jit(solution)/shard_map/all_to_all | solution.py:174
  157.7 72.6 %all_to_all.61 = bf16[16,32,2560]{2,1,0:T(8,128)(2,1)S(1)} all-to-all(bf16[16,32,2560]{2,1,0:T(8,128)(2,1)S(1)} %bitcast.90), channel_id=1, replica_groups=mesh['blk'=16,'exp'=16] {'exp'}, dimensions={0} | all-to-all | bytes 5242880 | tf_op jit(solution)/shard_map/all_to_all | solution.py:295
  230.4 2.2 fusion.1
  232.6 3.1 convolution_convert_fusion
  235.7 4.9 %all-to-all-start.6 = ((bf16[16,32,2560]{2,1,0:T(8,128)(2,1)}), bf16[16,32,2560]{2,1,0:T(8,128)(2,1)}, u32[]{:S(2)}, u32[]{:S(2)}) async-start(bf16[16,32,2560]{2,1,0:T(8,128)(2,1)} %bitcast.94), calls=%async_computation.6 | async-start | bytes 5242880 | tf_op jit(solution)/shard_map/all_to_all | solution.py:302
  241.2 0.9 copy-done.1
  242.2 1.6 fusion.34
  243.8 58.0 %all-to-all-done.6 = bf16[16,32,2560]{2,1,0:T(8,128)(2,1)} async-done(((bf16[16,32,2560]{2,1,0:T(8,128)(2,1)}), bf16[16,32,2560]{2,1,0:T(8,128)(2,1)}, u32[]{:S(2)}, u32[]{:S(2)}) %all-to-all-start.6) | async-done | bytes 2621472 | tf_op jit(solution)/shard_map/all_to_all | solution.py:302
  301.8 2.3 convert_reduce_fusion
  306.6 1.5 copy.42
  308.1 25.2 %all_to_all.62 = bf16[16,256,160]{1,2,0:T(8,128)(2,1)S(1)} all-to-all(bf16[16,256,160]{1,2,0:T(8,128)(2,1)} %bitcast.93), channel_id=1, replica_groups=mesh['blk'=16,'exp'=16] {'blk'}, dimensions={0} | all-to-all | bytes 2621440 | tf_op jit(solution)/shard_map/all_to_all | solution.py:182
  (66 shorter events, 10.5 us)
Async XLA Ops:
  0.6 231.9 %copy-start = (bf16[1,384,2560]{2,1,0:T(8,128)(2,1)S(1)}, bf16[1,384,2560]{2,1,0:T(8,128)(2,1)}, u32[]{:S(2)}) copy-start(bf16[1,384,2560]{2,1,0:T(8,128)(2,1)} %param.27) | copy-start | bytes 5898244
  1.8 25.5 %copy-start.9 = (f32[2560]{0:T(1024)S(1)}, f32[2560]{0:T(1024)}, u32[]{:S(2)}) copy-start(f32[2560]{0:T(1024)} %param.15) | copy-start | bytes 30724
  27.3 1.3 copy-start.2
  30.5 5.9 %copy-start.12 = (s32[1,64]{1,0:T(1,128)S(1)}, s32[1,64]{1,0:T(1,128)}, u32[]{:S(2)}) copy-start(s32[1,64]{1,0:T(1,128)} %param.19) | copy-start | bytes 772
  30.5 30.3 %all-to-all-start.1 = ((bf16[16,256,224]{1,2,0:T(8,128)(2,1)}), bf16[16,256,224]{1,2,0:T(8,128)(2,1)}, u32[]{:S(2)}, u32[]{:S(2)}) async-start(bf16[16,256,224]{1,2,0:T(8,128)(2,1)} %broadcast_in_dim.29), calls=%async_computation.1 | async-start | bytes 3670016 | tf_op jit(solution)/shard_map/all_to_all | solution.py:174
  67.8 1.0 slice-start
  107.7 23.3 %copy-start.5 = (bf16[2560,160]{0,1:T(8,128)(2,1)S(1)}, bf16[2560,160]{0,1:T(8,128)(2,1)}, u32[]{:S(2)}) copy-start(bf16[2560,160]{0,1:T(8,128)(2,1)} %param.17) | copy-start | bytes 2457604
  107.7 23.3 %copy-start.6 = (bf16[256,160]{0,1:T(8,128)(2,1)S(1)}, bf16[256,160]{0,1:T(8,128)(2,1)}, u32[]{:S(2)}) copy-start(bf16[256,160]{0,1:T(8,128)(2,1)} %param.14) | copy-start | bytes 245764
  132.7 4.6 %copy-start.8 = (s32[256,6]{0,1:T(8,128)S(1)}, s32[256,6]{0,1:T(8,128)}, u32[]{:S(2)}) copy-start(s32[256,6]{0,1:T(8,128)} %param.22) | copy-start | bytes 18436
  132.7 23.8 %copy-start.7 = (f32[2560]{0:T(1024)S(1)}, f32[2560]{0:T(1024)}, u32[]{:S(2)}) copy-start(f32[2560]{0:T(1024)} %param.21) | copy-start | bytes 30724
  132.7 23.4 %all-to-all-start.4 = ((bf16[16,256,160]{1,2,0:T(8,128)(2,1)}), bf16[16,256,160]{1,2,0:T(8,128)(2,1)S(1)}, u32[]{:S(2)}, u32[]{:S(2)}) async-start(bf16[16,256,160]{1,2,0:T(8,128)(2,1)} %broadcast_in_dim.32), calls=%async_computation.4 | async-start | bytes 2621440 | tf_op jit(solution)/shard_map/all_to_all | solution.py:174
  157.7 72.7 %copy-start.11 = (bf16[1,2560,768]{2,1,0:T(8,128)(2,1)S(1)}, bf16[1,2560,768]{2,1,0:T(8,128)(2,1)}, u32[]{:S(2)}) copy-start(bf16[1,2560,768]{2,1,0:T(8,128)(2,1)} %param.26) | copy-start | bytes 11796484
  235.7 4.9 %copy-start.10 = (f32[256,6]{0,1:T(8,128)S(1)}, f32[256,6]{0,1:T(8,128)}, u32[]{:S(2)}) copy-start(f32[256,6]{0,1:T(8,128)} %param.23) | copy-start | bytes 18436
  235.7 66.1 %all-to-all-start.6 = ((bf16[16,32,2560]{2,1,0:T(8,128)(2,1)}), bf16[16,32,2560]{2,1,0:T(8,128)(2,1)}, u32[]{:S(2)}, u32[]{:S(2)}) async-start(bf16[16,32,2560]{2,1,0:T(8,128)(2,1)} %bitcast.94), calls=%async_computation.6 | async-start | bytes 5242880 | tf_op jit(solution)/shard_map/all_to_all | solution.py:302
  240.6 1.5 copy-start.1
  304.7 1.0 copy-start.3
  304.7 1.3 copy-start.4

commit v16 on v15

--- a/solution.py
+++ b/solution.py
@@ -310,8 +310,11 @@
     upper_part = slot_values.astype(jnp.bfloat16)
     lower_part = (slot_values - upper_part.astype(jnp.float32)).astype(jnp.bfloat16)
     routed = jnp.einsum(
-        "ect,ecd->td", selector, upper_part, preferred_element_type=jnp.float32
-    ) + jnp.einsum("ect,ecd->td", selector, lower_part, preferred_element_type=jnp.float32)
+        "ect,ecd->td",
+        jnp.concatenate([selector, selector], axis=1),
+        jnp.concatenate([upper_part, lower_part], axis=1),
+        preferred_element_type=jnp.float32,
+    )
     layer_term = shared_term + routed
     summed_cols = scatter_sum_blocks(layer_term)
     hidden_out = (mixed_cols.astype(jnp.float32) + summed_cols).astype(jnp.bfloat16)

time: 335 us -> 335 us (level)
  no operation moved by 1% of the time
where the time goes in v16:
time: 335 us; the launch traced here: 334 us
  blocking collectives  171 us (51%)
  waiting for transfers between devices  95.7 us (29%)
  local copies, waits for them, and re-layouts  16.5 us (5%)
  starting transfers between devices  14.7 us (4%)
  Pallas kernels  13.8 us (4%)
  other arithmetic  11.4 us (3%)
  matrix products  9.62 us (3%)
    all_to_all x1, blocking collectives, per_device(): lax.all_to_all(outgoing, 'exp', split_axis=0, concat_axis=0, tiled=True)  72.6 us
    all_to_all x1, waiting for transfers between devices, per_device(): lax.all_to_all(result.reshape(received.shape), 'exp', split_axis=0, conca...  58 us
    all_to_all x2, waiting for transfers between devices, gather_blocks(): lax.all_to_all(stacked, 'blk', split_axis=0, concat_axis=axis + 1, tiled=...  37.7 us
    all_to_all x1, blocking collectives, scatter_sum_blocks(): lax.all_to_all(pieces.astype(jnp.bfloat16), 'blk', split_axis=0, concat_a...  25.2 us
    all_to_all x1, blocking collectives, gather_blocks(): lax.all_to_all(stacked, 'blk', split_axis=0, concat_axis=axis + 1, tiled=...  25.1 us
    all_to_all x1, blocking collectives, per_device(): lax.all_to_all(payload, 'blk', split_axis=0, concat_axis=0, tiled=True)  24.3 us
    all_to_all x1, blocking collectives, per_device(): lax.all_to_all(own_attention, 'blk', split_axis=0, concat_axis=0, tiled=T...  23.2 us
    pallas_call x1, Pallas kernels, local_attention(): pl.pallas_call(attention_kernel, out_shape=(jax.ShapeDtypeStruct((NEW, wi...  10.3 us
  transfers between devices with their start and end apart: 3, of which 3 were waited for; matrix products, arithmetic and copies ran while one was open for 2% of the time, Pallas kernels for 0%

profile of v16, /device:TPU:1, one launch (start us, length us, event | category | flops | bytes accessed | tf_op | source)
XLA Modules:
  0.0 333.7 jit_solution(15703770300733898723)
XLA Ops:
  0.6 1.1 broadcast_in_dim.28
  1.8 25.1 %all_to_all.58 = bf16[16,256,160]{1,2,0:T(8,128)(2,1)S(1)} all-to-all(bf16[16,256,160]{1,2,0:T(8,128)(2,1)S(1)} %broadcast_in_dim.28), channel_id=1, replica_groups=mesh['blk'=16,'exp'=16] {'blk'}, dimensions={0} | all-to-all | bytes 2621440 | tf_op jit(solution)/shard_map/all_to_all | solution.py:174
  27.7 0.8 copy-done.2
  29.0 1.4 broadcast_in_dim.29
  30.5 5.3 %all-to-all-start.1 = ((bf16[16,256,224]{1,2,0:T(8,128)(2,1)}), bf16[16,256,224]{1,2,0:T(8,128)(2,1)}, u32[]{:S(2)}, u32[]{:S(2)}) async-start(bf16[16,256,224]{1,2,0:T(8,128)(2,1)} %broadcast_in_dim.29), calls=%async_computation.1 | async-start | bytes 3670016 | tf_op jit(solution)/shard_map/all_to_all | solution.py:174
  37.2 0.9 copy.38.offset_ref
  38.1 0.7 iota_add_fusion.qpos_ref
  39.3 0.8 pad_maximum_fusion.2
  40.2 20.6 %all-to-all-done.1 = bf16[16,256,224]{1,2,0:T(8,128)(2,1)} async-done(((bf16[16,256,224]{1,2,0:T(8,128)(2,1)}), bf16[16,256,224]{1,2,0:T(8,128)(2,1)}, u32[]{:S(2)}, u32[]{:S(2)}) %all-to-all-start.1) | async-done | bytes 1835040 | tf_op jit(solution)/shard_map/all_to_all | solution.py:174
  60.8 1.0 slice.40
  61.8 3.8 %copy.37.proj_ref = bf16[256,3584]{1,0:T(8,128)(2,1)} copy(bf16[256,3584]{0,1:T(8,128)(2,1)} %bitcast.5) | data formatting | bytes 3670016 | tf_op jit(solution)/shard_map/reshape | solution.py:175
  65.6 0.7 fusion.30
  66.6 1.2 copy.46
  68.7 0.9 pad_maximum_fusion.fresh_ref
  69.6 10.3 %shard_map.149 = (bf16[256,2688]{1,0:T(8,128)(2,1)}, bf16[512,1024]{1,0:T(8,128)(2,1)}) custom-call(bf16[256,3584]{1,0:T(8,128)(2,1)} %copy.37.proj_ref, f32[256,128]{1,0:T(8,128)} %get-tuple-element.17.cos_ref, f32[256,128]{1,0:T(8,128)} %get-tuple-element.18.sin_ref, bf16[512,1024]{1,0:T(8,128)(2,1)} %bitcast.107, ...), custom_call_target="tpu_custom_call" | custom-call | flops 1342177280 | bytes 5308416 | tf_op jit(solution)/shard_map/pallas_call | solution.py:107
  79.9 24.3 %all_to_all.59.part_ref = bf16[16,16,2688]{2,1,0:T(8,128)(2,1)} all-to-all(bf16[16,16,2688]{2,1,0:T(8,128)(2,1)} %bitcast.94), channel_id=1, replica_groups=mesh['blk'=16,'exp'=16] {'blk'}, dimensions={0} | all-to-all | bytes 2752512 | tf_op jit(solution)/shard_map/all_to_all | solution.py:260
  104.3 3.4 %shard_map.150 = bf16[16,16,2560]{2,1,0:T(8,128)(2,1)} custom-call(bf16[16,16,2688]{2,1,0:T(8,128)(2,1)} %all_to_all.59.part_ref), custom_call_target="tpu_custom_call" | custom-call | flops 2064384 | bytes 2686976 | tf_op jit(solution)/shard_map/pallas_call | solution.py:159
  107.7 23.2 %all_to_all.60 = bf16[16,16,2560]{2,1,0:T(8,128)(2,1)S(1)} all-to-all(bf16[16,16,2560]{2,1,0:T(8,128)(2,1)} %shard_map.150), channel_id=1, replica_groups=mesh['blk'=16,'exp'=16] {'blk'}, dimensions={0} | all-to-all | bytes 2621440 | tf_op jit(solution)/shard_map/all_to_all | solution.py:263
  131.5 1.2 broadcast_in_dim.32
  132.7 4.6 %all-to-all-start.4 = ((bf16[16,256,160]{1,2,0:T(8,128)(2,1)}), bf16[16,256,160]{1,2,0:T(8,128)(2,1)S(1)}, u32[]{:S(2)}, u32[]{:S(2)}) async-start(bf16[16,256,160]{1,2,0:T(8,128)(2,1)} %broadcast_in_dim.32), calls=%async_computation.4 | async-start | bytes 2621440 | tf_op jit(solution)/shard_map/all_to_all | solution.py:174
  137.5 1.2 reduce-window.6
  139.1 17.0 %all-to-all-done.4 = bf16[16,256,160]{1,2,0:T(8,128)(2,1)S(1)} async-done(((bf16[16,256,160]{1,2,0:T(8,128)(2,1)}), bf16[16,256,160]{1,2,0:T(8,128)(2,1)S(1)}, u32[]{:S(2)}, u32[]{:S(2)}) %all-to-all-start.4) | async-done | bytes 1310752 | tf_op jit(solution)/shard_map/all_to_all | solution.py:174
  157.7 72.6 %all_to_all.61 = bf16[16,32,2560]{2,1,0:T(8,128)(2,1)S(1)} all-to-all(bf16[16,32,2560]{2,1,0:T(8,128)(2,1)S(1)} %bitcast.86), channel_id=1, replica_groups=mesh['blk'=16,'exp'=16] {'exp'}, dimensions={0} | all-to-all | bytes 5242880 | tf_op jit(solution)/shard_map/all_to_all | solution.py:295
  230.4 2.2 fusion
  232.6 3.1 convolution_convert_fusion
  235.7 4.9 %all-to-all-start.6 = ((bf16[16,32,2560]{2,1,0:T(8,128)(2,1)}), bf16[16,32,2560]{2,1,0:T(8,128)(2,1)}, u32[]{:S(2)}, u32[]{:S(2)}) async-start(bf16[16,32,2560]{2,1,0:T(8,128)(2,1)} %bitcast.90), calls=%async_computation.6 | async-start | bytes 5242880 | tf_op jit(solution)/shard_map/all_to_all | solution.py:302
  241.3 0.9 copy-done.1
  242.1 1.6 fusion.31
  243.8 58.0 %all-to-all-done.6 = bf16[16,32,2560]{2,1,0:T(8,128)(2,1)} async-done(((bf16[16,32,2560]{2,1,0:T(8,128)(2,1)}), bf16[16,32,2560]{2,1,0:T(8,128)(2,1)}, u32[]{:S(2)}, u32[]{:S(2)}) %all-to-all-start.6) | async-done | bytes 2621472 | tf_op jit(solution)/shard_map/all_to_all | solution.py:302
  301.8 2.3 convert_reduce_fusion
  306.2 1.5 copy.42
  307.7 25.2 %all_to_all.62 = bf16[16,256,160]{1,2,0:T(8,128)(2,1)S(1)} all-to-all(bf16[16,256,160]{1,2,0:T(8,128)(2,1)} %bitcast.89), channel_id=1, replica_groups=mesh['blk'=16,'exp'=16] {'blk'}, dimensions={0} | all-to-all | bytes 2621440 | tf_op jit(solution)/shard_map/all_to_all | solution.py:182
  (67 shorter events, 10.1 us)
Async XLA Ops:
  0.6 231.9 %copy-start = (bf16[1,384,2560]{2,1,0:T(8,128)(2,1)S(1)}, bf16[1,384,2560]{2,1,0:T(8,128)(2,1)}, u32[]{:S(2)}) copy-start(bf16[1,384,2560]{2,1,0:T(8,128)(2,1)} %param.27) | copy-start | bytes 5898244
  1.8 25.5 %copy-start.9 = (f32[2560]{0:T(1024)S(1)}, f32[2560]{0:T(1024)}, u32[]{:S(2)}) copy-start(f32[2560]{0:T(1024)} %param.15) | copy-start | bytes 30724
  27.3 1.3 copy-start.2
  30.5 5.9 %copy-start.12 = (s32[1,64]{1,0:T(1,128)S(1)}, s32[1,64]{1,0:T(1,128)}, u32[]{:S(2)}) copy-start(s32[1,64]{1,0:T(1,128)} %param.19) | copy-start | bytes 772
  30.5 30.3 %all-to-all-start.1 = ((bf16[16,256,224]{1,2,0:T(8,128)(2,1)}), bf16[16,256,224]{1,2,0:T(8,128)(2,1)}, u32[]{:S(2)}, u32[]{:S(2)}) async-start(bf16[16,256,224]{1,2,0:T(8,128)(2,1)} %broadcast_in_dim.29), calls=%async_computation.1 | async-start | bytes 3670016 | tf_op jit(solution)/shard_map/all_to_all | solution.py:174
  67.8 1.0 slice-start
  107.7 23.3 %copy-start.5 = (bf16[2560,160]{0,1:T(8,128)(2,1)S(1)}, bf16[2560,160]{0,1:T(8,128)(2,1)}, u32[]{:S(2)}) copy-start(bf16[2560,160]{0,1:T(8,128)(2,1)} %param.17) | copy-start | bytes 2457604
  107.7 23.3 %copy-start.6 = (bf16[256,160]{0,1:T(8,128)(2,1)S(1)}, bf16[256,160]{0,1:T(8,128)(2,1)}, u32[]{:S(2)}) copy-start(bf16[256,160]{0,1:T(8,128)(2,1)} %param.14) | copy-start | bytes 245764
  132.7 4.6 %copy-start.8 = (s32[256,6]{0,1:T(8,128)S(1)}, s32[256,6]{0,1:T(8,128)}, u32[]{:S(2)}) copy-start(s32[256,6]{0,1:T(8,128)} %param.22) | copy-start | bytes 18436
  132.7 23.8 %copy-start.7 = (f32[2560]{0:T(1024)S(1)}, f32[2560]{0:T(1024)}, u32[]{:S(2)}) copy-start(f32[2560]{0:T(1024)} %param.21) | copy-start | bytes 30724
  132.7 23.4 %all-to-all-start.4 = ((bf16[16,256,160]{1,2,0:T(8,128)(2,1)}), bf16[16,256,160]{1,2,0:T(8,128)(2,1)S(1)}, u32[]{:S(2)}, u32[]{:S(2)}) async-start(bf16[16,256,160]{1,2,0:T(8,128)(2,1)} %broadcast_in_dim.32), calls=%async_computation.4 | async-start | bytes 2621440 | tf_op jit(solution)/shard_map/all_to_all | solution.py:174
  157.7 72.7 %copy-start.11 = (bf16[1,2560,768]{2,1,0:T(8,128)(2,1)S(1)}, bf16[1,2560,768]{2,1,0:T(8,128)(2,1)}, u32[]{:S(2)}) copy-start(bf16[1,2560,768]{2,1,0:T(8,128)(2,1)} %param.26) | copy-start | bytes 11796484
  235.7 4.9 %copy-start.10 = (f32[256,6]{0,1:T(8,128)S(1)}, f32[256,6]{0,1:T(8,128)}, u32[]{:S(2)}) copy-start(f32[256,6]{0,1:T(8,128)} %param.23) | copy-start | bytes 18436
  235.7 66.1 %all-to-all-start.6 = ((bf16[16,32,2560]{2,1,0:T(8,128)(2,1)}), bf16[16,32,2560]{2,1,0:T(8,128)(2,1)}, u32[]{:S(2)}, u32[]{:S(2)}) async-start(bf16[16,32,2560]{2,1,0:T(8,128)(2,1)} %bitcast.90), calls=%async_computation.6 | async-start | bytes 5242880 | tf_op jit(solution)/shard_map/all_to_all | solution.py:302
  240.6 1.5 copy-start.1
  304.3 1.0 copy-start.3
  304.3 1.3 copy-start.4
